TPU v7x, 256 devices: a whole 4x4x8 slice. The times are simulated.
256 devices in a mesh: seq: 16 (over y, x_hi, core), dp: 16 (over x_lo, z).
Axes of the slice: x: 4 (x_hi: 2, x_lo: 2; x = x_hi * 2 + x_lo), y: 4, z: 8, core: 2. Of those that a mesh axis runs over, the one named last changes fastest.
Arguments:
- features: bfloat16 [32, 6144, 768], P('dp', 'seq'), may hold values from -32 to 32
- weight: bfloat16 [5, 768, 768], replicated, may hold values from -0.09375 to 0.09375
- cotangent: bfloat16 [32, 3072, 768], P('dp', 'seq'), may hold values from -6 to 6
Outputs:
- trunk_input: bfloat16 [32, 3072, 768], P('dp', None, 'seq')
- input_grad: bfloat16 [32, 6144, 768], P('dp', 'seq')
- weight_grad: float32 [5, 768, 768], P(None, 'dp', 'seq')
All inputs are finite; a program needn't handle non-finite values.
Results may differ from a plain program's by a relative error of at most 0.0027.
Values may be sent and summed in bfloat16 or wider, within the bound.
No kernel may reach another device: no remote copies, remote signals or barrier semaphores. Data moves between devices by JAX's collectives and lax.ppermute only.
A program may use at most 128 MiB of HBM per device.

v0:
```python
import jax
import jax.numpy as jnp
from jax import lax
from jax.sharding import PartitionSpec as P
import numpy as np

epsilon = 1e-06
root_half = 0.7071067811865476
inv_root_two_pi = 0.3989422804014327


def with_halo(block, sides, width):
    for axis, dim in sides:
        count = lax.axis_size(axis)
        forward = [(i, i + 1) for i in range(count - 1)]
        backward = [(target, source) for source, target in forward]
        low = lax.ppermute(
            lax.slice_in_dim(block, block.shape[dim] - width, None, axis=dim), axis, forward
        )
        high = lax.ppermute(lax.slice_in_dim(block, 0, width, axis=dim), axis, backward)
        block = jnp.concatenate([low, block, high], axis=dim)
    return block


def halved(block, axis, bit, dim):
    count = lax.axis_size(axis)
    partners = [(i, i ^ (1 << bit)) for i in range(count)]
    mine = (lax.axis_index(axis) >> bit) & 1
    half = block.shape[dim] // 2
    keep = lax.dynamic_slice_in_dim(block, mine * half, half, axis=dim)
    send = lax.dynamic_slice_in_dim(block, (1 - mine) * half, half, axis=dim)
    return keep + lax.ppermute(send, axis, partners)


def sources_of(channels, orders):
    pieces = len(orders)
    width = channels // (16 * pieces)
    sources = []
    for piece, bits in enumerate(orders):
        for place in range(16 * width):
            code, rest = divmod(place, width)
            index = 0
            for step, bit in enumerate(bits):
                index |= ((code >> (len(bits) - 1 - step)) & 1) << bit
            sources.append((index * pieces + piece) * width + rest)
    return np.array(sources, np.int32)


def picked(block, sources):
    rows = lax.broadcasted_iota(jnp.int32, (block.shape[-1], sources.shape[0]), 0)
    one_hot = (rows == sources[None, :]).astype(block.dtype)
    moved = jnp.einsum("blc,co->blo", block, one_hot, preferred_element_type=jnp.float32)
    return moved.astype(block.dtype)


CHAINS = (
    (("seq", 0), ("seq", 2), ("seq", 1), ("dp", 0), ("seq", 3), ("dp", 3), ("dp", 1), ("dp", 2)),
    (("seq", 0), ("seq", 1), ("dp", 0), ("seq", 2), ("seq", 3), ("dp", 3), ("dp", 1), ("dp", 2)),
    (("seq", 0), ("dp", 0), ("seq", 2), ("seq", 1), ("seq", 3), ("dp", 3), ("dp", 1), ("dp", 2)),
)


def gaussian_unit(value):
    return 0.5 * value * (1.0 + jax.scipy.special.erf(value * root_half))


def gaussian_slope(value):
    return 0.5 * (
        1.0 + jax.scipy.special.erf(value * root_half)
    ) + value * inv_root_two_pi * jnp.exp(-0.5 * value * value)


def windows(padded, length, taps):
    return jnp.stack([padded[:, offset : offset + length] for offset in range(taps)], axis=2)


def shards(features, weight, cotangent):
    taps = weight.shape[0]
    channels = weight.shape[2]
    batch = features.shape[0]
    length = features.shape[1]
    reach = taps // 2
    floats = features.astype(jnp.float32)
    inverse = lax.rsqrt(jnp.mean(floats * floats, axis=-1, keepdims=True) + epsilon)
    normed = floats * inverse
    activations = gaussian_unit(normed).astype(jnp.bfloat16)
    spread = (
        lax.broadcasted_iota(jnp.int32, (length, length // 2), 0) // 2
        == lax.broadcasted_iota(jnp.int32, (length, length // 2), 1)
    ).astype(cotangent.dtype)
    upward = 0.5 * jnp.einsum("bjc,lj->blc", cotangent, spread, preferred_element_type=jnp.float32)
    branch_grad = upward.astype(jnp.bfloat16)
    padded_acts = with_halo(activations, (("seq", 1),), reach)
    padded_grad = with_halo(branch_grad, (("seq", 1),), reach)
    dp_order = tuple(bit for axis, bit in CHAINS[0] if axis == "dp")
    act_window = windows(
        picked(padded_acts, jnp.asarray(sources_of(padded_acts.shape[-1], (dp_order,)))), length, taps
    )
    orders = [tuple(bit for axis, bit in steps if axis == "seq") for steps in CHAINS]
    columns = jnp.asarray(sources_of(channels, orders)).reshape(len(CHAINS), 2, -1)
    axis, bit = CHAINS[0][0]
    mine = (lax.axis_index(axis) >> bit) & 1
    halves = []
    for side in (mine, 1 - mine):
        chosen = lax.dynamic_index_in_dim(columns, side, axis=1, keepdims=False).reshape(-1)
        product = jnp.einsum(
            "blo,blki->oki", picked(branch_grad, chosen), act_window, preferred_element_type=jnp.float32
        )
        halves.append(product)
    partners = [(i, i ^ (1 << bit)) for i in range(lax.axis_size(axis))]
    partial = halves[0] + lax.ppermute(halves[1], axis, partners)
    partial = partial.reshape((len(CHAINS), -1) + partial.shape[1:])
    partial, padded_acts, padded_grad, floats, upward = lax.optimization_barrier(
        (partial, padded_acts, padded_grad, floats, upward)
    )
    inverse = lax.rsqrt(jnp.mean(floats * floats, axis=-1, keepdims=True) + epsilon)
    normed = floats * inverse
    grad_window = jnp.stack(
        [padded_grad[:, taps - 1 - k : taps - 1 - k + length] for k in range(taps)], axis=2
    )
    act_grad = jnp.einsum("blko,kio->bli", grad_window, weight, preferred_element_type=jnp.float32)
    slope_grad = act_grad * gaussian_slope(normed)
    centred = jnp.mean(slope_grad * floats, axis=-1, keepdims=True)
    input_grad = (upward + inverse * slope_grad - floats * inverse**3 * centred).astype(
        jnp.bfloat16
    )
    window = windows(padded_acts, length, taps)
    mixed = jnp.einsum("blki,kio->blo", window, weight, preferred_element_type=jnp.float32)
    summed = floats + mixed
    paired = summed.reshape(batch, length // 2, 2, channels)
    pooled = (0.5 * (paired[:, :, 0] + paired[:, :, 1])).astype(jnp.bfloat16)
    trunk_input = lax.all_to_all(pooled, "seq", split_axis=2, concat_axis=1, tiled=True)
    shared = [step for step in range(len(CHAINS[0])) if len({steps[step] for steps in CHAINS}) == 1]
    for step in range(1, len(CHAINS[0])):
        if step in shared:
            if isinstance(partial, list):
                partial, trunk_input = lax.optimization_barrier((jnp.stack(partial), trunk_input))
            axis, bit = CHAINS[0][step]
            partial = halved(partial, axis, bit, 1 if axis == "seq" else 3)
        else:
            partial = [
                halved(partial[piece], axis, bit, 0 if axis == "seq" else 2)
                for piece, (axis, bit) in enumerate(steps[step] for steps in CHAINS)
            ]
    weight_grad = jnp.transpose(partial.reshape((-1,) + partial.shape[2:]), (1, 2, 0))
    return (trunk_input, input_grad, weight_grad)


def solution(mesh):
    return jax.shard_map(
        shards,
        mesh=mesh,
        in_specs=(P("dp", "seq", None), P(), P("dp", "seq", None)),
        out_specs=(P("dp", None, "seq"), P("dp", "seq", None), P(None, "dp", "seq")),
        check_vma=False,
    )
```

profile of v0, /device:TPU:2, one launch (start us, length us, event | category | flops | bytes accessed | tf_op | source)
XLA Modules:
  0.0 168.8 jit_solution(4950320885457104088)
XLA Ops:
  5.6 3.0 %collective-permute-start = (bf16[2,2,768]{2,1,0:T(2,128)(2,1)S(1)}, bf16[2,2,768]{2,1,0:T(2,128)(2,1)S(1)}, u32[]{:S(2)}, u32[]{:S(2)}) collective-permute-start(bf16[2,2,768]{2,1,0:T(2,128)(2,1)S(1)} %get-tuple-element.35), channel_id=1, source_target_pairs={{0,16},{16,32},{32,48},{48,64},{64,80},{80,96},{96,112},{112,128},... | collective-permute-start | bytes 18440 | tf_op jit(solution)/shard_map/ppermute | solution.py:17
  13.2 2.5 %copy-done.14 = bf16[2,384,5,768]{3,1,0,2:T(8,128)(2,1)} copy-done((bf16[2,384,5,768]{3,1,0,2:T(8,128)(2,1)}, bf16[2,384,5,768]{3,1,0,2:T(8,128)(2,1)S(1)}, u32[]{:S(2)}) %copy-start.14) | copy-done | bytes 5898264
  15.8 8.6 %convolution_bitcast_fusion = f32[384,5,768]{2,0,1:T(8,128)} fusion(bf16[2,384,5,768]{3,1,0,2:T(8,128)(2,1)} %copy-done.14, bf16[2,384,768]{2,1,0:T(8,128)(2,1)S(1)} %get-tuple-element.39, s32[384]{0:T(512)S(1)} %bitcast.139), kind=kOutput, calls=%fused_computation.6 | convolution fusion | flops 2718498816 | bytes 12977664 | tf_op jit(solution)/shard_map/blo,blki->oki/dot_general | solution.py:106
  24.4 2.6 %collective-permute-start.2 = (f32[384,5,768]{2,0,1:T(8,128)}, f32[384,5,768]{2,0,1:T(8,128)}, u32[]{:S(2)}, u32[]{:S(2)}) collective-permute-start(f32[384,5,768]{2,0,1:T(8,128)} %convolution_bitcast_fusion), channel_id=1, source_target_pairs={{0,16},{16,0},{32,48},{48,32},{64,80},{80,64},{96,112},{112,96},{1... | collective-permute-start | bytes 17694728 | tf_op jit(solution)/shard_map/ppermute | solution.py:111
  28.3 3.2 %collective-permute-start.3 = (bf16[2,2,768]{2,1,0:T(2,128)(2,1)S(1)}, bf16[2,2,768]{2,1,0:T(2,128)(2,1)S(1)}, u32[]{:S(2)}, u32[]{:S(2)}) collective-permute-start(bf16[2,2,768]{2,1,0:T(2,128)(2,1)S(1)} %get-tuple-element.33), channel_id=1, source_target_pairs={{0,16},{16,32},{32,48},{48,64},{64,80},{80,96},{96,112},{112,128},... | collective-permute-start | bytes 18440 | tf_op jit(solution)/shard_map/ppermute | solution.py:17
  37.8 10.6 %bitcast_add_fusion = f32[384,5,768]{2,0,1:T(8,128)} fusion(f32[384,5,768]{2,0,1:T(8,128)} %collective-permute-done.2, bf16[2,384,5,768]{3,1,0,2:T(8,128)(2,1)} %copy-done.14, bf16[2,384,768]{2,1,0:T(8,128)(2,1)} %copy-done.12, s32[384]{0:T(512)S(1)} %bitcast.138), kind=kOutput, calls=%fused_computation.4 | convolution fusion | flops 2719973376 | bytes 18875904 | tf_op jit(solution)/shard_map/blo,blki->oki/dot_general | solution.py:106
  48.4 3.5 %fusion.51 = (f32[1,128,5,768]{3,1,2,0:T(8,128)S(1)}, f32[1,128,5,768]{3,1,2,0:T(8,128)S(1)}, f32[1,128,5,768]{3,1,2,0:T(8,128)S(1)}) fusion(f32[3,128,5,768]{3,1,0,2:T(8,128)} %bitcast.133), kind=kLoop, calls=%fused_computation.106 | loop fusion | bytes 11796480 | tf_op jit(solution)/shard_map/slice | solution.py:142
  55.9 3.0 %collective-permute-start.8 = (f32[64,5,768]{2,0,1:T(8,128)}, f32[64,5,768]{2,0,1:T(8,128)}, u32[]{:S(2)}, u32[]{:S(2)}) collective-permute-start(f32[64,5,768]{2,0,1:T(8,128)} %dynamic-slice_bitcast_fusion.1), channel_id=1, source_target_pairs={{0,32},{16,48},{32,0},{48,16},{64,96},{80,112},{96,64},{112,80},{1... | collective-permute-start | bytes 2949128 | tf_op jit(solution)/shard_map/ppermute | solution.py:32
  60.0 3.5 %collective-permute-start.5 = (f32[64,5,768]{2,0,1:T(8,128)}, f32[64,5,768]{2,0,1:T(8,128)}, u32[]{:S(2)}, u32[]{:S(2)}) collective-permute-start(f32[64,5,768]{2,0,1:T(8,128)} %dynamic-slice_bitcast_fusion.2), channel_id=1, source_target_pairs={{0,64},{16,80},{32,96},{48,112},{64,0},{80,16},{96,32},{112,48},{1... | collective-permute-start | bytes 2949128 | tf_op jit(solution)/shard_map/ppermute | solution.py:32
  65.8 6.2 %bitcast_add_fusion.1 = f32[2,384,768]{2,1,0:T(8,128)} fusion(f32[2,384,768]{2,1,0:T(8,128)S(1)} %copy-done.2, bf16[2,384,5,768]{3,1,0,2:T(8,128)(2,1)S(1)} %bitcast_dynamic-update-slice_fusion.5, bf16[5,768,768]{2,1,0:T(8,128)(2,1)S(1)} %bitcast.141), kind=kOutput, calls=%fused_computation.11 | convolution fusion | flops 4530438144 | bytes 16515072 | tf_op jit(solution)/shard_map/blki,kio->blo/dot_general | solution.py:128
  72.0 4.0 %reshape.61 = f32[2,192,2,768]{3,2,1,0:T(2,128)} reshape(f32[2,384,768]{2,1,0:T(8,128)} %bitcast_add_fusion.1) | data formatting | bytes 4718592 | tf_op jit(solution)/shard_map/reshape | solution.py:130
  76.0 4.4 %fusion.52 = (f32[2,192,1,768]{3,2,1,0:T(1,128)S(1)}, f32[2,192,1,768]{3,2,1,0:T(1,128)S(1)}) fusion(f32[2,192,2,768]{3,2,1,0:T(2,128)} %reshape.61), kind=kLoop, calls=%fused_computation.107 | loop fusion | bytes 4718592 | tf_op jit(solution)/shard_map/slice | solution.py:131
  82.3 5.5 %all-to-all-start = ((bf16[2,192,768]{1,0,2:T(2,128)(2,1)}), bf16[2,192,768]{1,0,2:T(2,128)(2,1)S(1)}, u32[]{:S(2)}, u32[]{:S(2)}) async-start(bf16[2,192,768]{1,0,2:T(2,128)(2,1)} %copy.39), calls=%async_computation | async-start | bytes 1572864 | tf_op jit(solution)/shard_map/all_to_all | solution.py:132
  89.0 2.5 %copy-done.15 = bf16[2,384,5,768]{3,1,0,2:T(8,128)(2,1)} copy-done((bf16[2,384,5,768]{3,1,0,2:T(8,128)(2,1)}, bf16[2,384,5,768]{3,1,0,2:T(8,128)(2,1)S(1)}, u32[]{:S(2)}) %copy-start.15) | copy-done | bytes 5898264
  91.8 11.3 %all-to-all-done = bf16[2,192,768]{1,0,2:T(2,128)(2,1)S(1)} async-done(((bf16[2,192,768]{1,0,2:T(2,128)(2,1)}), bf16[2,192,768]{1,0,2:T(2,128)(2,1)S(1)}, u32[]{:S(2)}, u32[]{:S(2)}) %all-to-all-start) | async-done | bytes 589856 | tf_op jit(solution)/shard_map/all_to_all | solution.py:132
  111.6 8.1 %collective-permute-done.12 = f32[64,5,384]{2,0,1:T(8,128)S(1)} collective-permute-done((f32[64,5,384]{2,0,1:T(8,128)S(1)}, f32[64,5,384]{2,0,1:T(8,128)S(1)}, u32[]{:S(2)}, u32[]{:S(2)}) %collective-permute-start.12) | collective-permute-done | bytes 491552 | tf_op jit(solution)/shard_map/ppermute | solution.py:32
  121.2 2.8 %collective-permute-done.6 = f32[32,5,768]{2,0,1:T(8,128)S(1)} collective-permute-done((f32[32,5,768]{2,0,1:T(8,128)S(1)}, f32[32,5,768]{2,0,1:T(8,128)S(1)}, u32[]{:S(2)}, u32[]{:S(2)}) %collective-permute-start.6) | collective-permute-done | bytes 491552 | tf_op jit(solution)/shard_map/ppermute | solution.py:32
  124.6 2.2 %collective-permute-start.10 = (f32[32,5,384]{2,0,1:T(8,128)S(1)}, f32[32,5,384]{2,0,1:T(8,128)S(1)}, u32[]{:S(2)}, u32[]{:S(2)}) collective-permute-start(f32[32,5,384]{2,0,1:T(8,128)S(1)} %constant_dynamic-slice_fusion.6), channel_id=1, source_target_pairs={{0,64},{16,80},{32,96},{48,112},{64,0},{80,16},{96,32},{112,48},{1... | collective-permute-start | bytes 737288 | tf_op jit(solution)/shard_map/ppermute | solution.py:32
  131.6 2.0 %collective-permute-start.14 = (f32[3,16,5,384]{3,1,2,0:T(8,128)S(1)}, f32[3,16,5,384]{3,1,2,0:T(8,128)S(1)}, u32[]{:S(2)}, u32[]{:S(2)}) collective-permute-start(f32[3,16,5,384]{3,1,2,0:T(8,128)S(1)} %constant_dynamic-slice_fusion.3), channel_id=1, source_target_pairs={{0,128},{16,144},{32,160},{48,176},{64,192},{80,208},{96,224},{112... | collective-permute-start | bytes 1105928 | tf_op jit(solution)/shard_map/ppermute | solution.py:32
  133.7 7.9 %collective-permute-done.14 = f32[3,16,5,384]{3,1,2,0:T(8,128)S(1)} collective-permute-done((f32[3,16,5,384]{3,1,2,0:T(8,128)S(1)}, f32[3,16,5,384]{3,1,2,0:T(8,128)S(1)}, u32[]{:S(2)}, u32[]{:S(2)}) %collective-permute-start.14) | collective-permute-done | bytes 368672 | tf_op jit(solution)/shard_map/ppermute | solution.py:32
  143.4 5.4 %multiply_reduce_fusion = (f32[2,384]{1,0:T(2,128)S(1)}, f32[2,384,768]{2,1,0:T(8,128)S(1)}) fusion(f32[2,384,768]{2,1,0:T(8,128)S(1)} %copy-done.4, f32[2,384]{1,0:T(2,128)S(1)} %get-tuple-element.38, bf16[2,384,5,768]{3,1,0,2:T(8,128)(2,1)S(1)} %bitcast_dynamic-update-slice_fusion, bf16[5,768,768]{2,1,0:T(8,128)(2,1)S(1)} %bitcast.143), kind=kOutput, calls=%fused_computation.13 | convolution fusion | flops 4536925184 | bytes 16521216 | tf_op jit(solution)/shard_map/blko,kio->bli/dot_general | solution.py:121
  149.0 3.4 %collective-permute-start.16 = (f32[3,16,5,96]{3,1,2,0:T(8,128)S(1)}, f32[3,16,5,96]{3,1,2,0:T(8,128)S(1)}, u32[]{:S(2)}, u32[]{:S(2)}) collective-permute-start(f32[3,16,5,96]{3,1,2,0:T(8,128)S(1)} %constant_dynamic-slice_fusion.1), channel_id=1, source_target_pairs={{0,2},{1,3},{2,0},{3,1},{4,6},{5,7},{6,4},{7,5},{8,10},{9,11},{10,... | collective-permute-start | bytes 276488 | tf_op jit(solution)/shard_map/ppermute | solution.py:32
  152.4 4.2 %collective-permute-done.16 = f32[3,16,5,96]{3,1,2,0:T(8,128)S(1)} collective-permute-done((f32[3,16,5,96]{3,1,2,0:T(8,128)S(1)}, f32[3,16,5,96]{3,1,2,0:T(8,128)S(1)}, u32[]{:S(2)}, u32[]{:S(2)}) %collective-permute-start.16) | collective-permute-done | bytes 92192 | tf_op jit(solution)/shard_map/ppermute | solution.py:32
  156.8 8.3 %collective-permute-start.17 = (f32[3,16,5,48]{3,1,2,0:T(8,128)S(1)}, f32[3,16,5,48]{3,1,2,0:T(8,128)S(1)}, u32[]{:S(2)}, u32[]{:S(2)}) collective-permute-start(f32[3,16,5,48]{3,1,2,0:T(8,128)S(1)} %constant_dynamic-slice_fusion), channel_id=1, source_target_pairs={{0,4},{1,5},{2,6},{3,7},{4,0},{5,1},{6,2},{7,3},{8,12},{9,13},{10,... | collective-permute-start | bytes 138248 | tf_op jit(solution)/shard_map/ppermute | solution.py:32
  (138 shorter events, 49.0 us)
Async XLA Ops:
  4.2 6.4 %collective-permute-start.1 = (bf16[2,2,768]{2,1,0:T(2,128)(2,1)S(1)}, bf16[2,2,768]{2,1,0:T(2,128)(2,1)S(1)}, u32[]{:S(2)}, u32[]{:S(2)}) collective-permute-start(bf16[2,2,768]{2,1,0:T(2,128)(2,1)S(1)} %get-tuple-element.36), channel_id=1, source_target_pairs={{16,0},{32,16},{48,32},{64,48},{80,64},{96,80},{112,96},{128,112},... | collective-permute-start | bytes 18440 | tf_op jit(solution)/shard_map/ppermute | solution.py:20
  5.6 5.0 %collective-permute-start = (bf16[2,2,768]{2,1,0:T(2,128)(2,1)S(1)}, bf16[2,2,768]{2,1,0:T(2,128)(2,1)S(1)}, u32[]{:S(2)}, u32[]{:S(2)}) collective-permute-start(bf16[2,2,768]{2,1,0:T(2,128)(2,1)S(1)} %get-tuple-element.35), channel_id=1, source_target_pairs={{0,16},{16,32},{32,48},{48,64},{64,80},{80,96},{96,112},{112,128},... | collective-permute-start | bytes 18440 | tf_op jit(solution)/shard_map/ppermute | solution.py:17
  10.6 16.4 %copy-start.12 = (bf16[2,384,768]{2,1,0:T(8,128)(2,1)}, bf16[2,384,768]{2,1,0:T(8,128)(2,1)S(1)}, u32[]{:S(2)}) copy-start(bf16[2,384,768]{2,1,0:T(8,128)(2,1)S(1)} %get-tuple-element.39) | copy-start | bytes 3538948
  24.4 13.4 %collective-permute-start.2 = (f32[384,5,768]{2,0,1:T(8,128)}, f32[384,5,768]{2,0,1:T(8,128)}, u32[]{:S(2)}, u32[]{:S(2)}) collective-permute-start(f32[384,5,768]{2,0,1:T(8,128)} %convolution_bitcast_fusion), channel_id=1, source_target_pairs={{0,16},{16,0},{32,48},{48,32},{64,80},{80,64},{96,112},{112,96},{1... | collective-permute-start | bytes 17694728 | tf_op jit(solution)/shard_map/ppermute | solution.py:111
  27.0 9.1 %collective-permute-start.4 = (bf16[2,2,768]{2,1,0:T(2,128)(2,1)S(1)}, bf16[2,2,768]{2,1,0:T(2,128)(2,1)S(1)}, u32[]{:S(2)}, u32[]{:S(2)}) collective-permute-start(bf16[2,2,768]{2,1,0:T(2,128)(2,1)S(1)} %get-tuple-element.34), channel_id=1, source_target_pairs={{16,0},{32,16},{48,32},{64,48},{80,64},{96,80},{112,96},{128,112},... | collective-permute-start | bytes 18440 | tf_op jit(solution)/shard_map/ppermute | solution.py:20
  28.3 7.9 %collective-permute-start.3 = (bf16[2,2,768]{2,1,0:T(2,128)(2,1)S(1)}, bf16[2,2,768]{2,1,0:T(2,128)(2,1)S(1)}, u32[]{:S(2)}, u32[]{:S(2)}) collective-permute-start(bf16[2,2,768]{2,1,0:T(2,128)(2,1)S(1)} %get-tuple-element.33), channel_id=1, source_target_pairs={{0,16},{16,32},{32,48},{48,64},{64,80},{80,96},{96,112},{112,128},... | collective-permute-start | bytes 18440 | tf_op jit(solution)/shard_map/ppermute | solution.py:17
  53.0 52.1 %collective-permute-start.11 = (f32[128,5,384]{2,0,1:T(8,128)}, f32[128,5,384]{2,0,1:T(8,128)}, u32[]{:S(2)}, u32[]{:S(2)}) collective-permute-start(f32[128,5,384]{2,0,1:T(8,128)} %dynamic-slice_bitcast_fusion), channel_id=1, source_target_pairs={{0,1},{1,0},{2,3},{3,2},{4,5},{5,4},{6,7},{7,6},{8,9},{9,8},{10,11... | collective-permute-start | bytes 2949128 | tf_op jit(solution)/shard_map/ppermute | solution.py:32
  55.9 53.9 %collective-permute-start.8 = (f32[64,5,768]{2,0,1:T(8,128)}, f32[64,5,768]{2,0,1:T(8,128)}, u32[]{:S(2)}, u32[]{:S(2)}) collective-permute-start(f32[64,5,768]{2,0,1:T(8,128)} %dynamic-slice_bitcast_fusion.1), channel_id=1, source_target_pairs={{0,32},{16,48},{32,0},{48,16},{64,96},{80,112},{96,64},{112,80},{1... | collective-permute-start | bytes 2949128 | tf_op jit(solution)/shard_map/ppermute | solution.py:32
  60.0 47.0 %collective-permute-start.5 = (f32[64,5,768]{2,0,1:T(8,128)}, f32[64,5,768]{2,0,1:T(8,128)}, u32[]{:S(2)}, u32[]{:S(2)}) collective-permute-start(f32[64,5,768]{2,0,1:T(8,128)} %dynamic-slice_bitcast_fusion.2), channel_id=1, source_target_pairs={{0,64},{16,80},{32,96},{48,112},{64,0},{80,16},{96,32},{112,48},{1... | collective-permute-start | bytes 2949128 | tf_op jit(solution)/shard_map/ppermute | solution.py:32
  82.3 20.7 %all-to-all-start = ((bf16[2,192,768]{1,0,2:T(2,128)(2,1)}), bf16[2,192,768]{1,0,2:T(2,128)(2,1)S(1)}, u32[]{:S(2)}, u32[]{:S(2)}) async-start(bf16[2,192,768]{1,0,2:T(2,128)(2,1)} %copy.39), calls=%async_computation | async-start | bytes 1572864 | tf_op jit(solution)/shard_map/all_to_all | solution.py:132
  106.9 12.8 %collective-permute-start.12 = (f32[64,5,384]{2,0,1:T(8,128)S(1)}, f32[64,5,384]{2,0,1:T(8,128)S(1)}, u32[]{:S(2)}, u32[]{:S(2)}) collective-permute-start(f32[64,5,384]{2,0,1:T(8,128)S(1)} %constant_dynamic-slice_fusion.5), channel_id=1, source_target_pairs={{0,64},{16,80},{32,96},{48,112},{64,0},{80,16},{96,32},{112,48},{1... | collective-permute-start | bytes 1474568 | tf_op jit(solution)/shard_map/ppermute | solution.py:32
  107.2 36.2 %slice-start.4 = ((s8[5898240]{0:T(1024)(128)(4,1)}), s8[4194304]{0:T(1024)(128)(4,1)S(1)}, s32[]{:S(2)}) async-start(s8[5898240]{0:T(1024)(128)(4,1)} %bitcast.142), calls=%async_computation.5 | async-start | bytes 8388608
  108.8 15.2 %collective-permute-start.6 = (f32[32,5,768]{2,0,1:T(8,128)S(1)}, f32[32,5,768]{2,0,1:T(8,128)S(1)}, u32[]{:S(2)}, u32[]{:S(2)}) collective-permute-start(f32[32,5,768]{2,0,1:T(8,128)S(1)} %constant_dynamic-slice_fusion.9), channel_id=1, source_target_pairs={{0,32},{16,48},{32,0},{48,16},{64,96},{80,112},{96,64},{112,80},{1... | collective-permute-start | bytes 1474568 | tf_op jit(solution)/shard_map/ppermute | solution.py:32
  109.9 23.7 %slice-start = ((s8[5898240]{0:T(1024)(128)(4,1)}), s8[4194304]{0:T(1024)(128)(4,1)S(1)}, s32[]{:S(2)}) async-start(s8[5898240]{0:T(1024)(128)(4,1)} %bitcast.136), calls=%async_computation.1 | async-start | bytes 8388608
  111.4 13.0 %collective-permute-start.9 = (f32[64,5,384]{2,0,1:T(8,128)S(1)}, f32[64,5,384]{2,0,1:T(8,128)S(1)}, u32[]{:S(2)}, u32[]{:S(2)}) collective-permute-start(f32[64,5,384]{2,0,1:T(8,128)S(1)} %constant_dynamic-slice_fusion.7), channel_id=1, source_target_pairs={{0,1},{1,0},{2,3},{3,2},{4,5},{5,4},{6,7},{7,6},{8,9},{9,8},{10,11... | collective-permute-start | bytes 1474568 | tf_op jit(solution)/shard_map/ppermute | solution.py:32
  119.8 23.6 %slice-start.5 = ((s8[5898240]{0:T(1024)(128)(4,1)}), s8[1703936]{0:T(1024)(128)(4,1)S(1)}, s32[]{:S(2)}) async-start(s8[5898240]{0:T(1024)(128)(4,1)} %bitcast.142), calls=%async_computation.6 | async-start | bytes 3407872
  119.8 8.8 %collective-permute-start.13 = (f32[32,5,384]{2,0,1:T(8,128)S(1)}, f32[32,5,384]{2,0,1:T(8,128)S(1)}, u32[]{:S(2)}, u32[]{:S(2)}) collective-permute-start(f32[32,5,384]{2,0,1:T(8,128)S(1)} %constant_dynamic-slice_fusion.4), channel_id=1, source_target_pairs={{0,32},{16,48},{32,0},{48,16},{64,96},{80,112},{96,64},{112,80},{1... | collective-permute-start | bytes 737288 | tf_op jit(solution)/shard_map/ppermute | solution.py:32
  124.0 6.3 %collective-permute-start.7 = (f32[32,5,384]{2,0,1:T(8,128)S(1)}, f32[32,5,384]{2,0,1:T(8,128)S(1)}, u32[]{:S(2)}, u32[]{:S(2)}) collective-permute-start(f32[32,5,384]{2,0,1:T(8,128)S(1)} %constant_dynamic-slice_fusion.8), channel_id=1, source_target_pairs={{0,1},{1,0},{2,3},{3,2},{4,5},{5,4},{6,7},{7,6},{8,9},{9,8},{10,11... | collective-permute-start | bytes 737288 | tf_op jit(solution)/shard_map/ppermute | solution.py:32
  124.6 6.9 %collective-permute-start.10 = (f32[32,5,384]{2,0,1:T(8,128)S(1)}, f32[32,5,384]{2,0,1:T(8,128)S(1)}, u32[]{:S(2)}, u32[]{:S(2)}) collective-permute-start(f32[32,5,384]{2,0,1:T(8,128)S(1)} %constant_dynamic-slice_fusion.6), channel_id=1, source_target_pairs={{0,64},{16,80},{32,96},{48,112},{64,0},{80,16},{96,32},{112,48},{1... | collective-permute-start | bytes 737288 | tf_op jit(solution)/shard_map/ppermute | solution.py:32
  131.6 10.0 %collective-permute-start.14 = (f32[3,16,5,384]{3,1,2,0:T(8,128)S(1)}, f32[3,16,5,384]{3,1,2,0:T(8,128)S(1)}, u32[]{:S(2)}, u32[]{:S(2)}) collective-permute-start(f32[3,16,5,384]{3,1,2,0:T(8,128)S(1)} %constant_dynamic-slice_fusion.3), channel_id=1, source_target_pairs={{0,128},{16,144},{32,160},{48,176},{64,192},{80,208},{96,224},{112... | collective-permute-start | bytes 1105928 | tf_op jit(solution)/shard_map/ppermute | solution.py:32
  141.8 7.0 %collective-permute-start.15 = (f32[3,16,5,192]{3,1,2,0:T(8,128)S(1)}, f32[3,16,5,192]{3,1,2,0:T(8,128)S(1)}, u32[]{:S(2)}, u32[]{:S(2)}) collective-permute-start(f32[3,16,5,192]{3,1,2,0:T(8,128)S(1)} %constant_dynamic-slice_fusion.2), channel_id=1, source_target_pairs={{0,8},{1,9},{2,10},{3,11},{4,12},{5,13},{6,14},{7,15},{8,0},{9,1},... | collective-permute-start | bytes 552968 | tf_op jit(solution)/shard_map/ppermute | solution.py:32
  143.4 21.7 %copy-start.6 = (f32[2,384,768]{2,1,0:T(8,128)S(1)}, f32[2,384,768]{2,1,0:T(8,128)}, u32[]{:S(2)}) copy-start(f32[2,384,768]{2,1,0:T(8,128)} %get-tuple-element.14) | copy-start | bytes 7077892
  149.0 7.5 %collective-permute-start.16 = (f32[3,16,5,96]{3,1,2,0:T(8,128)S(1)}, f32[3,16,5,96]{3,1,2,0:T(8,128)S(1)}, u32[]{:S(2)}, u32[]{:S(2)}) collective-permute-start(f32[3,16,5,96]{3,1,2,0:T(8,128)S(1)} %constant_dynamic-slice_fusion.1), channel_id=1, source_target_pairs={{0,2},{1,3},{2,0},{3,1},{4,6},{5,7},{6,4},{7,5},{8,10},{9,11},{10,... | collective-permute-start | bytes 276488 | tf_op jit(solution)/shard_map/ppermute | solution.py:32
  156.8 11.2 %collective-permute-start.17 = (f32[3,16,5,48]{3,1,2,0:T(8,128)S(1)}, f32[3,16,5,48]{3,1,2,0:T(8,128)S(1)}, u32[]{:S(2)}, u32[]{:S(2)}) collective-permute-start(f32[3,16,5,48]{3,1,2,0:T(8,128)S(1)} %constant_dynamic-slice_fusion), channel_id=1, source_target_pairs={{0,4},{1,5},{2,6},{3,7},{4,0},{5,1},{6,2},{7,3},{8,12},{9,13},{10,... | collective-permute-start | bytes 138248 | tf_op jit(solution)/shard_map/ppermute | solution.py:32
  (19 other events, 139.8 us)
where the time goes:
time: 170 us; the launch traced here: 169 us
  starting transfers between devices  45.9 us (27%)
  waiting for transfers between devices  41.9 us (25%)
  matrix products  34 us (20%)
  local copies, waits for them, and re-layouts  30.3 us (18%)
  other arithmetic  15.5 us (9%)
    ppermute x13, waiting for transfers between devices, halved(): return keep + lax.ppermute(send, axis, partners)  29 us
    ppermute x13, starting transfers between devices, halved(): return keep + lax.ppermute(send, axis, partners)  28.9 us
    dot_general x2, matrix products, shards(): jnp.einsum('blo,blki->oki', picked(branch_grad, chosen), act_window, pref...  19.2 us
    all_to_all x1, waiting for transfers between devices, shards(): lax.all_to_all(pooled, 'seq', split_axis=2, concat_axis=1, tiled=True)  11.3 us
    unnamed x61, local copies, waits for them, and re-layouts  10.2 us
    ppermute x2, starting transfers between devices, with_halo(): lax.ppermute(lax.slice_in_dim(block, block.shape[dim] - width, None, axis...  6.24 us
    dot_general x1, matrix products, shards(): jnp.einsum('blki,kio->blo', window, weight, preferred_element_type=jnp.fl...  6.19 us
    all_to_all x1, starting transfers between devices, shards(): lax.all_to_all(pooled, 'seq', split_axis=2, concat_axis=1, tiled=True)  5.5 us
  transfers between devices with their start and end apart: 19, of which 12 were waited for; matrix products, arithmetic and copies ran while one was open for 24% of the time, Pallas kernels for 0%

commit v1 on v0

--- a/solution.py
+++ b/solution.py
@@ -100,18 +100,27 @@
     columns = jnp.asarray(sources_of(channels, orders)).reshape(len(CHAINS), 2, -1)
     axis, bit = CHAINS[0][0]
     mine = (lax.axis_index(axis) >> bit) & 1
-    halves = []
-    for side in (mine, 1 - mine):
+
+    def product(side, grads, acts):
         chosen = lax.dynamic_index_in_dim(columns, side, axis=1, keepdims=False).reshape(-1)
-        product = jnp.einsum(
-            "blo,blki->oki", picked(branch_grad, chosen), act_window, preferred_element_type=jnp.float32
+        return jnp.einsum(
+            "blo,blki->oki", picked(grads, chosen), acts, preferred_element_type=jnp.float32
         )
-        halves.append(product)
+
+    sent = product(1 - mine, branch_grad, act_window)
+    sent, forward_acts, forward_floats = lax.optimization_barrier((sent, padded_acts, floats))
+    window = windows(forward_acts, length, taps)
+    mixed = jnp.einsum("blki,kio->blo", window, weight, preferred_element_type=jnp.float32)
+    summed = forward_floats + mixed
+    paired = summed.reshape(batch, length // 2, 2, channels)
+    pooled = (0.5 * (paired[:, :, 0] + paired[:, :, 1])).astype(jnp.bfloat16)
+    trunk_input = lax.all_to_all(pooled, "seq", split_axis=2, concat_axis=1, tiled=True)
+    pooled, kept_grads, kept_acts = lax.optimization_barrier((pooled, branch_grad, act_window))
     partners = [(i, i ^ (1 << bit)) for i in range(lax.axis_size(axis))]
-    partial = halves[0] + lax.ppermute(halves[1], axis, partners)
+    partial = product(mine, kept_grads, kept_acts) + lax.ppermute(sent, axis, partners)
     partial = partial.reshape((len(CHAINS), -1) + partial.shape[1:])
-    partial, padded_acts, padded_grad, floats, upward = lax.optimization_barrier(
-        (partial, padded_acts, padded_grad, floats, upward)
+    partial, padded_grad, floats, upward = lax.optimization_barrier(
+        (partial, padded_grad, floats, upward)
     )
     inverse = lax.rsqrt(jnp.mean(floats * floats, axis=-1, keepdims=True) + epsilon)
     normed = floats * inverse
@@ -124,12 +133,6 @@
     input_grad = (upward + inverse * slope_grad - floats * inverse**3 * centred).astype(
         jnp.bfloat16
     )
-    window = windows(padded_acts, length, taps)
-    mixed = jnp.einsum("blki,kio->blo", window, weight, preferred_element_type=jnp.float32)
-    summed = floats + mixed
-    paired = summed.reshape(batch, length // 2, 2, channels)
-    pooled = (0.5 * (paired[:, :, 0] + paired[:, :, 1])).astype(jnp.bfloat16)
-    trunk_input = lax.all_to_all(pooled, "seq", split_axis=2, concat_axis=1, tiled=True)
     shared = [step for step in range(len(CHAINS[0])) if len({steps[step] for steps in CHAINS}) == 1]
     for step in range(1, len(CHAINS[0])):
         if step in shared:

time: 170 us -> 174 us (1.024)
  waiting for transfers between devices: 41.9 us -> 58.5 us
  other arithmetic: 15.5 us -> 10.4 us
  local copies, waits for them, and re-layouts: 30.3 us -> 25.7 us
  starting transfers between devices: 45.9 us -> 43.5 us
    ppermute x13, waiting for transfers between devices: 29 us -> 48.2 us  [halved(): return keep + lax.ppermute(send, axis, partners)]
    add x10, other arithmetic: 5.25 us -> 0.92 us  [halved(): return keep + lax.ppermute(send, axis, partners)]
    ppermute x13, starting transfers between devices: 28.9 us -> 24.7 us  [halved(): return keep + lax.ppermute(send, axis, partners)]
    dynamic_slice x13, local copies, waits for them, and re-layouts: 3.76 us -> 0.77 us  [halved(): send = lax.dynamic_slice_in_dim(block, (1 - mine) * half, half, axis=dim)]
    slice x1, local copies, waits for them, and re-layouts: 4.41 us -> 1.82 us  [shards(): pooled = (0.5 * (paired[:, :, 0] + paired[:, :, 1])).astype(jnp.bfloat16)]
    unnamed x61 -> x39, local copies, waits for them, and re-layouts: 10.2 us -> 9.31 us
  transfers between devices with their start and end apart: 19 -> 19, of which waited for: 12 -> 12; matrix products, arithmetic and copies ran while one was open for 24% -> 16% of each run, Pallas kernels for 0% -> 0%
where the time goes in v1:
time: 174 us; the launch traced here: 173 us
  waiting for transfers between devices  58.5 us (34%)
  starting transfers between devices  43.5 us (25%)
  matrix products  33.9 us (19%)
  local copies, waits for them, and re-layouts  25.7 us (15%)
  other arithmetic  10.4 us (6%)
    ppermute x13, waiting for transfers between devices, halved(): return keep + lax.ppermute(send, axis, partners)  48.2 us
    ppermute x13, starting transfers between devices, halved(): return keep + lax.ppermute(send, axis, partners)  24.7 us
    dot_general x2, matrix products, product(): jnp.einsum('blo,blki->oki', picked(grads, chosen), acts, preferred_elemen...  18.9 us
    all_to_all x1, waiting for transfers between devices, shards(): lax.all_to_all(pooled, 'seq', split_axis=2, concat_axis=1, tiled=True)  9.75 us
    unnamed x39, local copies, waits for them, and re-layouts  9.31 us
    all_to_all x1, starting transfers between devices, shards(): lax.all_to_all(pooled, 'seq', split_axis=2, concat_axis=1, tiled=True)  7.03 us
    ppermute x2, starting transfers between devices, with_halo(): lax.ppermute(lax.slice_in_dim(block, block.shape[dim] - width, None, axis...  6.28 us
    dot_general x1, matrix products, shards(): jnp.einsum('blko,kio->bli', grad_window, weight, preferred_element_type=j...  5.39 us
  transfers between devices with their start and end apart: 19, of which 12 were waited for; matrix products, arithmetic and copies ran while one was open for 16% of the time, Pallas kernels for 0%

profile of v1, /device:TPU:2, one launch (start us, length us, event | category | flops | bytes accessed | tf_op | source)
XLA Modules:
  0.0 173.2 jit_solution(12225650777739786143)
XLA Ops:
  6.2 3.0 %collective-permute-start = (bf16[2,2,768]{2,1,0:T(2,128)(2,1)}, bf16[2,2,768]{2,1,0:T(2,128)(2,1)S(1)}, u32[]{:S(2)}, u32[]{:S(2)}) collective-permute-start(bf16[2,2,768]{2,1,0:T(2,128)(2,1)} %get-tuple-element.43), channel_id=1, source_target_pairs={{0,16},{16,32},{32,48},{48,64},{64,80},{80,96},{96,112},{112,128},... | collective-permute-start | bytes 18440 | tf_op jit(solution)/shard_map/ppermute | solution.py:17
  9.2 2.3 %fusion.53 = (bf16[2,384,768]{2,1,0:T(8,128)(2,1)}, f32[2,384,768]{2,1,0:T(8,128)}) fusion(bf16[2,192,768]{2,1,0:T(8,128)(2,1)S(1)} %copy-done, s32[384]{0:T(512)S(1)} %get-tuple-element.51, s32[384]{0:T(512)S(1)} %get-tuple-element.52, pred[384]{0:T(512)(128)(4,1)S(1)} %fusion.46), kind=kOutput, calls=%fused_computation.110 | convolution fusion | flops 227819520 | bytes 4132224 | tf_op jit(solution)/shard_map/bjc,lj->blc/dot_general | solution.py:91
  13.2 2.6 %fusion.13 = bf16[2,388,768]{2,1,0:T(8,128)(2,1)S(1)} fusion(s32[768]{0:T(1024)} %constant.85.clone, bf16[2,2,768]{2,1,0:T(2,128)(2,1)S(1)} %collective-permute-done.1, bf16[2,384,768]{2,1,0:T(8,128)(2,1)} %copy-done.7, bf16[2,2,768]{2,1,0:T(2,128)(2,1)S(1)} %collective-permute-done), kind=kOutput, calls=%fused_computation.21 | convolution fusion | flops 920168448 | bytes 2386944 | tf_op jit(solution)/shard_map/blc,co->blo/dot_general | solution.py:52
  22.2 8.6 %convolution_bitcast_fusion = f32[384,5,768]{2,0,1:T(8,128)} fusion(bf16[2,384,5,768]{3,1,0,2:T(8,128)(2,1)} %fusion.18, bf16[2,384,768]{2,1,0:T(8,128)(2,1)S(1)} %copy-done.6, s32[384]{0:T(512)} %bitcast.135), kind=kOutput, calls=%fused_computation.6 | convolution fusion | flops 2718498816 | bytes 12977664 | tf_op jit(solution)/shard_map/blo,blki->oki/dot_general | solution.py:106
  32.5 2.8 %collective-permute-start.2 = (f32[384,5,768]{2,0,1:T(8,128)}, f32[384,5,768]{2,0,1:T(8,128)}, u32[]{:S(2)}, u32[]{:S(2)}) collective-permute-start(f32[384,5,768]{2,0,1:T(8,128)} %convolution_bitcast_fusion), channel_id=1, source_target_pairs={{0,16},{16,0},{32,48},{48,32},{64,80},{80,64},{96,112},{112,96},{1... | collective-permute-start | bytes 17694728 | tf_op jit(solution)/shard_map/ppermute | solution.py:120
  36.9 4.7 %fusion.2 = f32[2,384,768,1]{2,1,0,3:T(8,128)S(1)} fusion(bf16[2,384,5,768]{3,1,0,2:T(8,128)(2,1)S(1)} %bitcast_dynamic-update-slice_fusion.5, bf16[5,768,768]{2,1,0:T(8,128)(2,1)S(1)} %bitcast.137), kind=kOutput, calls=%fused_computation.2 | convolution fusion | flops 4529848320 | bytes 14155776 | tf_op jit(solution)/shard_map/blki,kio->blo/dot_general | solution.py:113
  43.3 3.0 %reshape.60 = f32[2,192,2,768]{3,2,1,0:T(2,128)S(1)} reshape(f32[2,384,768]{2,1,0:T(8,128)} %bitcast_add_fusion.1) | data formatting | bytes 4718592 | tf_op jit(solution)/shard_map/reshape | solution.py:115
  50.1 7.0 %all-to-all-start = ((bf16[2,192,768]{1,0,2:T(2,128)(2,1)}), bf16[2,192,768]{1,0,2:T(2,128)(2,1)S(1)}, u32[]{:S(2)}, u32[]{:S(2)}) async-start(bf16[2,192,768]{1,0,2:T(2,128)(2,1)} %copy.39), calls=%async_computation | async-start | bytes 1572864 | tf_op jit(solution)/shard_map/all_to_all | solution.py:117
  58.5 3.3 %collective-permute-start.3 = (bf16[2,2,768]{2,1,0:T(2,128)(2,1)S(1)}, bf16[2,2,768]{2,1,0:T(2,128)(2,1)S(1)}, u32[]{:S(2)}, u32[]{:S(2)}) collective-permute-start(bf16[2,2,768]{2,1,0:T(2,128)(2,1)S(1)} %get-tuple-element.41), channel_id=1, source_target_pairs={{0,16},{16,32},{32,48},{48,64},{64,80},{80,96},{96,112},{112,128},... | collective-permute-start | bytes 18440 | tf_op jit(solution)/shard_map/ppermute | solution.py:17
  62.6 9.7 %all-to-all-done = bf16[2,192,768]{1,0,2:T(2,128)(2,1)S(1)} async-done(((bf16[2,192,768]{1,0,2:T(2,128)(2,1)}), bf16[2,192,768]{1,0,2:T(2,128)(2,1)S(1)}, u32[]{:S(2)}, u32[]{:S(2)}) %all-to-all-start) | async-done | bytes 589856 | tf_op jit(solution)/shard_map/all_to_all | solution.py:117
  74.4 10.3 %bitcast_add_fusion = f32[384,5,768]{2,0,1:T(8,128)} fusion(f32[384,5,768]{2,0,1:T(8,128)} %collective-permute-done.2, bf16[2,384,5,768]{3,1,0,2:T(8,128)(2,1)} %fusion.18, bf16[2,384,768]{2,1,0:T(8,128)(2,1)S(1)} %copy-done.6, s32[384]{0:T(512)S(1)} %bitcast.134), kind=kOutput, calls=%fused_computation.4 | convolution fusion | flops 2719973376 | bytes 18875904 | tf_op jit(solution)/shard_map/blo,blki->oki/dot_general | solution.py:106
  84.7 3.3 %fusion.49 = (f32[1,128,5,768]{3,1,2,0:T(8,128)S(1)}, f32[1,128,5,768]{3,1,2,0:T(8,128)S(1)}, f32[1,128,5,768]{3,1,2,0:T(8,128)S(1)}) fusion(f32[3,128,5,768]{3,1,0,2:T(8,128)} %bitcast.131), kind=kLoop, calls=%fused_computation.106 | loop fusion | bytes 11796480 | tf_op jit(solution)/shard_map/slice | solution.py:145
  93.6 18.0 %collective-permute-done.11 = f32[128,5,384]{2,0,1:T(8,128)S(1)} collective-permute-done((f32[128,5,384]{2,0,1:T(8,128)S(1)}, f32[128,5,384]{2,0,1:T(8,128)S(1)}, u32[]{:S(2)}, u32[]{:S(2)}) %collective-permute-start.11) | collective-permute-done | bytes 983072 | tf_op jit(solution)/shard_map/ppermute | solution.py:32
  112.1 3.3 %collective-permute-done.5 = f32[64,5,768]{2,0,1:T(8,128)S(1)} collective-permute-done((f32[64,5,768]{2,0,1:T(8,128)S(1)}, f32[64,5,768]{2,0,1:T(8,128)S(1)}, u32[]{:S(2)}, u32[]{:S(2)}) %collective-permute-start.5) | collective-permute-done | bytes 983072 | tf_op jit(solution)/shard_map/ppermute | solution.py:32
  115.6 2.7 %collective-permute-start.6 = (f32[32,5,768]{2,0,1:T(8,128)S(1)}, f32[32,5,768]{2,0,1:T(8,128)S(1)}, u32[]{:S(2)}, u32[]{:S(2)}) collective-permute-start(f32[32,5,768]{2,0,1:T(8,128)S(1)} %constant_dynamic-slice_fusion.9), channel_id=1, source_target_pairs={{0,32},{16,48},{32,0},{48,16},{64,96},{80,112},{96,64},{112,80},{1... | collective-permute-start | bytes 1474568 | tf_op jit(solution)/shard_map/ppermute | solution.py:32
  118.6 6.3 %collective-permute-done.12 = f32[64,5,384]{2,0,1:T(8,128)S(1)} collective-permute-done((f32[64,5,384]{2,0,1:T(8,128)S(1)}, f32[64,5,384]{2,0,1:T(8,128)S(1)}, u32[]{:S(2)}, u32[]{:S(2)}) %collective-permute-start.12) | collective-permute-done | bytes 491552 | tf_op jit(solution)/shard_map/ppermute | solution.py:32
  125.0 2.3 %collective-permute-start.13 = (f32[32,5,384]{2,0,1:T(8,128)S(1)}, f32[32,5,384]{2,0,1:T(8,128)S(1)}, u32[]{:S(2)}, u32[]{:S(2)}) collective-permute-start(f32[32,5,384]{2,0,1:T(8,128)S(1)} %constant_dynamic-slice_fusion.4), channel_id=1, source_target_pairs={{0,32},{16,48},{32,0},{48,16},{64,96},{80,112},{96,64},{112,80},{1... | collective-permute-start | bytes 737288 | tf_op jit(solution)/shard_map/ppermute | solution.py:32
  130.0 3.5 %collective-permute-done.13 = f32[32,5,384]{2,0,1:T(8,128)S(1)} collective-permute-done((f32[32,5,384]{2,0,1:T(8,128)S(1)}, f32[32,5,384]{2,0,1:T(8,128)S(1)}, u32[]{:S(2)}, u32[]{:S(2)}) %collective-permute-start.13) | collective-permute-done | bytes 245792 | tf_op jit(solution)/shard_map/ppermute | solution.py:32
  134.3 2.2 %collective-permute-done.10 = f32[32,5,384]{2,0,1:T(8,128)S(1)} collective-permute-done((f32[32,5,384]{2,0,1:T(8,128)S(1)}, f32[32,5,384]{2,0,1:T(8,128)S(1)}, u32[]{:S(2)}, u32[]{:S(2)}) %collective-permute-start.10) | collective-permute-done | bytes 245792 | tf_op jit(solution)/shard_map/ppermute | solution.py:32
  137.7 8.1 %collective-permute-done.14 = f32[3,16,5,384]{3,1,2,0:T(8,128)S(1)} collective-permute-done((f32[3,16,5,384]{3,1,2,0:T(8,128)S(1)}, f32[3,16,5,384]{3,1,2,0:T(8,128)S(1)}, u32[]{:S(2)}, u32[]{:S(2)}) %collective-permute-start.14) | collective-permute-done | bytes 368672 | tf_op jit(solution)/shard_map/ppermute | solution.py:32
  147.2 5.4 %multiply_reduce_fusion = (f32[2,384]{1,0:T(2,128)S(1)}, f32[2,384,768]{2,1,0:T(8,128)S(1)}) fusion(f32[2,384,768]{2,1,0:T(8,128)S(1)} %copy-done.3, f32[2,384]{1,0:T(2,128)S(1)} %get-tuple-element.46, bf16[2,384,5,768]{3,1,0,2:T(8,128)(2,1)S(1)} %bitcast_dynamic-update-slice_fusion, bf16[5,768,768]{2,1,0:T(8,128)(2,1)S(1)} %bitcast.139), kind=kOutput, calls=%fused_computation.13 | convolution fusion | flops 4536925184 | bytes 16521216 | tf_op jit(solution)/shard_map/blko,kio->bli/dot_general | solution.py:130
  152.8 3.4 %collective-permute-start.16 = (f32[3,16,5,96]{3,1,2,0:T(8,128)S(1)}, f32[3,16,5,96]{3,1,2,0:T(8,128)S(1)}, u32[]{:S(2)}, u32[]{:S(2)}) collective-permute-start(f32[3,16,5,96]{3,1,2,0:T(8,128)S(1)} %constant_dynamic-slice_fusion.1), channel_id=1, source_target_pairs={{0,2},{1,3},{2,0},{3,1},{4,6},{5,7},{6,4},{7,5},{8,10},{9,11},{10,... | collective-permute-start | bytes 276488 | tf_op jit(solution)/shard_map/ppermute | solution.py:32
  156.2 4.2 %collective-permute-done.16 = f32[3,16,5,96]{3,1,2,0:T(8,128)S(1)} collective-permute-done((f32[3,16,5,96]{3,1,2,0:T(8,128)S(1)}, f32[3,16,5,96]{3,1,2,0:T(8,128)S(1)}, u32[]{:S(2)}, u32[]{:S(2)}) %collective-permute-start.16) | collective-permute-done | bytes 92192 | tf_op jit(solution)/shard_map/ppermute | solution.py:32
  160.6 8.9 %collective-permute-start.17 = (f32[3,16,5,48]{3,1,2,0:T(8,128)S(1)}, f32[3,16,5,48]{3,1,2,0:T(8,128)S(1)}, u32[]{:S(2)}, u32[]{:S(2)}) collective-permute-start(f32[3,16,5,48]{3,1,2,0:T(8,128)S(1)} %constant_dynamic-slice_fusion), channel_id=1, source_target_pairs={{0,4},{1,5},{2,6},{3,7},{4,0},{5,1},{6,2},{7,3},{8,12},{9,13},{10,... | collective-permute-start | bytes 138248 | tf_op jit(solution)/shard_map/ppermute | solution.py:32
  (116 shorter events, 43.1 us)
Async XLA Ops:
  4.8 8.4 %collective-permute-start.1 = (bf16[2,2,768]{2,1,0:T(2,128)(2,1)}, bf16[2,2,768]{2,1,0:T(2,128)(2,1)S(1)}, u32[]{:S(2)}, u32[]{:S(2)}) collective-permute-start(bf16[2,2,768]{2,1,0:T(2,128)(2,1)} %get-tuple-element.44), channel_id=1, source_target_pairs={{16,0},{32,16},{48,32},{64,48},{80,64},{96,80},{112,96},{128,112},... | collective-permute-start | bytes 18440 | tf_op jit(solution)/shard_map/ppermute | solution.py:20
  6.2 7.0 %collective-permute-start = (bf16[2,2,768]{2,1,0:T(2,128)(2,1)}, bf16[2,2,768]{2,1,0:T(2,128)(2,1)S(1)}, u32[]{:S(2)}, u32[]{:S(2)}) collective-permute-start(bf16[2,2,768]{2,1,0:T(2,128)(2,1)} %get-tuple-element.43), channel_id=1, source_target_pairs={{0,16},{16,32},{32,48},{48,64},{64,80},{80,96},{96,112},{112,128},... | collective-permute-start | bytes 18440 | tf_op jit(solution)/shard_map/ppermute | solution.py:17
  11.7 29.9 %copy-start.2 = (f32[2,384,768]{2,1,0:T(8,128)}, f32[2,384,768]{2,1,0:T(8,128)S(1)}, u32[]{:S(2)}) copy-start(f32[2,384,768]{2,1,0:T(8,128)S(1)} %convert_element_type.33) | copy-start | bytes 7077892
  32.5 41.9 %collective-permute-start.2 = (f32[384,5,768]{2,0,1:T(8,128)}, f32[384,5,768]{2,0,1:T(8,128)}, u32[]{:S(2)}, u32[]{:S(2)}) collective-permute-start(f32[384,5,768]{2,0,1:T(8,128)} %convolution_bitcast_fusion), channel_id=1, source_target_pairs={{0,16},{16,0},{32,48},{48,32},{64,80},{80,64},{96,112},{112,96},{1... | collective-permute-start | bytes 17694728 | tf_op jit(solution)/shard_map/ppermute | solution.py:120
  50.1 22.3 %all-to-all-start = ((bf16[2,192,768]{1,0,2:T(2,128)(2,1)}), bf16[2,192,768]{1,0,2:T(2,128)(2,1)S(1)}, u32[]{:S(2)}, u32[]{:S(2)}) async-start(bf16[2,192,768]{1,0,2:T(2,128)(2,1)} %copy.39), calls=%async_computation | async-start | bytes 1572864 | tf_op jit(solution)/shard_map/all_to_all | solution.py:117
  57.2 4.6 %collective-permute-start.4 = (bf16[2,2,768]{2,1,0:T(2,128)(2,1)S(1)}, bf16[2,2,768]{2,1,0:T(2,128)(2,1)S(1)}, u32[]{:S(2)}, u32[]{:S(2)}) collective-permute-start(bf16[2,2,768]{2,1,0:T(2,128)(2,1)S(1)} %get-tuple-element.42), channel_id=1, source_target_pairs={{16,0},{32,16},{48,32},{64,48},{80,64},{96,80},{112,96},{128,112},... | collective-permute-start | bytes 18440 | tf_op jit(solution)/shard_map/ppermute | solution.py:20
  58.5 3.8 %collective-permute-start.3 = (bf16[2,2,768]{2,1,0:T(2,128)(2,1)S(1)}, bf16[2,2,768]{2,1,0:T(2,128)(2,1)S(1)}, u32[]{:S(2)}, u32[]{:S(2)}) collective-permute-start(bf16[2,2,768]{2,1,0:T(2,128)(2,1)S(1)} %get-tuple-element.41), channel_id=1, source_target_pairs={{0,16},{16,32},{32,48},{48,64},{64,80},{80,96},{96,112},{112,128},... | collective-permute-start | bytes 18440 | tf_op jit(solution)/shard_map/ppermute | solution.py:17
  62.6 11.8 %copy-start.8 = (s32[3,128]{1,0:T(4,128)S(1)}, s32[3,128]{1,0:T(4,128)}, u32[]{:S(2)}) copy-start(s32[3,128]{1,0:T(4,128)} %get-tuple-element.34) | copy-start | bytes 4612
  88.1 23.5 %collective-permute-start.11 = (f32[128,5,384]{2,0,1:T(8,128)S(1)}, f32[128,5,384]{2,0,1:T(8,128)S(1)}, u32[]{:S(2)}, u32[]{:S(2)}) collective-permute-start(f32[128,5,384]{2,0,1:T(8,128)S(1)} %dynamic-slice_bitcast_fusion), channel_id=1, source_target_pairs={{0,1},{1,0},{2,3},{3,2},{4,5},{5,4},{6,7},{7,6},{8,9},{9,8},{10,11... | collective-permute-start | bytes 2949128 | tf_op jit(solution)/shard_map/ppermute | solution.py:32
  90.2 28.1 %collective-permute-start.8 = (f32[64,5,768]{2,0,1:T(8,128)S(1)}, f32[64,5,768]{2,0,1:T(8,128)S(1)}, u32[]{:S(2)}, u32[]{:S(2)}) collective-permute-start(f32[64,5,768]{2,0,1:T(8,128)S(1)} %dynamic-slice_bitcast_fusion.1), channel_id=1, source_target_pairs={{0,32},{16,48},{32,0},{48,16},{64,96},{80,112},{96,64},{112,80},{1... | collective-permute-start | bytes 2949128 | tf_op jit(solution)/shard_map/ppermute | solution.py:32
  91.1 24.3 %collective-permute-start.5 = (f32[64,5,768]{2,0,1:T(8,128)S(1)}, f32[64,5,768]{2,0,1:T(8,128)S(1)}, u32[]{:S(2)}, u32[]{:S(2)}) collective-permute-start(f32[64,5,768]{2,0,1:T(8,128)S(1)} %dynamic-slice_bitcast_fusion.2), channel_id=1, source_target_pairs={{0,64},{16,80},{32,96},{48,112},{64,0},{80,16},{96,32},{112,48},{1... | collective-permute-start | bytes 2949128 | tf_op jit(solution)/shard_map/ppermute | solution.py:32
  111.8 13.2 %collective-permute-start.12 = (f32[64,5,384]{2,0,1:T(8,128)S(1)}, f32[64,5,384]{2,0,1:T(8,128)S(1)}, u32[]{:S(2)}, u32[]{:S(2)}) collective-permute-start(f32[64,5,384]{2,0,1:T(8,128)S(1)} %constant_dynamic-slice_fusion.5), channel_id=1, source_target_pairs={{0,64},{16,80},{32,96},{48,112},{64,0},{80,16},{96,32},{112,48},{1... | collective-permute-start | bytes 1474568 | tf_op jit(solution)/shard_map/ppermute | solution.py:32
  115.6 12.3 %collective-permute-start.6 = (f32[32,5,768]{2,0,1:T(8,128)S(1)}, f32[32,5,768]{2,0,1:T(8,128)S(1)}, u32[]{:S(2)}, u32[]{:S(2)}) collective-permute-start(f32[32,5,768]{2,0,1:T(8,128)S(1)} %constant_dynamic-slice_fusion.9), channel_id=1, source_target_pairs={{0,32},{16,48},{32,0},{48,16},{64,96},{80,112},{96,64},{112,80},{1... | collective-permute-start | bytes 1474568 | tf_op jit(solution)/shard_map/ppermute | solution.py:32
  118.4 28.8 %slice-start.2 = ((s8[5898240]{0:T(1024)(128)(4,1)}), s8[4194304]{0:T(1024)(128)(4,1)S(1)}, s32[]{:S(2)}) async-start(s8[5898240]{0:T(1024)(128)(4,1)} %bitcast.138), calls=%async_computation.3 | async-start | bytes 8388608
  118.5 11.1 %collective-permute-start.9 = (f32[64,5,384]{2,0,1:T(8,128)S(1)}, f32[64,5,384]{2,0,1:T(8,128)S(1)}, u32[]{:S(2)}, u32[]{:S(2)}) collective-permute-start(f32[64,5,384]{2,0,1:T(8,128)S(1)} %constant_dynamic-slice_fusion.7), channel_id=1, source_target_pairs={{0,1},{1,0},{2,3},{3,2},{4,5},{5,4},{6,7},{7,6},{8,9},{9,8},{10,11... | collective-permute-start | bytes 1474568 | tf_op jit(solution)/shard_map/ppermute | solution.py:32
  125.0 8.5 %collective-permute-start.13 = (f32[32,5,384]{2,0,1:T(8,128)S(1)}, f32[32,5,384]{2,0,1:T(8,128)S(1)}, u32[]{:S(2)}, u32[]{:S(2)}) collective-permute-start(f32[32,5,384]{2,0,1:T(8,128)S(1)} %constant_dynamic-slice_fusion.4), channel_id=1, source_target_pairs={{0,32},{16,48},{32,0},{48,16},{64,96},{80,112},{96,64},{112,80},{1... | collective-permute-start | bytes 737288 | tf_op jit(solution)/shard_map/ppermute | solution.py:32
  128.0 6.3 %collective-permute-start.7 = (f32[32,5,384]{2,0,1:T(8,128)S(1)}, f32[32,5,384]{2,0,1:T(8,128)S(1)}, u32[]{:S(2)}, u32[]{:S(2)}) collective-permute-start(f32[32,5,384]{2,0,1:T(8,128)S(1)} %constant_dynamic-slice_fusion.8), channel_id=1, source_target_pairs={{0,1},{1,0},{2,3},{3,2},{4,5},{5,4},{6,7},{7,6},{8,9},{9,8},{10,11... | collective-permute-start | bytes 737288 | tf_op jit(solution)/shard_map/ppermute | solution.py:32
  129.6 6.9 %collective-permute-start.10 = (f32[32,5,384]{2,0,1:T(8,128)S(1)}, f32[32,5,384]{2,0,1:T(8,128)S(1)}, u32[]{:S(2)}, u32[]{:S(2)}) collective-permute-start(f32[32,5,384]{2,0,1:T(8,128)S(1)} %constant_dynamic-slice_fusion.6), channel_id=1, source_target_pairs={{0,64},{16,80},{32,96},{48,112},{64,0},{80,16},{96,32},{112,48},{1... | collective-permute-start | bytes 737288 | tf_op jit(solution)/shard_map/ppermute | solution.py:32
  133.5 13.7 %slice-start.3 = ((s8[5898240]{0:T(1024)(128)(4,1)}), s8[1703936]{0:T(1024)(128)(4,1)S(1)}, s32[]{:S(2)}) async-start(s8[5898240]{0:T(1024)(128)(4,1)} %bitcast.138), calls=%async_computation.4 | async-start | bytes 3407872
  136.6 9.1 %collective-permute-start.14 = (f32[3,16,5,384]{3,1,2,0:T(8,128)S(1)}, f32[3,16,5,384]{3,1,2,0:T(8,128)S(1)}, u32[]{:S(2)}, u32[]{:S(2)}) collective-permute-start(f32[3,16,5,384]{3,1,2,0:T(8,128)S(1)} %constant_dynamic-slice_fusion.3), channel_id=1, source_target_pairs={{0,128},{16,144},{32,160},{48,176},{64,192},{80,208},{96,224},{112... | collective-permute-start | bytes 1105928 | tf_op jit(solution)/shard_map/ppermute | solution.py:32
  145.9 6.6 %collective-permute-start.15 = (f32[3,16,5,192]{3,1,2,0:T(8,128)S(1)}, f32[3,16,5,192]{3,1,2,0:T(8,128)S(1)}, u32[]{:S(2)}, u32[]{:S(2)}) collective-permute-start(f32[3,16,5,192]{3,1,2,0:T(8,128)S(1)} %constant_dynamic-slice_fusion.2), channel_id=1, source_target_pairs={{0,8},{1,9},{2,10},{3,11},{4,12},{5,13},{6,14},{7,15},{8,0},{9,1},... | collective-permute-start | bytes 552968 | tf_op jit(solution)/shard_map/ppermute | solution.py:32
  147.2 22.3 %copy-start.5 = (f32[2,384,768]{2,1,0:T(8,128)S(1)}, f32[2,384,768]{2,1,0:T(8,128)}, u32[]{:S(2)}) copy-start(f32[2,384,768]{2,1,0:T(8,128)} %get-tuple-element.21) | copy-start | bytes 7077892
  152.8 7.6 %collective-permute-start.16 = (f32[3,16,5,96]{3,1,2,0:T(8,128)S(1)}, f32[3,16,5,96]{3,1,2,0:T(8,128)S(1)}, u32[]{:S(2)}, u32[]{:S(2)}) collective-permute-start(f32[3,16,5,96]{3,1,2,0:T(8,128)S(1)} %constant_dynamic-slice_fusion.1), channel_id=1, source_target_pairs={{0,2},{1,3},{2,0},{3,1},{4,6},{5,7},{6,4},{7,5},{8,10},{9,11},{10,... | collective-permute-start | bytes 276488 | tf_op jit(solution)/shard_map/ppermute | solution.py:32
  160.6 11.7 %collective-permute-start.17 = (f32[3,16,5,48]{3,1,2,0:T(8,128)S(1)}, f32[3,16,5,48]{3,1,2,0:T(8,128)S(1)}, u32[]{:S(2)}, u32[]{:S(2)}) collective-permute-start(f32[3,16,5,48]{3,1,2,0:T(8,128)S(1)} %constant_dynamic-slice_fusion), channel_id=1, source_target_pairs={{0,4},{1,5},{2,6},{3,7},{4,0},{5,1},{6,2},{7,3},{8,12},{9,13},{10,... | collective-permute-start | bytes 138248 | tf_op jit(solution)/shard_map/ppermute | solution.py:32
  (8 other events, 38.7 us)

commit v2 on v0

--- a/solution.py
+++ b/solution.py
@@ -90,8 +90,18 @@
     ).astype(cotangent.dtype)
     upward = 0.5 * jnp.einsum("bjc,lj->blc", cotangent, spread, preferred_element_type=jnp.float32)
     branch_grad = upward.astype(jnp.bfloat16)
-    padded_acts = with_halo(activations, (("seq", 1),), reach)
-    padded_grad = with_halo(branch_grad, (("seq", 1),), reach)
+    count = lax.axis_size("seq")
+    forward = [(i, i + 1) for i in range(count - 1)]
+    backward = [(target, source) for source, target in forward]
+    both = (activations, branch_grad)
+    low = lax.ppermute(jnp.concatenate([x[:, length - reach :] for x in both], axis=-1), "seq", forward)
+    high = lax.ppermute(jnp.concatenate([x[:, :reach] for x in both], axis=-1), "seq", backward)
+    padded_acts, padded_grad = (
+        jnp.concatenate([edge_low, x, edge_high], axis=1)
+        for x, edge_low, edge_high in zip(
+            both, jnp.split(low, 2, axis=-1), jnp.split(high, 2, axis=-1)
+        )
+    )
     dp_order = tuple(bit for axis, bit in CHAINS[0] if axis == "dp")
     act_window = windows(
         picked(padded_acts, jnp.asarray(sources_of(padded_acts.shape[-1], (dp_order,)))), length, taps

time: 170 us -> 171 us (level)
  waiting for transfers between devices: 41.9 us -> 47.3 us
  starting transfers between devices: 45.9 us -> 41.9 us
  other arithmetic: 15.5 us -> 12 us
  local copies, waits for them, and re-layouts: 30.3 us -> 32.3 us
    ppermute x1, waiting for transfers between devices: 0.01 us -> 6.02 us  [shards(): partial = halves[0] + lax.ppermute(halves[1], axis, partners)]
    ppermute x4 -> x2, starting transfers between devices: 8.96 us -> 4.32 us  [the longest x1 3.03 us: shards(): lax.ppermute(jnp.concatenate([x[:, length - reach:] for x in both], axis=...]
    unnamed x61 -> x63, local copies, waits for them, and re-layouts: 10.2 us -> 12.2 us
  transfers between devices with their start and end apart: 19 -> 17, of which waited for: 12 -> 12; matrix products, arithmetic and copies ran while one was open for 24% -> 22% of each run, Pallas kernels for 0% -> 0%
where the time goes in v2:
time: 171 us; the launch traced here: 170 us
  waiting for transfers between devices  47.3 us (28%)
  starting transfers between devices  41.9 us (25%)
  matrix products  35.2 us (21%)
  local copies, waits for them, and re-layouts  32.3 us (19%)
  other arithmetic  12 us (7%)
    ppermute x13, waiting for transfers between devices, halved(): return keep + lax.ppermute(send, axis, partners)  29.2 us
    ppermute x13, starting transfers between devices, halved(): return keep + lax.ppermute(send, axis, partners)  28.1 us
    dot_general x2, matrix products, shards(): jnp.einsum('blo,blki->oki', picked(branch_grad, chosen), act_window, pref...  19.1 us
    unnamed x63, local copies, waits for them, and re-layouts  12.2 us
    all_to_all x1, waiting for transfers between devices, shards(): lax.all_to_all(pooled, 'seq', split_axis=2, concat_axis=1, tiled=True)  11.3 us
    all_to_all x1, starting transfers between devices, shards(): lax.all_to_all(pooled, 'seq', split_axis=2, concat_axis=1, tiled=True)  6.92 us
    dot_general x1, matrix products, shards(): jnp.einsum('blki,kio->blo', window, weight, preferred_element_type=jnp.fl...  6.2 us
    ppermute x1, waiting for transfers between devices, shards(): partial = halves[0] + lax.ppermute(halves[1], axis, partners)  6.02 us
  transfers between devices with their start and end apart: 17, of which 12 were waited for; matrix products, arithmetic and copies ran while one was open for 22% of the time, Pallas kernels for 0%

profile of v2, /device:TPU:2, one launch (start us, length us, event | category | flops | bytes accessed | tf_op | source)
XLA Modules:
  0.0 169.9 jit_solution(11111935185657026516)
XLA Ops:
  7.1 3.0 %collective-permute-start = (bf16[2,2,1536]{2,1,0:T(2,128)(2,1)S(1)}, bf16[2,2,1536]{2,1,0:T(2,128)(2,1)S(1)}, u32[]{:S(2)}, u32[]{:S(2)}) collective-permute-start(bf16[2,2,1536]{2,1,0:T(2,128)(2,1)S(1)} %pad_maximum_fusion.3), channel_id=1, source_target_pairs={{0,16},{16,32},{32,48},{48,64},{64,80},{80,96},{96,112},{112,128},... | collective-permute-start | bytes 36872 | tf_op jit(solution)/shard_map/ppermute | solution.py:97
  11.0 2.6 %fusion.15 = bf16[2,388,768]{2,1,0:T(8,128)(2,1)S(1)} fusion(s32[768]{0:T(1024)S(1)} %copy-done.18, bf16[2,2,768]{2,1,0:T(2,128)(2,1)S(1)} %get-tuple-element.40, bf16[2,384,768]{2,1,0:T(8,128)(2,1)} %copy-done.14, bf16[2,2,768]{2,1,0:T(2,128)(2,1)S(1)} %get-tuple-element.38), kind=kOutput, calls=%fused_computation.21 | convolution fusion | flops 920168448 | bytes 2386944 | tf_op jit(solution)/shard_map/blc,co->blo/dot_general | solution.py:52
  14.9 2.5 %copy-done.15 = bf16[2,384,5,768]{3,1,0,2:T(8,128)(2,1)} copy-done((bf16[2,384,5,768]{3,1,0,2:T(8,128)(2,1)}, bf16[2,384,5,768]{3,1,0,2:T(8,128)(2,1)S(1)}, u32[]{:S(2)}) %copy-start.15) | copy-done | bytes 5898264
  17.4 8.5 %convolution_bitcast_fusion = f32[384,5,768]{2,0,1:T(8,128)} fusion(bf16[2,384,5,768]{3,1,0,2:T(8,128)(2,1)} %copy-done.15, bf16[2,384,768]{2,1,0:T(8,128)(2,1)S(1)} %get-tuple-element.43, s32[384]{0:T(512)S(1)} %bitcast.139), kind=kOutput, calls=%fused_computation.6 | convolution fusion | flops 2718498816 | bytes 12977664 | tf_op jit(solution)/shard_map/blo,blki->oki/dot_general | solution.py:116
  25.9 2.6 %collective-permute-start.2 = (f32[384,5,768]{2,0,1:T(8,128)}, f32[384,5,768]{2,0,1:T(8,128)}, u32[]{:S(2)}, u32[]{:S(2)}) collective-permute-start(f32[384,5,768]{2,0,1:T(8,128)} %convolution_bitcast_fusion), channel_id=1, source_target_pairs={{0,16},{16,0},{32,48},{48,32},{64,80},{80,64},{96,112},{112,96},{1... | collective-permute-start | bytes 17694728 | tf_op jit(solution)/shard_map/ppermute | solution.py:121
  32.0 6.0 %collective-permute-done.2 = f32[384,5,768]{2,0,1:T(8,128)} collective-permute-done((f32[384,5,768]{2,0,1:T(8,128)}, f32[384,5,768]{2,0,1:T(8,128)}, u32[]{:S(2)}, u32[]{:S(2)}) %collective-permute-start.2) | collective-permute-done | bytes 5898272 | tf_op jit(solution)/shard_map/ppermute | solution.py:121
  38.0 10.6 %bitcast_add_fusion = f32[384,5,768]{2,0,1:T(8,128)} fusion(f32[384,5,768]{2,0,1:T(8,128)} %collective-permute-done.2, bf16[2,384,5,768]{3,1,0,2:T(8,128)(2,1)} %copy-done.15, bf16[2,384,768]{2,1,0:T(8,128)(2,1)} %copy-done.12, s32[384]{0:T(512)S(1)} %bitcast.138), kind=kOutput, calls=%fused_computation.4 | convolution fusion | flops 2719973376 | bytes 18875904 | tf_op jit(solution)/shard_map/blo,blki->oki/dot_general | solution.py:116
  48.6 3.5 %fusion.51 = (f32[1,128,5,768]{3,1,2,0:T(8,128)S(1)}, f32[1,128,5,768]{3,1,2,0:T(8,128)S(1)}, f32[1,128,5,768]{3,1,2,0:T(8,128)S(1)}) fusion(f32[3,128,5,768]{3,1,0,2:T(8,128)} %bitcast.133), kind=kLoop, calls=%fused_computation.108 | loop fusion | bytes 11796480 | tf_op jit(solution)/shard_map/slice | solution.py:152
  56.2 4.0 %collective-permute-start.6 = (f32[64,5,768]{2,0,1:T(8,128)}, f32[64,5,768]{2,0,1:T(8,128)}, u32[]{:S(2)}, u32[]{:S(2)}) collective-permute-start(f32[64,5,768]{2,0,1:T(8,128)} %dynamic-slice_bitcast_fusion.1), channel_id=1, source_target_pairs={{0,32},{16,48},{32,0},{48,16},{64,96},{80,112},{96,64},{112,80},{1... | collective-permute-start | bytes 2949128 | tf_op jit(solution)/shard_map/ppermute | solution.py:32
  65.5 6.2 %bitcast_add_fusion.1 = f32[2,384,768]{2,1,0:T(8,128)} fusion(f32[2,384,768]{2,1,0:T(8,128)S(1)} %copy-done.2, bf16[2,384,5,768]{3,1,0,2:T(8,128)(2,1)S(1)} %bitcast_dynamic-update-slice_fusion.5, bf16[5,768,768]{2,1,0:T(8,128)(2,1)S(1)} %bitcast.141), kind=kOutput, calls=%fused_computation.11 | convolution fusion | flops 4530438144 | bytes 16515072 | tf_op jit(solution)/shard_map/blki,kio->blo/dot_general | solution.py:138
  71.7 4.0 %reshape.61 = f32[2,192,2,768]{3,2,1,0:T(2,128)} reshape(f32[2,384,768]{2,1,0:T(8,128)} %bitcast_add_fusion.1) | data formatting | bytes 4718592 | tf_op jit(solution)/shard_map/reshape | solution.py:140
  75.7 4.4 %fusion.52 = (f32[2,192,1,768]{3,2,1,0:T(1,128)S(1)}, f32[2,192,1,768]{3,2,1,0:T(1,128)S(1)}) fusion(f32[2,192,2,768]{3,2,1,0:T(2,128)} %reshape.61), kind=kLoop, calls=%fused_computation.109 | loop fusion | bytes 4718592 | tf_op jit(solution)/shard_map/slice | solution.py:141
  82.0 6.9 %all-to-all-start = ((bf16[2,192,768]{1,0,2:T(2,128)(2,1)}), bf16[2,192,768]{1,0,2:T(2,128)(2,1)S(1)}, u32[]{:S(2)}, u32[]{:S(2)}) async-start(bf16[2,192,768]{1,0,2:T(2,128)(2,1)} %copy.39), calls=%async_computation | async-start | bytes 1572864 | tf_op jit(solution)/shard_map/all_to_all | solution.py:142
  90.1 2.5 %copy-done.16 = bf16[2,384,5,768]{3,1,0,2:T(8,128)(2,1)} copy-done((bf16[2,384,5,768]{3,1,0,2:T(8,128)(2,1)}, bf16[2,384,5,768]{3,1,0,2:T(8,128)(2,1)S(1)}, u32[]{:S(2)}) %copy-start.16) | copy-done | bytes 5898264
  92.9 11.3 %all-to-all-done = bf16[2,192,768]{1,0,2:T(2,128)(2,1)S(1)} async-done(((bf16[2,192,768]{1,0,2:T(2,128)(2,1)}), bf16[2,192,768]{1,0,2:T(2,128)(2,1)S(1)}, u32[]{:S(2)}, u32[]{:S(2)}) %all-to-all-start) | async-done | bytes 589856 | tf_op jit(solution)/shard_map/all_to_all | solution.py:142
  112.7 8.1 %collective-permute-done.10 = f32[64,5,384]{2,0,1:T(8,128)S(1)} collective-permute-done((f32[64,5,384]{2,0,1:T(8,128)S(1)}, f32[64,5,384]{2,0,1:T(8,128)S(1)}, u32[]{:S(2)}, u32[]{:S(2)}) %collective-permute-start.10) | collective-permute-done | bytes 491552 | tf_op jit(solution)/shard_map/ppermute | solution.py:32
  122.3 2.8 %collective-permute-done.4 = f32[32,5,768]{2,0,1:T(8,128)S(1)} collective-permute-done((f32[32,5,768]{2,0,1:T(8,128)S(1)}, f32[32,5,768]{2,0,1:T(8,128)S(1)}, u32[]{:S(2)}, u32[]{:S(2)}) %collective-permute-start.4) | collective-permute-done | bytes 491552 | tf_op jit(solution)/shard_map/ppermute | solution.py:32
  125.7 2.2 %collective-permute-start.8 = (f32[32,5,384]{2,0,1:T(8,128)S(1)}, f32[32,5,384]{2,0,1:T(8,128)S(1)}, u32[]{:S(2)}, u32[]{:S(2)}) collective-permute-start(f32[32,5,384]{2,0,1:T(8,128)S(1)} %constant_dynamic-slice_fusion.6), channel_id=1, source_target_pairs={{0,64},{16,80},{32,96},{48,112},{64,0},{80,16},{96,32},{112,48},{1... | collective-permute-start | bytes 737288 | tf_op jit(solution)/shard_map/ppermute | solution.py:32
  132.7 1.9 %collective-permute-start.12 = (f32[3,16,5,384]{3,1,2,0:T(8,128)S(1)}, f32[3,16,5,384]{3,1,2,0:T(8,128)S(1)}, u32[]{:S(2)}, u32[]{:S(2)}) collective-permute-start(f32[3,16,5,384]{3,1,2,0:T(8,128)S(1)} %constant_dynamic-slice_fusion.3), channel_id=1, source_target_pairs={{0,128},{16,144},{32,160},{48,176},{64,192},{80,208},{96,224},{112... | collective-permute-start | bytes 1105928 | tf_op jit(solution)/shard_map/ppermute | solution.py:32
  134.8 8.0 %collective-permute-done.12 = f32[3,16,5,384]{3,1,2,0:T(8,128)S(1)} collective-permute-done((f32[3,16,5,384]{3,1,2,0:T(8,128)S(1)}, f32[3,16,5,384]{3,1,2,0:T(8,128)S(1)}, u32[]{:S(2)}, u32[]{:S(2)}) %collective-permute-start.12) | collective-permute-done | bytes 368672 | tf_op jit(solution)/shard_map/ppermute | solution.py:32
  144.5 5.4 %multiply_reduce_fusion = (f32[2,384]{1,0:T(2,128)S(1)}, f32[2,384,768]{2,1,0:T(8,128)S(1)}) fusion(f32[2,384,768]{2,1,0:T(8,128)S(1)} %copy-done.4, f32[2,384]{1,0:T(2,128)S(1)} %get-tuple-element.42, bf16[2,384,5,768]{3,1,0,2:T(8,128)(2,1)S(1)} %bitcast_dynamic-update-slice_fusion, bf16[5,768,768]{2,1,0:T(8,128)(2,1)S(1)} %bitcast.143), kind=kOutput, calls=%fused_computation.13 | convolution fusion | flops 4536925184 | bytes 16521216 | tf_op jit(solution)/shard_map/blko,kio->bli/dot_general | solution.py:131
  150.1 3.4 %collective-permute-start.14 = (f32[3,16,5,96]{3,1,2,0:T(8,128)S(1)}, f32[3,16,5,96]{3,1,2,0:T(8,128)S(1)}, u32[]{:S(2)}, u32[]{:S(2)}) collective-permute-start(f32[3,16,5,96]{3,1,2,0:T(8,128)S(1)} %constant_dynamic-slice_fusion.1), channel_id=1, source_target_pairs={{0,2},{1,3},{2,0},{3,1},{4,6},{5,7},{6,4},{7,5},{8,10},{9,11},{10,... | collective-permute-start | bytes 276488 | tf_op jit(solution)/shard_map/ppermute | solution.py:32
  153.5 4.2 %collective-permute-done.14 = f32[3,16,5,96]{3,1,2,0:T(8,128)S(1)} collective-permute-done((f32[3,16,5,96]{3,1,2,0:T(8,128)S(1)}, f32[3,16,5,96]{3,1,2,0:T(8,128)S(1)}, u32[]{:S(2)}, u32[]{:S(2)}) %collective-permute-start.14) | collective-permute-done | bytes 92192 | tf_op jit(solution)/shard_map/ppermute | solution.py:32
  157.9 8.3 %collective-permute-start.15 = (f32[3,16,5,48]{3,1,2,0:T(8,128)S(1)}, f32[3,16,5,48]{3,1,2,0:T(8,128)S(1)}, u32[]{:S(2)}, u32[]{:S(2)}) collective-permute-start(f32[3,16,5,48]{3,1,2,0:T(8,128)S(1)} %constant_dynamic-slice_fusion), channel_id=1, source_target_pairs={{0,4},{1,5},{2,6},{3,7},{4,0},{5,1},{6,2},{7,3},{8,12},{9,13},{10,... | collective-permute-start | bytes 138248 | tf_op jit(solution)/shard_map/ppermute | solution.py:32
  (140 shorter events, 45.8 us)
Async XLA Ops:
  3.6 13.8 %copy-start.12 = (bf16[2,384,768]{2,1,0:T(8,128)(2,1)}, bf16[2,384,768]{2,1,0:T(8,128)(2,1)S(1)}, u32[]{:S(2)}) copy-start(bf16[2,384,768]{2,1,0:T(8,128)(2,1)S(1)} %get-tuple-element.43) | copy-start | bytes 3538948
  5.8 4.4 %collective-permute-start.1 = (bf16[2,2,1536]{2,1,0:T(2,128)(2,1)S(1)}, bf16[2,2,1536]{2,1,0:T(2,128)(2,1)S(1)}, u32[]{:S(2)}, u32[]{:S(2)}) collective-permute-start(bf16[2,2,1536]{2,1,0:T(2,128)(2,1)S(1)} %pad_maximum_fusion.4), channel_id=1, source_target_pairs={{16,0},{32,16},{48,32},{64,48},{80,64},{96,80},{112,96},{128,112},... | collective-permute-start | bytes 36872 | tf_op jit(solution)/shard_map/ppermute | solution.py:98
  7.1 3.9 %collective-permute-start = (bf16[2,2,1536]{2,1,0:T(2,128)(2,1)S(1)}, bf16[2,2,1536]{2,1,0:T(2,128)(2,1)S(1)}, u32[]{:S(2)}, u32[]{:S(2)}) collective-permute-start(bf16[2,2,1536]{2,1,0:T(2,128)(2,1)S(1)} %pad_maximum_fusion.3), channel_id=1, source_target_pairs={{0,16},{16,32},{32,48},{48,64},{64,80},{80,96},{96,112},{112,128},... | collective-permute-start | bytes 36872 | tf_op jit(solution)/shard_map/ppermute | solution.py:97
  25.9 12.1 %collective-permute-start.2 = (f32[384,5,768]{2,0,1:T(8,128)}, f32[384,5,768]{2,0,1:T(8,128)}, u32[]{:S(2)}, u32[]{:S(2)}) collective-permute-start(f32[384,5,768]{2,0,1:T(8,128)} %convolution_bitcast_fusion), channel_id=1, source_target_pairs={{0,16},{16,0},{32,48},{48,32},{64,80},{80,64},{96,112},{112,96},{1... | collective-permute-start | bytes 17694728 | tf_op jit(solution)/shard_map/ppermute | solution.py:121
  48.6 15.8 %slice-start.2 = ((s8[5898240]{0:T(1024)(128)(4,1)}), s8[4194304]{0:T(1024)(128)(4,1)S(1)}, s32[]{:S(2)}) async-start(s8[5898240]{0:T(1024)(128)(4,1)} %bitcast.140), calls=%async_computation.3 | async-start | bytes 8388608
  53.2 53.0 %collective-permute-start.9 = (f32[128,5,384]{2,0,1:T(8,128)}, f32[128,5,384]{2,0,1:T(8,128)}, u32[]{:S(2)}, u32[]{:S(2)}) collective-permute-start(f32[128,5,384]{2,0,1:T(8,128)} %dynamic-slice_bitcast_fusion), channel_id=1, source_target_pairs={{0,1},{1,0},{2,3},{3,2},{4,5},{5,4},{6,7},{7,6},{8,9},{9,8},{10,11... | collective-permute-start | bytes 2949128 | tf_op jit(solution)/shard_map/ppermute | solution.py:32
  56.2 54.8 %collective-permute-start.6 = (f32[64,5,768]{2,0,1:T(8,128)}, f32[64,5,768]{2,0,1:T(8,128)}, u32[]{:S(2)}, u32[]{:S(2)}) collective-permute-start(f32[64,5,768]{2,0,1:T(8,128)} %dynamic-slice_bitcast_fusion.1), channel_id=1, source_target_pairs={{0,32},{16,48},{32,0},{48,16},{64,96},{80,112},{96,64},{112,80},{1... | collective-permute-start | bytes 2949128 | tf_op jit(solution)/shard_map/ppermute | solution.py:32
  61.3 46.8 %collective-permute-start.3 = (f32[64,5,768]{2,0,1:T(8,128)}, f32[64,5,768]{2,0,1:T(8,128)}, u32[]{:S(2)}, u32[]{:S(2)}) collective-permute-start(f32[64,5,768]{2,0,1:T(8,128)} %dynamic-slice_bitcast_fusion.2), channel_id=1, source_target_pairs={{0,64},{16,80},{32,96},{48,112},{64,0},{80,16},{96,32},{112,48},{1... | collective-permute-start | bytes 2949128 | tf_op jit(solution)/shard_map/ppermute | solution.py:32
  82.0 22.2 %all-to-all-start = ((bf16[2,192,768]{1,0,2:T(2,128)(2,1)}), bf16[2,192,768]{1,0,2:T(2,128)(2,1)S(1)}, u32[]{:S(2)}, u32[]{:S(2)}) async-start(bf16[2,192,768]{1,0,2:T(2,128)(2,1)} %copy.39), calls=%async_computation | async-start | bytes 1572864 | tf_op jit(solution)/shard_map/all_to_all | solution.py:142
  108.0 12.8 %collective-permute-start.10 = (f32[64,5,384]{2,0,1:T(8,128)S(1)}, f32[64,5,384]{2,0,1:T(8,128)S(1)}, u32[]{:S(2)}, u32[]{:S(2)}) collective-permute-start(f32[64,5,384]{2,0,1:T(8,128)S(1)} %constant_dynamic-slice_fusion.5), channel_id=1, source_target_pairs={{0,64},{16,80},{32,96},{48,112},{64,0},{80,16},{96,32},{112,48},{1... | collective-permute-start | bytes 1474568 | tf_op jit(solution)/shard_map/ppermute | solution.py:32
  108.3 36.2 %slice-start.4 = ((s8[5898240]{0:T(1024)(128)(4,1)}), s8[4194304]{0:T(1024)(128)(4,1)S(1)}, s32[]{:S(2)}) async-start(s8[5898240]{0:T(1024)(128)(4,1)} %bitcast.142), calls=%async_computation.5 | async-start | bytes 8388608
  109.9 15.2 %collective-permute-start.4 = (f32[32,5,768]{2,0,1:T(8,128)S(1)}, f32[32,5,768]{2,0,1:T(8,128)S(1)}, u32[]{:S(2)}, u32[]{:S(2)}) collective-permute-start(f32[32,5,768]{2,0,1:T(8,128)S(1)} %constant_dynamic-slice_fusion.9), channel_id=1, source_target_pairs={{0,32},{16,48},{32,0},{48,16},{64,96},{80,112},{96,64},{112,80},{1... | collective-permute-start | bytes 1474568 | tf_op jit(solution)/shard_map/ppermute | solution.py:32
  111.0 23.7 %slice-start = ((s8[5898240]{0:T(1024)(128)(4,1)}), s8[4194304]{0:T(1024)(128)(4,1)S(1)}, s32[]{:S(2)}) async-start(s8[5898240]{0:T(1024)(128)(4,1)} %bitcast.136), calls=%async_computation.1 | async-start | bytes 8388608
  112.5 13.0 %collective-permute-start.7 = (f32[64,5,384]{2,0,1:T(8,128)S(1)}, f32[64,5,384]{2,0,1:T(8,128)S(1)}, u32[]{:S(2)}, u32[]{:S(2)}) collective-permute-start(f32[64,5,384]{2,0,1:T(8,128)S(1)} %constant_dynamic-slice_fusion.7), channel_id=1, source_target_pairs={{0,1},{1,0},{2,3},{3,2},{4,5},{5,4},{6,7},{7,6},{8,9},{9,8},{10,11... | collective-permute-start | bytes 1474568 | tf_op jit(solution)/shard_map/ppermute | solution.py:32
  120.9 13.8 %slice-start.1 = ((s8[5898240]{0:T(1024)(128)(4,1)}), s8[1703936]{0:T(1024)(128)(4,1)S(1)}, s32[]{:S(2)}) async-start(s8[5898240]{0:T(1024)(128)(4,1)} %bitcast.136), calls=%async_computation.2 | async-start | bytes 3407872
  120.9 23.6 %slice-start.5 = ((s8[5898240]{0:T(1024)(128)(4,1)}), s8[1703936]{0:T(1024)(128)(4,1)S(1)}, s32[]{:S(2)}) async-start(s8[5898240]{0:T(1024)(128)(4,1)} %bitcast.142), calls=%async_computation.6 | async-start | bytes 3407872
  120.9 8.8 %collective-permute-start.11 = (f32[32,5,384]{2,0,1:T(8,128)S(1)}, f32[32,5,384]{2,0,1:T(8,128)S(1)}, u32[]{:S(2)}, u32[]{:S(2)}) collective-permute-start(f32[32,5,384]{2,0,1:T(8,128)S(1)} %constant_dynamic-slice_fusion.4), channel_id=1, source_target_pairs={{0,32},{16,48},{32,0},{48,16},{64,96},{80,112},{96,64},{112,80},{1... | collective-permute-start | bytes 737288 | tf_op jit(solution)/shard_map/ppermute | solution.py:32
  125.1 6.3 %collective-permute-start.5 = (f32[32,5,384]{2,0,1:T(8,128)S(1)}, f32[32,5,384]{2,0,1:T(8,128)S(1)}, u32[]{:S(2)}, u32[]{:S(2)}) collective-permute-start(f32[32,5,384]{2,0,1:T(8,128)S(1)} %constant_dynamic-slice_fusion.8), channel_id=1, source_target_pairs={{0,1},{1,0},{2,3},{3,2},{4,5},{5,4},{6,7},{7,6},{8,9},{9,8},{10,11... | collective-permute-start | bytes 737288 | tf_op jit(solution)/shard_map/ppermute | solution.py:32
  125.7 6.9 %collective-permute-start.8 = (f32[32,5,384]{2,0,1:T(8,128)S(1)}, f32[32,5,384]{2,0,1:T(8,128)S(1)}, u32[]{:S(2)}, u32[]{:S(2)}) collective-permute-start(f32[32,5,384]{2,0,1:T(8,128)S(1)} %constant_dynamic-slice_fusion.6), channel_id=1, source_target_pairs={{0,64},{16,80},{32,96},{48,112},{64,0},{80,16},{96,32},{112,48},{1... | collective-permute-start | bytes 737288 | tf_op jit(solution)/shard_map/ppermute | solution.py:32
  132.7 10.0 %collective-permute-start.12 = (f32[3,16,5,384]{3,1,2,0:T(8,128)S(1)}, f32[3,16,5,384]{3,1,2,0:T(8,128)S(1)}, u32[]{:S(2)}, u32[]{:S(2)}) collective-permute-start(f32[3,16,5,384]{3,1,2,0:T(8,128)S(1)} %constant_dynamic-slice_fusion.3), channel_id=1, source_target_pairs={{0,128},{16,144},{32,160},{48,176},{64,192},{80,208},{96,224},{112... | collective-permute-start | bytes 1105928 | tf_op jit(solution)/shard_map/ppermute | solution.py:32
  142.9 6.9 %collective-permute-start.13 = (f32[3,16,5,192]{3,1,2,0:T(8,128)S(1)}, f32[3,16,5,192]{3,1,2,0:T(8,128)S(1)}, u32[]{:S(2)}, u32[]{:S(2)}) collective-permute-start(f32[3,16,5,192]{3,1,2,0:T(8,128)S(1)} %constant_dynamic-slice_fusion.2), channel_id=1, source_target_pairs={{0,8},{1,9},{2,10},{3,11},{4,12},{5,13},{6,14},{7,15},{8,0},{9,1},... | collective-permute-start | bytes 552968 | tf_op jit(solution)/shard_map/ppermute | solution.py:32
  144.5 21.7 %copy-start.6 = (f32[2,384,768]{2,1,0:T(8,128)S(1)}, f32[2,384,768]{2,1,0:T(8,128)}, u32[]{:S(2)}) copy-start(f32[2,384,768]{2,1,0:T(8,128)} %get-tuple-element.14) | copy-start | bytes 7077892
  150.1 7.6 %collective-permute-start.14 = (f32[3,16,5,96]{3,1,2,0:T(8,128)S(1)}, f32[3,16,5,96]{3,1,2,0:T(8,128)S(1)}, u32[]{:S(2)}, u32[]{:S(2)}) collective-permute-start(f32[3,16,5,96]{3,1,2,0:T(8,128)S(1)} %constant_dynamic-slice_fusion.1), channel_id=1, source_target_pairs={{0,2},{1,3},{2,0},{3,1},{4,6},{5,7},{6,4},{7,5},{8,10},{9,11},{10,... | collective-permute-start | bytes 276488 | tf_op jit(solution)/shard_map/ppermute | solution.py:32
  157.9 11.2 %collective-permute-start.15 = (f32[3,16,5,48]{3,1,2,0:T(8,128)S(1)}, f32[3,16,5,48]{3,1,2,0:T(8,128)S(1)}, u32[]{:S(2)}, u32[]{:S(2)}) collective-permute-start(f32[3,16,5,48]{3,1,2,0:T(8,128)S(1)} %constant_dynamic-slice_fusion), channel_id=1, source_target_pairs={{0,4},{1,5},{2,6},{3,7},{4,0},{5,1},{6,2},{7,3},{8,12},{9,13},{10,... | collective-permute-start | bytes 138248 | tf_op jit(solution)/shard_map/ppermute | solution.py:32
  (18 other events, 88.0 us)

commit v3 on v0

--- a/solution.py
+++ b/solution.py
@@ -124,11 +124,19 @@
     input_grad = (upward + inverse * slope_grad - floats * inverse**3 * centred).astype(
         jnp.bfloat16
     )
-    window = windows(padded_acts, length, taps)
-    mixed = jnp.einsum("blki,kio->blo", window, weight, preferred_element_type=jnp.float32)
-    summed = floats + mixed
-    paired = summed.reshape(batch, length // 2, 2, channels)
-    pooled = (0.5 * (paired[:, :, 0] + paired[:, :, 1])).astype(jnp.bfloat16)
+    summed = [
+        floats[:, parity::2]
+        + jnp.einsum(
+            "blki,kio->blo",
+            jnp.stack(
+                [padded_acts[:, parity + k : parity + k + length : 2] for k in range(taps)], axis=2
+            ),
+            weight,
+            preferred_element_type=jnp.float32,
+        )
+        for parity in (0, 1)
+    ]
+    pooled = (0.5 * (summed[0] + summed[1])).astype(jnp.bfloat16)
     trunk_input = lax.all_to_all(pooled, "seq", split_axis=2, concat_axis=1, tiled=True)
     shared = [step for step in range(len(CHAINS[0])) if len({steps[step] for steps in CHAINS}) == 1]
     for step in range(1, len(CHAINS[0])):

time: 170 us -> 197 us (1.16)
  local copies, waits for them, and re-layouts: 30.3 us -> 53.7 us
  starting transfers between devices: 45.9 us -> 48.4 us
    slice x1 -> x8, local copies, waits for them, and re-layouts: 4.41 us -> 32.7 us  [the longest x6 19.7 us: shards(): padded_acts[:, parity + k:parity + k + length:2]]
    reshape x1 -> x0, local copies, waits for them, and re-layouts: 3.96 us -> none  [shards(): paired = summed.reshape(batch, length // 2, 2, channels)]
    ppermute x13, starting transfers between devices: 28.9 us -> 31.3 us  [halved(): return keep + lax.ppermute(send, axis, partners)]
    dot_general x1 -> x2, matrix products: 6.19 us -> 7.86 us  [shards(): jnp.einsum('blki,kio->blo', jnp.stack([padded_acts[:, parity + k:parity +...]
    unnamed x61 -> x74, local copies, waits for them, and re-layouts: 10.2 us -> 9.6 us
  transfers between devices with their start and end apart: 19 -> 19, of which waited for: 12 -> 11; matrix products, arithmetic and copies ran while one was open for 24% -> 17% of each run, Pallas kernels for 0% -> 0%
where the time goes in v3:
time: 197 us; the launch traced here: 196 us
  local copies, waits for them, and re-layouts  53.7 us (27%)
  starting transfers between devices  48.4 us (25%)
  waiting for transfers between devices  41.3 us (21%)
  matrix products  35.7 us (18%)
  other arithmetic  15.4 us (8%)
    ppermute x13, starting transfers between devices, halved(): return keep + lax.ppermute(send, axis, partners)  31.3 us
    ppermute x13, waiting for transfers between devices, halved(): return keep + lax.ppermute(send, axis, partners)  27.9 us
    slice x6, local copies, waits for them, and re-layouts, shards(): padded_acts[:, parity + k:parity + k + length:2]  19.7 us
    dot_general x2, matrix products, shards(): jnp.einsum('blo,blki->oki', picked(branch_grad, chosen), act_window, pref...  19.3 us
    slice x2, local copies, waits for them, and re-layouts, shards(): floats[:, parity::2]  13 us
    all_to_all x1, waiting for transfers between devices, shards(): lax.all_to_all(pooled, 'seq', split_axis=2, concat_axis=1, tiled=True)  11.8 us
    unnamed x74, local copies, waits for them, and re-layouts  9.6 us
    dot_general x2, matrix products, shards(): jnp.einsum('blki,kio->blo', jnp.stack([padded_acts[:, parity + k:parity +...  7.86 us
  transfers between devices with their start and end apart: 19, of which 11 were waited for; matrix products, arithmetic and copies ran while one was open for 17% of the time, Pallas kernels for 0%

profile of v3, /device:TPU:2, one launch (start us, length us, event | category | flops | bytes accessed | tf_op | source)
XLA Modules:
  0.0 195.8 jit_solution(4788202301122305170)
XLA Ops:
  5.6 3.0 %collective-permute-start = (bf16[2,2,768]{2,1,0:T(2,128)(2,1)S(1)}, bf16[2,2,768]{2,1,0:T(2,128)(2,1)S(1)}, u32[]{:S(2)}, u32[]{:S(2)}) collective-permute-start(bf16[2,2,768]{2,1,0:T(2,128)(2,1)S(1)} %get-tuple-element.33), channel_id=1, source_target_pairs={{0,16},{16,32},{32,48},{48,64},{64,80},{80,96},{96,112},{112,128},... | collective-permute-start | bytes 18440 | tf_op jit(solution)/shard_map/ppermute | solution.py:17
  15.7 8.7 %convolution_bitcast_fusion = f32[384,5,768]{2,0,1:T(8,128)} fusion(bf16[2,384,5,768]{3,1,0,2:T(8,128)(2,1)} %copy-done.20, bf16[2,384,768]{2,1,0:T(8,128)(2,1)S(1)} %get-tuple-element.45, s32[384]{0:T(512)S(1)} %bitcast.170), kind=kOutput, calls=%fused_computation.8 | convolution fusion | flops 2718498816 | bytes 12977664 | tf_op jit(solution)/shard_map/blo,blki->oki/dot_general | solution.py:106
  28.3 3.2 %collective-permute-start.3 = (bf16[2,2,768]{2,1,0:T(2,128)(2,1)S(1)}, bf16[2,2,768]{2,1,0:T(2,128)(2,1)S(1)}, u32[]{:S(2)}, u32[]{:S(2)}) collective-permute-start(bf16[2,2,768]{2,1,0:T(2,128)(2,1)S(1)} %get-tuple-element.31), channel_id=1, source_target_pairs={{0,16},{16,32},{32,48},{48,64},{64,80},{80,96},{96,112},{112,128},... | collective-permute-start | bytes 18440 | tf_op jit(solution)/shard_map/ppermute | solution.py:17
  37.8 10.6 %bitcast_add_fusion = f32[384,5,768]{2,0,1:T(8,128)} fusion(f32[384,5,768]{2,0,1:T(8,128)} %collective-permute-done.2, bf16[2,384,5,768]{3,1,0,2:T(8,128)(2,1)} %copy-done.20, bf16[2,384,768]{2,1,0:T(8,128)(2,1)} %copy-done.11, s32[384]{0:T(512)S(1)} %bitcast.169), kind=kOutput, calls=%fused_computation.6 | convolution fusion | flops 2719973376 | bytes 18875904 | tf_op jit(solution)/shard_map/blo,blki->oki/dot_general | solution.py:106
  48.4 3.6 %slice.93 = bf16[2,192,768]{2,1,0:T(8,128)(2,1)} slice(bf16[2,388,768]{2,1,0:T(8,128)(2,1)S(1)} %pad_maximum_fusion), slice={[0:2:1], [1:385:2], [0:768:1]} | slice | bytes 1179648 | tf_op jit(solution)/shard_map/slice | solution.py:132
  52.0 3.6 %slice.92 = bf16[2,192,768]{2,1,0:T(8,128)(2,1)} slice(bf16[2,388,768]{2,1,0:T(8,128)(2,1)S(1)} %pad_maximum_fusion), slice={[0:2:1], [0:384:2], [0:768:1]} | slice | bytes 1179648 | tf_op jit(solution)/shard_map/slice | solution.py:132
  55.5 3.7 %slice.94 = bf16[2,192,768]{2,1,0:T(8,128)(2,1)} slice(bf16[2,388,768]{2,1,0:T(8,128)(2,1)S(1)} %pad_maximum_fusion), slice={[0:2:1], [2:386:2], [0:768:1]} | slice | bytes 1179648 | tf_op jit(solution)/shard_map/slice | solution.py:132
  59.2 3.7 %slice.95 = bf16[2,192,768]{2,1,0:T(8,128)(2,1)} slice(bf16[2,388,768]{2,1,0:T(8,128)(2,1)S(1)} %pad_maximum_fusion), slice={[0:2:1], [3:387:2], [0:768:1]} | slice | bytes 1179648 | tf_op jit(solution)/shard_map/slice | solution.py:132
  64.3 6.5 %slice.91 = f32[2,192,768]{2,1,0:T(8,128)} slice(f32[2,384,768]{2,1,0:T(8,128)} %convert_element_type.30), slice={[0:2:1], [0:384:2], [0:768:1]} | slice | bytes 2359296 | tf_op jit(solution)/shard_map/slice | solution.py:128
  70.8 6.5 %slice.97 = f32[2,192,768]{2,1,0:T(8,128)} slice(f32[2,384,768]{2,1,0:T(8,128)} %convert_element_type.30), slice={[0:2:1], [1:384:2], [0:768:1]} | slice | bytes 2359296 | tf_op jit(solution)/shard_map/slice | solution.py:128
  77.3 3.7 %slice.98 = bf16[2,192,768]{2,1,0:T(8,128)(2,1)} slice(bf16[2,388,768]{2,1,0:T(8,128)(2,1)S(1)} %pad_maximum_fusion), slice={[0:2:1], [5:388:2], [0:768:1]} | slice | bytes 1179648 | tf_op jit(solution)/shard_map/slice | solution.py:132
  81.1 3.3 %fusion.69 = (f32[1,128,5,768]{3,1,2,0:T(8,128)S(1)}, f32[1,128,5,768]{3,1,2,0:T(8,128)S(1)}, f32[1,128,5,768]{3,1,2,0:T(8,128)S(1)}) fusion(f32[3,128,5,768]{3,1,0,2:T(8,128)} %bitcast.164), kind=kLoop, calls=%fused_computation.115 | loop fusion | bytes 11796480 | tf_op jit(solution)/shard_map/slice | solution.py:150
  88.5 3.0 %collective-permute-start.8 = (f32[64,5,768]{2,0,1:T(8,128)}, f32[64,5,768]{2,0,1:T(8,128)}, u32[]{:S(2)}, u32[]{:S(2)}) collective-permute-start(f32[64,5,768]{2,0,1:T(8,128)} %dynamic-slice_bitcast_fusion.1), channel_id=1, source_target_pairs={{0,32},{16,48},{32,0},{48,16},{64,96},{80,112},{96,64},{112,80},{1... | collective-permute-start | bytes 2949128 | tf_op jit(solution)/shard_map/ppermute | solution.py:32
  92.7 3.2 %collective-permute-start.5 = (f32[64,5,768]{2,0,1:T(8,128)}, f32[64,5,768]{2,0,1:T(8,128)}, u32[]{:S(2)}, u32[]{:S(2)}) collective-permute-start(f32[64,5,768]{2,0,1:T(8,128)} %dynamic-slice_bitcast_fusion.2), channel_id=1, source_target_pairs={{0,64},{16,80},{32,96},{48,112},{64,0},{80,16},{96,32},{112,48},{1... | collective-permute-start | bytes 2949128 | tf_op jit(solution)/shard_map/ppermute | solution.py:32
  97.6 5.4 %fusion.33 = f32[2,192,768]{2,1,0:T(8,128)S(1)} fusion(f32[2,192,768]{2,1,0:T(8,128)S(1)} %copy-done.19, bf16[2,192,5,768]{3,1,0,2:T(8,128)(2,1)S(1)} %get-tuple-element.36, bf16[5,768,768]{2,1,0:T(8,128)(2,1)} %param.6), kind=kOutput, calls=%fused_computation.28 | convolution fusion | flops 2265219072 | bytes 11206656 | tf_op jit(solution)/shard_map/blki,kio->blo/dot_general | solution.py:129
  107.3 5.5 %all-to-all-start = ((bf16[2,192,768]{1,0,2:T(2,128)(2,1)}), bf16[2,192,768]{1,0,2:T(2,128)(2,1)S(1)}, u32[]{:S(2)}, u32[]{:S(2)}) async-start(bf16[2,192,768]{1,0,2:T(2,128)(2,1)} %copy.35), calls=%async_computation | async-start | bytes 1572864 | tf_op jit(solution)/shard_map/all_to_all | solution.py:140
  116.7 11.8 %all-to-all-done = bf16[2,192,768]{1,0,2:T(2,128)(2,1)S(1)} async-done(((bf16[2,192,768]{1,0,2:T(2,128)(2,1)}), bf16[2,192,768]{1,0,2:T(2,128)(2,1)S(1)}, u32[]{:S(2)}, u32[]{:S(2)}) %all-to-all-start) | async-done | bytes 589856 | tf_op jit(solution)/shard_map/all_to_all | solution.py:140
  138.7 6.6 %collective-permute-done.12 = f32[64,5,384]{2,0,1:T(8,128)S(1)} collective-permute-done((f32[64,5,384]{2,0,1:T(8,128)S(1)}, f32[64,5,384]{2,0,1:T(8,128)S(1)}, u32[]{:S(2)}, u32[]{:S(2)}) %collective-permute-start.12) | collective-permute-done | bytes 491552 | tf_op jit(solution)/shard_map/ppermute | solution.py:32
  149.3 3.0 %collective-permute-done.9 = f32[64,5,384]{2,0,1:T(8,128)S(1)} collective-permute-done((f32[64,5,384]{2,0,1:T(8,128)S(1)}, f32[64,5,384]{2,0,1:T(8,128)S(1)}, u32[]{:S(2)}, u32[]{:S(2)}) %collective-permute-start.9) | collective-permute-done | bytes 491552 | tf_op jit(solution)/shard_map/ppermute | solution.py:32
  160.1 8.3 %collective-permute-done.14 = f32[3,16,5,384]{3,1,2,0:T(8,128)S(1)} collective-permute-done((f32[3,16,5,384]{3,1,2,0:T(8,128)S(1)}, f32[3,16,5,384]{3,1,2,0:T(8,128)S(1)}, u32[]{:S(2)}, u32[]{:S(2)}) %collective-permute-start.14) | collective-permute-done | bytes 368672 | tf_op jit(solution)/shard_map/ppermute | solution.py:32
  170.0 5.4 %multiply_reduce_fusion = (f32[2,384]{1,0:T(2,128)S(1)}, f32[2,384,768]{2,1,0:T(8,128)S(1)}) fusion(f32[2,384,768]{2,1,0:T(8,128)S(1)} %copy-done.3, f32[2,384]{1,0:T(2,128)S(1)} %get-tuple-element.44, bf16[2,384,5,768]{3,1,0,2:T(8,128)(2,1)S(1)} %bitcast_dynamic-update-slice_fusion, bf16[5,768,768]{2,1,0:T(8,128)(2,1)S(1)} %bitcast.174), kind=kOutput, calls=%fused_computation.14 | convolution fusion | flops 4536925184 | bytes 16521216 | tf_op jit(solution)/shard_map/blko,kio->bli/dot_general | solution.py:121
  175.7 3.4 %collective-permute-start.16 = (f32[3,16,5,96]{3,1,2,0:T(8,128)S(1)}, f32[3,16,5,96]{3,1,2,0:T(8,128)S(1)}, u32[]{:S(2)}, u32[]{:S(2)}) collective-permute-start(f32[3,16,5,96]{3,1,2,0:T(8,128)S(1)} %constant_dynamic-slice_fusion.1), channel_id=1, source_target_pairs={{0,2},{1,3},{2,0},{3,1},{4,6},{5,7},{6,4},{7,5},{8,10},{9,11},{10,... | collective-permute-start | bytes 276488 | tf_op jit(solution)/shard_map/ppermute | solution.py:32
  179.0 3.7 %collective-permute-done.16 = f32[3,16,5,96]{3,1,2,0:T(8,128)S(1)} collective-permute-done((f32[3,16,5,96]{3,1,2,0:T(8,128)S(1)}, f32[3,16,5,96]{3,1,2,0:T(8,128)S(1)}, u32[]{:S(2)}, u32[]{:S(2)}) %collective-permute-start.16) | collective-permute-done | bytes 92192 | tf_op jit(solution)/shard_map/ppermute | solution.py:32
  183.0 9.1 %collective-permute-start.17 = (f32[3,16,5,48]{3,1,2,0:T(8,128)S(1)}, f32[3,16,5,48]{3,1,2,0:T(8,128)S(1)}, u32[]{:S(2)}, u32[]{:S(2)}) collective-permute-start(f32[3,16,5,48]{3,1,2,0:T(8,128)S(1)} %constant_dynamic-slice_fusion), channel_id=1, source_target_pairs={{0,4},{1,5},{2,6},{3,7},{4,0},{5,1},{6,2},{7,3},{8,12},{9,13},{10,... | collective-permute-start | bytes 138248 | tf_op jit(solution)/shard_map/ppermute | solution.py:32
  (157 shorter events, 65.8 us)
Async XLA Ops:
  4.2 6.4 %collective-permute-start.1 = (bf16[2,2,768]{2,1,0:T(2,128)(2,1)S(1)}, bf16[2,2,768]{2,1,0:T(2,128)(2,1)S(1)}, u32[]{:S(2)}, u32[]{:S(2)}) collective-permute-start(bf16[2,2,768]{2,1,0:T(2,128)(2,1)S(1)} %get-tuple-element.34), channel_id=1, source_target_pairs={{16,0},{32,16},{48,32},{64,48},{80,64},{96,80},{112,96},{128,112},... | collective-permute-start | bytes 18440 | tf_op jit(solution)/shard_map/ppermute | solution.py:20
  5.6 5.0 %collective-permute-start = (bf16[2,2,768]{2,1,0:T(2,128)(2,1)S(1)}, bf16[2,2,768]{2,1,0:T(2,128)(2,1)S(1)}, u32[]{:S(2)}, u32[]{:S(2)}) collective-permute-start(bf16[2,2,768]{2,1,0:T(2,128)(2,1)S(1)} %get-tuple-element.33), channel_id=1, source_target_pairs={{0,16},{16,32},{32,48},{48,64},{64,80},{80,96},{96,112},{112,128},... | collective-permute-start | bytes 18440 | tf_op jit(solution)/shard_map/ppermute | solution.py:17
  10.6 16.4 %copy-start.11 = (bf16[2,384,768]{2,1,0:T(8,128)(2,1)}, bf16[2,384,768]{2,1,0:T(8,128)(2,1)S(1)}, u32[]{:S(2)}) copy-start(bf16[2,384,768]{2,1,0:T(8,128)(2,1)S(1)} %get-tuple-element.45) | copy-start | bytes 3538948
  24.4 13.4 %collective-permute-start.2 = (f32[384,5,768]{2,0,1:T(8,128)}, f32[384,5,768]{2,0,1:T(8,128)}, u32[]{:S(2)}, u32[]{:S(2)}) collective-permute-start(f32[384,5,768]{2,0,1:T(8,128)} %convolution_bitcast_fusion), channel_id=1, source_target_pairs={{0,16},{16,0},{32,48},{48,32},{64,80},{80,64},{96,112},{112,96},{1... | collective-permute-start | bytes 17694728 | tf_op jit(solution)/shard_map/ppermute | solution.py:111
  27.0 9.1 %collective-permute-start.4 = (bf16[2,2,768]{2,1,0:T(2,128)(2,1)S(1)}, bf16[2,2,768]{2,1,0:T(2,128)(2,1)S(1)}, u32[]{:S(2)}, u32[]{:S(2)}) collective-permute-start(bf16[2,2,768]{2,1,0:T(2,128)(2,1)S(1)} %get-tuple-element.32), channel_id=1, source_target_pairs={{16,0},{32,16},{48,32},{64,48},{80,64},{96,80},{112,96},{128,112},... | collective-permute-start | bytes 18440 | tf_op jit(solution)/shard_map/ppermute | solution.py:20
  28.3 7.9 %collective-permute-start.3 = (bf16[2,2,768]{2,1,0:T(2,128)(2,1)S(1)}, bf16[2,2,768]{2,1,0:T(2,128)(2,1)S(1)}, u32[]{:S(2)}, u32[]{:S(2)}) collective-permute-start(bf16[2,2,768]{2,1,0:T(2,128)(2,1)S(1)} %get-tuple-element.31), channel_id=1, source_target_pairs={{0,16},{16,32},{32,48},{48,64},{64,80},{80,96},{96,112},{112,128},... | collective-permute-start | bytes 18440 | tf_op jit(solution)/shard_map/ppermute | solution.py:17
  85.6 44.9 %collective-permute-start.11 = (f32[128,5,384]{2,0,1:T(8,128)}, f32[128,5,384]{2,0,1:T(8,128)}, u32[]{:S(2)}, u32[]{:S(2)}) collective-permute-start(f32[128,5,384]{2,0,1:T(8,128)} %dynamic-slice_bitcast_fusion), channel_id=1, source_target_pairs={{0,1},{1,0},{2,3},{3,2},{4,5},{5,4},{6,7},{7,6},{8,9},{9,8},{10,11... | collective-permute-start | bytes 2949128 | tf_op jit(solution)/shard_map/ppermute | solution.py:32
  88.5 48.1 %collective-permute-start.8 = (f32[64,5,768]{2,0,1:T(8,128)}, f32[64,5,768]{2,0,1:T(8,128)}, u32[]{:S(2)}, u32[]{:S(2)}) collective-permute-start(f32[64,5,768]{2,0,1:T(8,128)} %dynamic-slice_bitcast_fusion.1), channel_id=1, source_target_pairs={{0,32},{16,48},{32,0},{48,16},{64,96},{80,112},{96,64},{112,80},{1... | collective-permute-start | bytes 2949128 | tf_op jit(solution)/shard_map/ppermute | solution.py:32
  92.7 39.7 %collective-permute-start.5 = (f32[64,5,768]{2,0,1:T(8,128)}, f32[64,5,768]{2,0,1:T(8,128)}, u32[]{:S(2)}, u32[]{:S(2)}) collective-permute-start(f32[64,5,768]{2,0,1:T(8,128)} %dynamic-slice_bitcast_fusion.2), channel_id=1, source_target_pairs={{0,64},{16,80},{32,96},{48,112},{64,0},{80,16},{96,32},{112,48},{1... | collective-permute-start | bytes 2949128 | tf_op jit(solution)/shard_map/ppermute | solution.py:32
  107.3 21.2 %all-to-all-start = ((bf16[2,192,768]{1,0,2:T(2,128)(2,1)}), bf16[2,192,768]{1,0,2:T(2,128)(2,1)S(1)}, u32[]{:S(2)}, u32[]{:S(2)}) async-start(bf16[2,192,768]{1,0,2:T(2,128)(2,1)} %copy.35), calls=%async_computation | async-start | bytes 1572864 | tf_op jit(solution)/shard_map/all_to_all | solution.py:140
  132.3 13.0 %collective-permute-start.12 = (f32[64,5,384]{2,0,1:T(8,128)S(1)}, f32[64,5,384]{2,0,1:T(8,128)S(1)}, u32[]{:S(2)}, u32[]{:S(2)}) collective-permute-start(f32[64,5,384]{2,0,1:T(8,128)S(1)} %constant_dynamic-slice_fusion.5), channel_id=1, source_target_pairs={{0,64},{16,80},{32,96},{48,112},{64,0},{80,16},{96,32},{112,48},{1... | collective-permute-start | bytes 1474568 | tf_op jit(solution)/shard_map/ppermute | solution.py:32
  132.6 37.4 %slice-start.4 = ((s8[5898240]{0:T(1024)(128)(4,1)}), s8[4194304]{0:T(1024)(128)(4,1)S(1)}, s32[]{:S(2)}) async-start(s8[5898240]{0:T(1024)(128)(4,1)} %bitcast.173), calls=%async_computation.5 | async-start | bytes 8388608
  134.2 14.5 %collective-permute-start.6 = (f32[32,5,768]{2,0,1:T(8,128)S(1)}, f32[32,5,768]{2,0,1:T(8,128)S(1)}, u32[]{:S(2)}, u32[]{:S(2)}) collective-permute-start(f32[32,5,768]{2,0,1:T(8,128)S(1)} %constant_dynamic-slice_fusion.9), channel_id=1, source_target_pairs={{0,32},{16,48},{32,0},{48,16},{64,96},{80,112},{96,64},{112,80},{1... | collective-permute-start | bytes 1474568 | tf_op jit(solution)/shard_map/ppermute | solution.py:32
  136.6 23.3 %slice-start = ((s8[5898240]{0:T(1024)(128)(4,1)}), s8[4194304]{0:T(1024)(128)(4,1)S(1)}, s32[]{:S(2)}) async-start(s8[5898240]{0:T(1024)(128)(4,1)} %bitcast.167), calls=%async_computation.1 | async-start | bytes 8388608
  138.1 14.2 %collective-permute-start.9 = (f32[64,5,384]{2,0,1:T(8,128)S(1)}, f32[64,5,384]{2,0,1:T(8,128)S(1)}, u32[]{:S(2)}, u32[]{:S(2)}) collective-permute-start(f32[64,5,384]{2,0,1:T(8,128)S(1)} %constant_dynamic-slice_fusion.7), channel_id=1, source_target_pairs={{0,1},{1,0},{2,3},{3,2},{4,5},{5,4},{6,7},{7,6},{8,9},{9,8},{10,11... | collective-permute-start | bytes 1474568 | tf_op jit(solution)/shard_map/ppermute | solution.py:32
  145.4 24.6 %slice-start.5 = ((s8[5898240]{0:T(1024)(128)(4,1)}), s8[1703936]{0:T(1024)(128)(4,1)S(1)}, s32[]{:S(2)}) async-start(s8[5898240]{0:T(1024)(128)(4,1)} %bitcast.173), calls=%async_computation.6 | async-start | bytes 3407872
  145.4 8.9 %collective-permute-start.13 = (f32[32,5,384]{2,0,1:T(8,128)S(1)}, f32[32,5,384]{2,0,1:T(8,128)S(1)}, u32[]{:S(2)}, u32[]{:S(2)}) collective-permute-start(f32[32,5,384]{2,0,1:T(8,128)S(1)} %constant_dynamic-slice_fusion.4), channel_id=1, source_target_pairs={{0,32},{16,48},{32,0},{48,16},{64,96},{80,112},{96,64},{112,80},{1... | collective-permute-start | bytes 737288 | tf_op jit(solution)/shard_map/ppermute | solution.py:32
  148.8 7.9 %collective-permute-start.7 = (f32[32,5,384]{2,0,1:T(8,128)S(1)}, f32[32,5,384]{2,0,1:T(8,128)S(1)}, u32[]{:S(2)}, u32[]{:S(2)}) collective-permute-start(f32[32,5,384]{2,0,1:T(8,128)S(1)} %constant_dynamic-slice_fusion.8), channel_id=1, source_target_pairs={{0,1},{1,0},{2,3},{3,2},{4,5},{5,4},{6,7},{7,6},{8,9},{9,8},{10,11... | collective-permute-start | bytes 737288 | tf_op jit(solution)/shard_map/ppermute | solution.py:32
  152.4 6.6 %collective-permute-start.10 = (f32[32,5,384]{2,0,1:T(8,128)S(1)}, f32[32,5,384]{2,0,1:T(8,128)S(1)}, u32[]{:S(2)}, u32[]{:S(2)}) collective-permute-start(f32[32,5,384]{2,0,1:T(8,128)S(1)} %constant_dynamic-slice_fusion.6), channel_id=1, source_target_pairs={{0,64},{16,80},{32,96},{48,112},{64,0},{80,16},{96,32},{112,48},{1... | collective-permute-start | bytes 737288 | tf_op jit(solution)/shard_map/ppermute | solution.py:32
  159.2 9.1 %collective-permute-start.14 = (f32[3,16,5,384]{3,1,2,0:T(8,128)S(1)}, f32[3,16,5,384]{3,1,2,0:T(8,128)S(1)}, u32[]{:S(2)}, u32[]{:S(2)}) collective-permute-start(f32[3,16,5,384]{3,1,2,0:T(8,128)S(1)} %constant_dynamic-slice_fusion.3), channel_id=1, source_target_pairs={{0,128},{16,144},{32,160},{48,176},{64,192},{80,208},{96,224},{112... | collective-permute-start | bytes 1105928 | tf_op jit(solution)/shard_map/ppermute | solution.py:32
  168.5 6.9 %collective-permute-start.15 = (f32[3,16,5,192]{3,1,2,0:T(8,128)S(1)}, f32[3,16,5,192]{3,1,2,0:T(8,128)S(1)}, u32[]{:S(2)}, u32[]{:S(2)}) collective-permute-start(f32[3,16,5,192]{3,1,2,0:T(8,128)S(1)} %constant_dynamic-slice_fusion.2), channel_id=1, source_target_pairs={{0,8},{1,9},{2,10},{3,11},{4,12},{5,13},{6,14},{7,15},{8,0},{9,1},... | collective-permute-start | bytes 552968 | tf_op jit(solution)/shard_map/ppermute | solution.py:32
  170.0 22.0 %copy-start.5 = (f32[2,384,768]{2,1,0:T(8,128)S(1)}, f32[2,384,768]{2,1,0:T(8,128)}, u32[]{:S(2)}) copy-start(f32[2,384,768]{2,1,0:T(8,128)} %get-tuple-element.14) | copy-start | bytes 7077892
  175.7 7.1 %collective-permute-start.16 = (f32[3,16,5,96]{3,1,2,0:T(8,128)S(1)}, f32[3,16,5,96]{3,1,2,0:T(8,128)S(1)}, u32[]{:S(2)}, u32[]{:S(2)}) collective-permute-start(f32[3,16,5,96]{3,1,2,0:T(8,128)S(1)} %constant_dynamic-slice_fusion.1), channel_id=1, source_target_pairs={{0,2},{1,3},{2,0},{3,1},{4,6},{5,7},{6,4},{7,5},{8,10},{9,11},{10,... | collective-permute-start | bytes 276488 | tf_op jit(solution)/shard_map/ppermute | solution.py:32
  183.0 12.0 %collective-permute-start.17 = (f32[3,16,5,48]{3,1,2,0:T(8,128)S(1)}, f32[3,16,5,48]{3,1,2,0:T(8,128)S(1)}, u32[]{:S(2)}, u32[]{:S(2)}) collective-permute-start(f32[3,16,5,48]{3,1,2,0:T(8,128)S(1)} %constant_dynamic-slice_fusion), channel_id=1, source_target_pairs={{0,4},{1,5},{2,6},{3,7},{4,0},{5,1},{6,2},{7,3},{8,12},{9,13},{10,... | collective-permute-start | bytes 138248 | tf_op jit(solution)/shard_map/ppermute | solution.py:32
  (25 other events, 160.1 us)

commit v4 on v0

--- a/solution.py
+++ b/solution.py
@@ -54,9 +54,9 @@
 
 
 CHAINS = (
-    (("seq", 0), ("seq", 2), ("seq", 1), ("dp", 0), ("seq", 3), ("dp", 3), ("dp", 1), ("dp", 2)),
-    (("seq", 0), ("seq", 1), ("dp", 0), ("seq", 2), ("seq", 3), ("dp", 3), ("dp", 1), ("dp", 2)),
-    (("seq", 0), ("dp", 0), ("seq", 2), ("seq", 1), ("seq", 3), ("dp", 3), ("dp", 1), ("dp", 2)),
+    (("seq", 0), ("seq", 2), ("seq", 1), ("dp", 0), ("dp", 2), ("seq", 3), ("dp", 3), ("dp", 1)),
+    (("seq", 0), ("seq", 1), ("dp", 0), ("seq", 2), ("dp", 2), ("seq", 3), ("dp", 3), ("dp", 1)),
+    (("seq", 0), ("dp", 0), ("seq", 2), ("seq", 1), ("dp", 2), ("seq", 3), ("dp", 3), ("dp", 1)),
 )
 
 

time: 170 us -> 181 us (1.065)
  waiting for transfers between devices: 41.9 us -> 54.5 us
  starting transfers between devices: 45.9 us -> 43.9 us
    ppermute x13, waiting for transfers between devices: 29 us -> 41.6 us  [halved(): return keep + lax.ppermute(send, axis, partners)]
    ppermute x13, starting transfers between devices: 28.9 us -> 26.9 us  [halved(): return keep + lax.ppermute(send, axis, partners)]
  transfers between devices with their start and end apart: 19 -> 19, of which waited for: 12 -> 13; matrix products, arithmetic and copies ran while one was open for 24% -> 22% of each run, Pallas kernels for 0% -> 0%
where the time goes in v4:
time: 181 us; the launch traced here: 180 us
  waiting for transfers between devices  54.5 us (30%)
  starting transfers between devices  43.9 us (24%)
  matrix products  34 us (19%)
  local copies, waits for them, and re-layouts  30.3 us (17%)
  other arithmetic  15.6 us (9%)
    ppermute x13, waiting for transfers between devices, halved(): return keep + lax.ppermute(send, axis, partners)  41.6 us
    ppermute x13, starting transfers between devices, halved(): return keep + lax.ppermute(send, axis, partners)  26.9 us
    dot_general x2, matrix products, shards(): jnp.einsum('blo,blki->oki', picked(branch_grad, chosen), act_window, pref...  19.2 us
    all_to_all x1, waiting for transfers between devices, shards(): lax.all_to_all(pooled, 'seq', split_axis=2, concat_axis=1, tiled=True)  11.3 us
    unnamed x61, local copies, waits for them, and re-layouts  10.2 us
    ppermute x2, starting transfers between devices, with_halo(): lax.ppermute(lax.slice_in_dim(block, block.shape[dim] - width, None, axis...  6.24 us
    dot_general x1, matrix products, shards(): jnp.einsum('blki,kio->blo', window, weight, preferred_element_type=jnp.fl...  6.19 us
    all_to_all x1, starting transfers between devices, shards(): lax.all_to_all(pooled, 'seq', split_axis=2, concat_axis=1, tiled=True)  5.5 us
  transfers between devices with their start and end apart: 19, of which 13 were waited for; matrix products, arithmetic and copies ran while one was open for 22% of the time, Pallas kernels for 0%

profile of v4, /device:TPU:2, one launch (start us, length us, event | category | flops | bytes accessed | tf_op | source)
XLA Modules:
  0.0 179.6 jit_solution(381704552287463943)
XLA Ops:
  5.6 3.0 %collective-permute-start = (bf16[2,2,768]{2,1,0:T(2,128)(2,1)S(1)}, bf16[2,2,768]{2,1,0:T(2,128)(2,1)S(1)}, u32[]{:S(2)}, u32[]{:S(2)}) collective-permute-start(bf16[2,2,768]{2,1,0:T(2,128)(2,1)S(1)} %get-tuple-element.35), channel_id=1, source_target_pairs={{0,16},{16,32},{32,48},{48,64},{64,80},{80,96},{96,112},{112,128},... | collective-permute-start | bytes 18440 | tf_op jit(solution)/shard_map/ppermute | solution.py:17
  13.2 2.5 %copy-done.14 = bf16[2,384,5,768]{3,1,0,2:T(8,128)(2,1)} copy-done((bf16[2,384,5,768]{3,1,0,2:T(8,128)(2,1)}, bf16[2,384,5,768]{3,1,0,2:T(8,128)(2,1)S(1)}, u32[]{:S(2)}) %copy-start.14) | copy-done | bytes 5898264
  15.8 8.6 %convolution_bitcast_fusion = f32[384,5,768]{2,0,1:T(8,128)} fusion(bf16[2,384,5,768]{3,1,0,2:T(8,128)(2,1)} %copy-done.14, bf16[2,384,768]{2,1,0:T(8,128)(2,1)S(1)} %get-tuple-element.39, s32[384]{0:T(512)S(1)} %bitcast.139), kind=kOutput, calls=%fused_computation.6 | convolution fusion | flops 2718498816 | bytes 12977664 | tf_op jit(solution)/shard_map/blo,blki->oki/dot_general | solution.py:106
  24.4 2.6 %collective-permute-start.2 = (f32[384,5,768]{2,0,1:T(8,128)}, f32[384,5,768]{2,0,1:T(8,128)}, u32[]{:S(2)}, u32[]{:S(2)}) collective-permute-start(f32[384,5,768]{2,0,1:T(8,128)} %convolution_bitcast_fusion), channel_id=1, source_target_pairs={{0,16},{16,0},{32,48},{48,32},{64,80},{80,64},{96,112},{112,96},{1... | collective-permute-start | bytes 17694728 | tf_op jit(solution)/shard_map/ppermute | solution.py:111
  28.3 3.2 %collective-permute-start.3 = (bf16[2,2,768]{2,1,0:T(2,128)(2,1)S(1)}, bf16[2,2,768]{2,1,0:T(2,128)(2,1)S(1)}, u32[]{:S(2)}, u32[]{:S(2)}) collective-permute-start(bf16[2,2,768]{2,1,0:T(2,128)(2,1)S(1)} %get-tuple-element.33), channel_id=1, source_target_pairs={{0,16},{16,32},{32,48},{48,64},{64,80},{80,96},{96,112},{112,128},... | collective-permute-start | bytes 18440 | tf_op jit(solution)/shard_map/ppermute | solution.py:17
  37.8 10.6 %bitcast_add_fusion = f32[384,5,768]{2,0,1:T(8,128)} fusion(f32[384,5,768]{2,0,1:T(8,128)} %collective-permute-done.2, bf16[2,384,5,768]{3,1,0,2:T(8,128)(2,1)} %copy-done.14, bf16[2,384,768]{2,1,0:T(8,128)(2,1)} %copy-done.12, s32[384]{0:T(512)S(1)} %bitcast.138), kind=kOutput, calls=%fused_computation.4 | convolution fusion | flops 2719973376 | bytes 18875904 | tf_op jit(solution)/shard_map/blo,blki->oki/dot_general | solution.py:106
  48.4 3.5 %fusion.51 = (f32[1,128,5,768]{3,1,2,0:T(8,128)S(1)}, f32[1,128,5,768]{3,1,2,0:T(8,128)S(1)}, f32[1,128,5,768]{3,1,2,0:T(8,128)S(1)}) fusion(f32[3,128,5,768]{3,1,0,2:T(8,128)} %bitcast.133), kind=kLoop, calls=%fused_computation.106 | loop fusion | bytes 11796480 | tf_op jit(solution)/shard_map/slice | solution.py:142
  55.9 3.0 %collective-permute-start.8 = (f32[64,5,768]{2,0,1:T(8,128)}, f32[64,5,768]{2,0,1:T(8,128)}, u32[]{:S(2)}, u32[]{:S(2)}) collective-permute-start(f32[64,5,768]{2,0,1:T(8,128)} %dynamic-slice_bitcast_fusion.1), channel_id=1, source_target_pairs={{0,32},{16,48},{32,0},{48,16},{64,96},{80,112},{96,64},{112,80},{1... | collective-permute-start | bytes 2949128 | tf_op jit(solution)/shard_map/ppermute | solution.py:32
  60.0 3.5 %collective-permute-start.5 = (f32[64,5,768]{2,0,1:T(8,128)}, f32[64,5,768]{2,0,1:T(8,128)}, u32[]{:S(2)}, u32[]{:S(2)}) collective-permute-start(f32[64,5,768]{2,0,1:T(8,128)} %dynamic-slice_bitcast_fusion.2), channel_id=1, source_target_pairs={{0,64},{16,80},{32,96},{48,112},{64,0},{80,16},{96,32},{112,48},{1... | collective-permute-start | bytes 2949128 | tf_op jit(solution)/shard_map/ppermute | solution.py:32
  65.8 6.2 %bitcast_add_fusion.1 = f32[2,384,768]{2,1,0:T(8,128)} fusion(f32[2,384,768]{2,1,0:T(8,128)S(1)} %copy-done.2, bf16[2,384,5,768]{3,1,0,2:T(8,128)(2,1)S(1)} %bitcast_dynamic-update-slice_fusion.5, bf16[5,768,768]{2,1,0:T(8,128)(2,1)S(1)} %bitcast.141), kind=kOutput, calls=%fused_computation.11 | convolution fusion | flops 4530438144 | bytes 16515072 | tf_op jit(solution)/shard_map/blki,kio->blo/dot_general | solution.py:128
  72.0 4.0 %reshape.61 = f32[2,192,2,768]{3,2,1,0:T(2,128)} reshape(f32[2,384,768]{2,1,0:T(8,128)} %bitcast_add_fusion.1) | data formatting | bytes 4718592 | tf_op jit(solution)/shard_map/reshape | solution.py:130
  76.0 4.4 %fusion.52 = (f32[2,192,1,768]{3,2,1,0:T(1,128)S(1)}, f32[2,192,1,768]{3,2,1,0:T(1,128)S(1)}) fusion(f32[2,192,2,768]{3,2,1,0:T(2,128)} %reshape.61), kind=kLoop, calls=%fused_computation.107 | loop fusion | bytes 4718592 | tf_op jit(solution)/shard_map/slice | solution.py:131
  82.3 5.5 %all-to-all-start = ((bf16[2,192,768]{1,0,2:T(2,128)(2,1)}), bf16[2,192,768]{1,0,2:T(2,128)(2,1)S(1)}, u32[]{:S(2)}, u32[]{:S(2)}) async-start(bf16[2,192,768]{1,0,2:T(2,128)(2,1)} %copy.39), calls=%async_computation | async-start | bytes 1572864 | tf_op jit(solution)/shard_map/all_to_all | solution.py:132
  89.0 2.5 %copy-done.15 = bf16[2,384,5,768]{3,1,0,2:T(8,128)(2,1)} copy-done((bf16[2,384,5,768]{3,1,0,2:T(8,128)(2,1)}, bf16[2,384,5,768]{3,1,0,2:T(8,128)(2,1)S(1)}, u32[]{:S(2)}) %copy-start.15) | copy-done | bytes 5898264
  91.8 11.3 %all-to-all-done = bf16[2,192,768]{1,0,2:T(2,128)(2,1)S(1)} async-done(((bf16[2,192,768]{1,0,2:T(2,128)(2,1)}), bf16[2,192,768]{1,0,2:T(2,128)(2,1)S(1)}, u32[]{:S(2)}, u32[]{:S(2)}) %all-to-all-start) | async-done | bytes 589856 | tf_op jit(solution)/shard_map/all_to_all | solution.py:132
  111.6 8.1 %collective-permute-done.12 = f32[64,5,384]{2,0,1:T(8,128)S(1)} collective-permute-done((f32[64,5,384]{2,0,1:T(8,128)S(1)}, f32[64,5,384]{2,0,1:T(8,128)S(1)}, u32[]{:S(2)}, u32[]{:S(2)}) %collective-permute-start.12) | collective-permute-done | bytes 491552 | tf_op jit(solution)/shard_map/ppermute | solution.py:32
  121.2 2.8 %collective-permute-done.6 = f32[32,5,768]{2,0,1:T(8,128)S(1)} collective-permute-done((f32[32,5,768]{2,0,1:T(8,128)S(1)}, f32[32,5,768]{2,0,1:T(8,128)S(1)}, u32[]{:S(2)}, u32[]{:S(2)}) %collective-permute-start.6) | collective-permute-done | bytes 491552 | tf_op jit(solution)/shard_map/ppermute | solution.py:32
  124.6 2.3 %collective-permute-start.10 = (f32[32,5,384]{2,0,1:T(8,128)S(1)}, f32[32,5,384]{2,0,1:T(8,128)S(1)}, u32[]{:S(2)}, u32[]{:S(2)}) collective-permute-start(f32[32,5,384]{2,0,1:T(8,128)S(1)} %constant_dynamic-slice_fusion.6), channel_id=1, source_target_pairs={{0,64},{16,80},{32,96},{48,112},{64,0},{80,16},{96,32},{112,48},{1... | collective-permute-start | bytes 737288 | tf_op jit(solution)/shard_map/ppermute | solution.py:32
  131.8 6.8 %collective-permute-start.14 = (f32[3,32,5,192]{3,1,2,0:T(8,128)S(1)}, f32[3,32,5,192]{3,1,2,0:T(8,128)S(1)}, u32[]{:S(2)}, u32[]{:S(2)}) collective-permute-start(f32[3,32,5,192]{3,1,2,0:T(8,128)S(1)} %constant_dynamic-slice_fusion.3), channel_id=1, source_target_pairs={{0,4},{1,5},{2,6},{3,7},{4,0},{5,1},{6,2},{7,3},{8,12},{9,13},{10,... | collective-permute-start | bytes 1105928 | tf_op jit(solution)/shard_map/ppermute | solution.py:32
  138.7 18.2 %collective-permute-done.14 = f32[3,32,5,192]{3,1,2,0:T(8,128)S(1)} collective-permute-done((f32[3,32,5,192]{3,1,2,0:T(8,128)S(1)}, f32[3,32,5,192]{3,1,2,0:T(8,128)S(1)}, u32[]{:S(2)}, u32[]{:S(2)}) %collective-permute-start.14) | collective-permute-done | bytes 368672 | tf_op jit(solution)/shard_map/ppermute | solution.py:32
  157.3 5.4 %multiply_reduce_fusion = (f32[2,384]{1,0:T(2,128)S(1)}, f32[2,384,768]{2,1,0:T(8,128)S(1)}) fusion(f32[2,384,768]{2,1,0:T(8,128)S(1)} %copy-done.4, f32[2,384]{1,0:T(2,128)S(1)} %get-tuple-element.38, bf16[2,384,5,768]{3,1,0,2:T(8,128)(2,1)S(1)} %bitcast_dynamic-update-slice_fusion, bf16[5,768,768]{2,1,0:T(8,128)(2,1)S(1)} %bitcast.143), kind=kOutput, calls=%fused_computation.13 | convolution fusion | flops 4536925184 | bytes 16521216 | tf_op jit(solution)/shard_map/blko,kio->bli/dot_general | solution.py:121
  162.7 2.3 %collective-permute-done.15 = f32[3,16,5,192]{3,1,2,0:T(8,128)S(1)} collective-permute-done((f32[3,16,5,192]{3,1,2,0:T(8,128)S(1)}, f32[3,16,5,192]{3,1,2,0:T(8,128)S(1)}, u32[]{:S(2)}, u32[]{:S(2)}) %collective-permute-start.15) | collective-permute-done | bytes 184352 | tf_op jit(solution)/shard_map/ppermute | solution.py:32
  166.6 3.4 %collective-permute-done.16 = f32[3,16,5,96]{3,1,2,0:T(8,128)S(1)} collective-permute-done((f32[3,16,5,96]{3,1,2,0:T(8,128)S(1)}, f32[3,16,5,96]{3,1,2,0:T(8,128)S(1)}, u32[]{:S(2)}, u32[]{:S(2)}) %collective-permute-start.16) | collective-permute-done | bytes 92192 | tf_op jit(solution)/shard_map/ppermute | solution.py:32
  170.3 4.8 %collective-permute-start.17 = (f32[3,16,5,48]{3,1,2,0:T(8,128)S(1)}, f32[3,16,5,48]{3,1,2,0:T(8,128)S(1)}, u32[]{:S(2)}, u32[]{:S(2)}) collective-permute-start(f32[3,16,5,48]{3,1,2,0:T(8,128)S(1)} %constant_dynamic-slice_fusion), channel_id=1, source_target_pairs={{0,2},{1,3},{2,0},{3,1},{4,6},{5,7},{6,4},{7,5},{8,10},{9,11},{10,... | collective-permute-start | bytes 138248 | tf_op jit(solution)/shard_map/ppermute | solution.py:32
  (138 shorter events, 49.8 us)
Async XLA Ops:
  4.2 6.4 %collective-permute-start.1 = (bf16[2,2,768]{2,1,0:T(2,128)(2,1)S(1)}, bf16[2,2,768]{2,1,0:T(2,128)(2,1)S(1)}, u32[]{:S(2)}, u32[]{:S(2)}) collective-permute-start(bf16[2,2,768]{2,1,0:T(2,128)(2,1)S(1)} %get-tuple-element.36), channel_id=1, source_target_pairs={{16,0},{32,16},{48,32},{64,48},{80,64},{96,80},{112,96},{128,112},... | collective-permute-start | bytes 18440 | tf_op jit(solution)/shard_map/ppermute | solution.py:20
  5.6 5.0 %collective-permute-start = (bf16[2,2,768]{2,1,0:T(2,128)(2,1)S(1)}, bf16[2,2,768]{2,1,0:T(2,128)(2,1)S(1)}, u32[]{:S(2)}, u32[]{:S(2)}) collective-permute-start(bf16[2,2,768]{2,1,0:T(2,128)(2,1)S(1)} %get-tuple-element.35), channel_id=1, source_target_pairs={{0,16},{16,32},{32,48},{48,64},{64,80},{80,96},{96,112},{112,128},... | collective-permute-start | bytes 18440 | tf_op jit(solution)/shard_map/ppermute | solution.py:17
  24.4 13.4 %collective-permute-start.2 = (f32[384,5,768]{2,0,1:T(8,128)}, f32[384,5,768]{2,0,1:T(8,128)}, u32[]{:S(2)}, u32[]{:S(2)}) collective-permute-start(f32[384,5,768]{2,0,1:T(8,128)} %convolution_bitcast_fusion), channel_id=1, source_target_pairs={{0,16},{16,0},{32,48},{48,32},{64,80},{80,64},{96,112},{112,96},{1... | collective-permute-start | bytes 17694728 | tf_op jit(solution)/shard_map/ppermute | solution.py:111
  27.0 9.1 %collective-permute-start.4 = (bf16[2,2,768]{2,1,0:T(2,128)(2,1)S(1)}, bf16[2,2,768]{2,1,0:T(2,128)(2,1)S(1)}, u32[]{:S(2)}, u32[]{:S(2)}) collective-permute-start(bf16[2,2,768]{2,1,0:T(2,128)(2,1)S(1)} %get-tuple-element.34), channel_id=1, source_target_pairs={{16,0},{32,16},{48,32},{64,48},{80,64},{96,80},{112,96},{128,112},... | collective-permute-start | bytes 18440 | tf_op jit(solution)/shard_map/ppermute | solution.py:20
  28.3 7.9 %collective-permute-start.3 = (bf16[2,2,768]{2,1,0:T(2,128)(2,1)S(1)}, bf16[2,2,768]{2,1,0:T(2,128)(2,1)S(1)}, u32[]{:S(2)}, u32[]{:S(2)}) collective-permute-start(bf16[2,2,768]{2,1,0:T(2,128)(2,1)S(1)} %get-tuple-element.33), channel_id=1, source_target_pairs={{0,16},{16,32},{32,48},{48,64},{64,80},{80,96},{96,112},{112,128},... | collective-permute-start | bytes 18440 | tf_op jit(solution)/shard_map/ppermute | solution.py:17
  53.0 52.1 %collective-permute-start.11 = (f32[128,5,384]{2,0,1:T(8,128)}, f32[128,5,384]{2,0,1:T(8,128)}, u32[]{:S(2)}, u32[]{:S(2)}) collective-permute-start(f32[128,5,384]{2,0,1:T(8,128)} %dynamic-slice_bitcast_fusion), channel_id=1, source_target_pairs={{0,1},{1,0},{2,3},{3,2},{4,5},{5,4},{6,7},{7,6},{8,9},{9,8},{10,11... | collective-permute-start | bytes 2949128 | tf_op jit(solution)/shard_map/ppermute | solution.py:32
  55.9 53.9 %collective-permute-start.8 = (f32[64,5,768]{2,0,1:T(8,128)}, f32[64,5,768]{2,0,1:T(8,128)}, u32[]{:S(2)}, u32[]{:S(2)}) collective-permute-start(f32[64,5,768]{2,0,1:T(8,128)} %dynamic-slice_bitcast_fusion.1), channel_id=1, source_target_pairs={{0,32},{16,48},{32,0},{48,16},{64,96},{80,112},{96,64},{112,80},{1... | collective-permute-start | bytes 2949128 | tf_op jit(solution)/shard_map/ppermute | solution.py:32
  60.0 47.0 %collective-permute-start.5 = (f32[64,5,768]{2,0,1:T(8,128)}, f32[64,5,768]{2,0,1:T(8,128)}, u32[]{:S(2)}, u32[]{:S(2)}) collective-permute-start(f32[64,5,768]{2,0,1:T(8,128)} %dynamic-slice_bitcast_fusion.2), channel_id=1, source_target_pairs={{0,64},{16,80},{32,96},{48,112},{64,0},{80,16},{96,32},{112,48},{1... | collective-permute-start | bytes 2949128 | tf_op jit(solution)/shard_map/ppermute | solution.py:32
  82.3 20.7 %all-to-all-start = ((bf16[2,192,768]{1,0,2:T(2,128)(2,1)}), bf16[2,192,768]{1,0,2:T(2,128)(2,1)S(1)}, u32[]{:S(2)}, u32[]{:S(2)}) async-start(bf16[2,192,768]{1,0,2:T(2,128)(2,1)} %copy.39), calls=%async_computation | async-start | bytes 1572864 | tf_op jit(solution)/shard_map/all_to_all | solution.py:132
  106.9 12.8 %collective-permute-start.12 = (f32[64,5,384]{2,0,1:T(8,128)S(1)}, f32[64,5,384]{2,0,1:T(8,128)S(1)}, u32[]{:S(2)}, u32[]{:S(2)}) collective-permute-start(f32[64,5,384]{2,0,1:T(8,128)S(1)} %constant_dynamic-slice_fusion.5), channel_id=1, source_target_pairs={{0,64},{16,80},{32,96},{48,112},{64,0},{80,16},{96,32},{112,48},{1... | collective-permute-start | bytes 1474568 | tf_op jit(solution)/shard_map/ppermute | solution.py:32
  107.2 50.1 %slice-start.4 = ((s8[5898240]{0:T(1024)(128)(4,1)}), s8[4194304]{0:T(1024)(128)(4,1)S(1)}, s32[]{:S(2)}) async-start(s8[5898240]{0:T(1024)(128)(4,1)} %bitcast.142), calls=%async_computation.5 | async-start | bytes 8388608
  108.8 15.2 %collective-permute-start.6 = (f32[32,5,768]{2,0,1:T(8,128)S(1)}, f32[32,5,768]{2,0,1:T(8,128)S(1)}, u32[]{:S(2)}, u32[]{:S(2)}) collective-permute-start(f32[32,5,768]{2,0,1:T(8,128)S(1)} %constant_dynamic-slice_fusion.9), channel_id=1, source_target_pairs={{0,32},{16,48},{32,0},{48,16},{64,96},{80,112},{96,64},{112,80},{1... | collective-permute-start | bytes 1474568 | tf_op jit(solution)/shard_map/ppermute | solution.py:32
  109.9 28.7 %slice-start = ((s8[5898240]{0:T(1024)(128)(4,1)}), s8[4194304]{0:T(1024)(128)(4,1)S(1)}, s32[]{:S(2)}) async-start(s8[5898240]{0:T(1024)(128)(4,1)} %bitcast.136), calls=%async_computation.1 | async-start | bytes 8388608
  111.4 13.0 %collective-permute-start.9 = (f32[64,5,384]{2,0,1:T(8,128)S(1)}, f32[64,5,384]{2,0,1:T(8,128)S(1)}, u32[]{:S(2)}, u32[]{:S(2)}) collective-permute-start(f32[64,5,384]{2,0,1:T(8,128)S(1)} %constant_dynamic-slice_fusion.7), channel_id=1, source_target_pairs={{0,1},{1,0},{2,3},{3,2},{4,5},{5,4},{6,7},{7,6},{8,9},{9,8},{10,11... | collective-permute-start | bytes 1474568 | tf_op jit(solution)/shard_map/ppermute | solution.py:32
  119.8 18.8 %slice-start.1 = ((s8[5898240]{0:T(1024)(128)(4,1)}), s8[1703936]{0:T(1024)(128)(4,1)S(1)}, s32[]{:S(2)}) async-start(s8[5898240]{0:T(1024)(128)(4,1)} %bitcast.136), calls=%async_computation.2 | async-start | bytes 3407872
  119.8 8.8 %collective-permute-start.13 = (f32[32,5,384]{2,0,1:T(8,128)S(1)}, f32[32,5,384]{2,0,1:T(8,128)S(1)}, u32[]{:S(2)}, u32[]{:S(2)}) collective-permute-start(f32[32,5,384]{2,0,1:T(8,128)S(1)} %constant_dynamic-slice_fusion.4), channel_id=1, source_target_pairs={{0,32},{16,48},{32,0},{48,16},{64,96},{80,112},{96,64},{112,80},{1... | collective-permute-start | bytes 737288 | tf_op jit(solution)/shard_map/ppermute | solution.py:32
  124.0 33.3 %slice-start.5 = ((s8[5898240]{0:T(1024)(128)(4,1)}), s8[1703936]{0:T(1024)(128)(4,1)S(1)}, s32[]{:S(2)}) async-start(s8[5898240]{0:T(1024)(128)(4,1)} %bitcast.142), calls=%async_computation.6 | async-start | bytes 3407872
  124.1 6.3 %collective-permute-start.7 = (f32[32,5,384]{2,0,1:T(8,128)S(1)}, f32[32,5,384]{2,0,1:T(8,128)S(1)}, u32[]{:S(2)}, u32[]{:S(2)}) collective-permute-start(f32[32,5,384]{2,0,1:T(8,128)S(1)} %constant_dynamic-slice_fusion.8), channel_id=1, source_target_pairs={{0,1},{1,0},{2,3},{3,2},{4,5},{5,4},{6,7},{7,6},{8,9},{9,8},{10,11... | collective-permute-start | bytes 737288 | tf_op jit(solution)/shard_map/ppermute | solution.py:32
  124.6 6.9 %collective-permute-start.10 = (f32[32,5,384]{2,0,1:T(8,128)S(1)}, f32[32,5,384]{2,0,1:T(8,128)S(1)}, u32[]{:S(2)}, u32[]{:S(2)}) collective-permute-start(f32[32,5,384]{2,0,1:T(8,128)S(1)} %constant_dynamic-slice_fusion.6), channel_id=1, source_target_pairs={{0,64},{16,80},{32,96},{48,112},{64,0},{80,16},{96,32},{112,48},{1... | collective-permute-start | bytes 737288 | tf_op jit(solution)/shard_map/ppermute | solution.py:32
  131.8 25.5 %copy-start.4 = (f32[2,384,768]{2,1,0:T(8,128)S(1)}, f32[2,384,768]{2,1,0:T(8,128)}, u32[]{:S(2)}) copy-start(f32[2,384,768]{2,1,0:T(8,128)} %convert_element_type.33) | copy-start | bytes 7077892
  131.8 25.2 %collective-permute-start.14 = (f32[3,32,5,192]{3,1,2,0:T(8,128)S(1)}, f32[3,32,5,192]{3,1,2,0:T(8,128)S(1)}, u32[]{:S(2)}, u32[]{:S(2)}) collective-permute-start(f32[3,32,5,192]{3,1,2,0:T(8,128)S(1)} %constant_dynamic-slice_fusion.3), channel_id=1, source_target_pairs={{0,4},{1,5},{2,6},{3,7},{4,0},{5,1},{6,2},{7,3},{8,12},{9,13},{10,... | collective-permute-start | bytes 1105928 | tf_op jit(solution)/shard_map/ppermute | solution.py:32
  157.2 7.8 %collective-permute-start.15 = (f32[3,16,5,192]{3,1,2,0:T(8,128)S(1)}, f32[3,16,5,192]{3,1,2,0:T(8,128)S(1)}, u32[]{:S(2)}, u32[]{:S(2)}) collective-permute-start(f32[3,16,5,192]{3,1,2,0:T(8,128)S(1)} %constant_dynamic-slice_fusion.2), channel_id=1, source_target_pairs={{0,128},{16,144},{32,160},{48,176},{64,192},{80,208},{96,224},{112... | collective-permute-start | bytes 552968 | tf_op jit(solution)/shard_map/ppermute | solution.py:32
  165.1 5.0 %collective-permute-start.16 = (f32[3,16,5,96]{3,1,2,0:T(8,128)S(1)}, f32[3,16,5,96]{3,1,2,0:T(8,128)S(1)}, u32[]{:S(2)}, u32[]{:S(2)}) collective-permute-start(f32[3,16,5,96]{3,1,2,0:T(8,128)S(1)} %constant_dynamic-slice_fusion.1), channel_id=1, source_target_pairs={{0,8},{1,9},{2,10},{3,11},{4,12},{5,13},{6,14},{7,15},{8,0},{9,1},... | collective-permute-start | bytes 276488 | tf_op jit(solution)/shard_map/ppermute | solution.py:32
  170.3 8.4 %collective-permute-start.17 = (f32[3,16,5,48]{3,1,2,0:T(8,128)S(1)}, f32[3,16,5,48]{3,1,2,0:T(8,128)S(1)}, u32[]{:S(2)}, u32[]{:S(2)}) collective-permute-start(f32[3,16,5,48]{3,1,2,0:T(8,128)S(1)} %constant_dynamic-slice_fusion), channel_id=1, source_target_pairs={{0,2},{1,3},{2,0},{3,1},{4,6},{5,7},{6,4},{7,5},{8,10},{9,11},{10,... | collective-permute-start | bytes 138248 | tf_op jit(solution)/shard_map/ppermute | solution.py:32
  (19 other events, 149.1 us)

commit v5 on v0

--- a/solution.py
+++ b/solution.py
@@ -133,10 +133,13 @@
     shared = [step for step in range(len(CHAINS[0])) if len({steps[step] for steps in CHAINS}) == 1]
     for step in range(1, len(CHAINS[0])):
         if step in shared:
-            if isinstance(partial, list):
-                partial, trunk_input = lax.optimization_barrier((jnp.stack(partial), trunk_input))
+            joining = isinstance(partial, list)
+            if joining:
+                partial = jnp.stack(partial)
             axis, bit = CHAINS[0][step]
             partial = halved(partial, axis, bit, 1 if axis == "seq" else 3)
+            if joining:
+                partial, trunk_input = lax.optimization_barrier((partial, trunk_input))
         else:
             partial = [
                 halved(partial[piece], axis, bit, 0 if axis == "seq" else 2)

time: 170 us -> 166 us (0.976)
  waiting for transfers between devices: 41.9 us -> 23.5 us
  starting transfers between devices: 45.9 us -> 51.5 us
  local copies, waits for them, and re-layouts: 30.3 us -> 35.9 us
  matrix products: 34 us -> 38 us
    all_to_all x1, waiting for transfers between devices: 11.3 us -> 0.01 us  [shards(): lax.all_to_all(pooled, 'seq', split_axis=2, concat_axis=1, tiled=True)]
    ppermute x13, waiting for transfers between devices: 29 us -> 22 us  [halved(): return keep + lax.ppermute(send, axis, partners)]
    ppermute x13, starting transfers between devices: 28.9 us -> 34.4 us  [halved(): return keep + lax.ppermute(send, axis, partners)]
    dot_general x1, matrix products: 5.36 us -> 9.28 us  [shards(): jnp.einsum('blko,kio->bli', grad_window, weight, preferred_element_type=j...]
    unnamed x61 -> x55, local copies, waits for them, and re-layouts: 10.2 us -> 13 us
    all_to_all x3, local copies, waits for them, and re-layouts: 2 us -> 3.79 us  [shards(): lax.all_to_all(pooled, 'seq', split_axis=2, concat_axis=1, tiled=True)]
  transfers between devices with their start and end apart: 19 -> 19, of which waited for: 12 -> 10; matrix products, arithmetic and copies ran while one was open for 24% -> 30% of each run, Pallas kernels for 0% -> 0%
where the time goes in v5:
time: 166 us
  starting transfers between devices  51.5 us (31%)
  matrix products  38 us (23%)
  local copies, waits for them, and re-layouts  35.9 us (22%)
  waiting for transfers between devices  23.5 us (14%)
  other arithmetic  15.7 us (9%)
    ppermute x13, starting transfers between devices, halved(): return keep + lax.ppermute(send, axis, partners)  34.4 us
    ppermute x13, waiting for transfers between devices, halved(): return keep + lax.ppermute(send, axis, partners)  22 us
    dot_general x2, matrix products, shards(): jnp.einsum('blo,blki->oki', picked(branch_grad, chosen), act_window, pref...  19.2 us
    unnamed x55, local copies, waits for them, and re-layouts  13 us
    dot_general x1, matrix products, shards(): jnp.einsum('blko,kio->bli', grad_window, weight, preferred_element_type=j...  9.28 us
    ppermute x2, starting transfers between devices, with_halo(): lax.ppermute(lax.slice_in_dim(block, block.shape[dim] - width, None, axis...  6.24 us
    dot_general x1, matrix products, shards(): jnp.einsum('blki,kio->blo', window, weight, preferred_element_type=jnp.fl...  6.17 us
    all_to_all x1, starting transfers between devices, shards(): lax.all_to_all(pooled, 'seq', split_axis=2, concat_axis=1, tiled=True)  5.56 us
  transfers between devices with their start and end apart: 19, of which 10 were waited for; matrix products, arithmetic and copies ran while one was open for 30% of the time, Pallas kernels for 0%

profile of v5, /device:TPU:2, one launch (start us, length us, event | category | flops | bytes accessed | tf_op | source)
XLA Modules:
  0.0 165.8 jit_solution(12801460791441967450)
XLA Ops:
  5.6 3.0 %collective-permute-start = (bf16[2,2,768]{2,1,0:T(2,128)(2,1)S(1)}, bf16[2,2,768]{2,1,0:T(2,128)(2,1)S(1)}, u32[]{:S(2)}, u32[]{:S(2)}) collective-permute-start(bf16[2,2,768]{2,1,0:T(2,128)(2,1)S(1)} %get-tuple-element.35), channel_id=1, source_target_pairs={{0,16},{16,32},{32,48},{48,64},{64,80},{80,96},{96,112},{112,128},... | collective-permute-start | bytes 18440 | tf_op jit(solution)/shard_map/ppermute | solution.py:17
  13.3 2.5 %copy-done.16 = bf16[2,384,5,768]{3,1,0,2:T(8,128)(2,1)} copy-done((bf16[2,384,5,768]{3,1,0,2:T(8,128)(2,1)}, bf16[2,384,5,768]{3,1,0,2:T(8,128)(2,1)S(1)}, u32[]{:S(2)}) %copy-start.16) | copy-done | bytes 5898264
  15.8 8.6 %convolution_bitcast_fusion = f32[384,5,768]{2,0,1:T(8,128)} fusion(bf16[2,384,5,768]{3,1,0,2:T(8,128)(2,1)} %copy-done.16, bf16[2,384,768]{2,1,0:T(8,128)(2,1)S(1)} %get-tuple-element.39, s32[384]{0:T(512)S(1)} %bitcast.137), kind=kOutput, calls=%fused_computation.6 | convolution fusion | flops 2718498816 | bytes 12977664 | tf_op jit(solution)/shard_map/blo,blki->oki/dot_general | solution.py:106
  24.4 2.6 %collective-permute-start.2 = (f32[384,5,768]{2,0,1:T(8,128)}, f32[384,5,768]{2,0,1:T(8,128)}, u32[]{:S(2)}, u32[]{:S(2)}) collective-permute-start(f32[384,5,768]{2,0,1:T(8,128)} %convolution_bitcast_fusion), channel_id=1, source_target_pairs={{0,16},{16,0},{32,48},{48,32},{64,80},{80,64},{96,112},{112,96},{1... | collective-permute-start | bytes 17694728 | tf_op jit(solution)/shard_map/ppermute | solution.py:111
  28.3 3.2 %collective-permute-start.3 = (bf16[2,2,768]{2,1,0:T(2,128)(2,1)S(1)}, bf16[2,2,768]{2,1,0:T(2,128)(2,1)S(1)}, u32[]{:S(2)}, u32[]{:S(2)}) collective-permute-start(bf16[2,2,768]{2,1,0:T(2,128)(2,1)S(1)} %get-tuple-element.33), channel_id=1, source_target_pairs={{0,16},{16,32},{32,48},{48,64},{64,80},{80,96},{96,112},{112,128},... | collective-permute-start | bytes 18440 | tf_op jit(solution)/shard_map/ppermute | solution.py:17
  37.8 10.6 %bitcast_add_fusion = f32[384,5,768]{2,0,1:T(8,128)} fusion(f32[384,5,768]{2,0,1:T(8,128)} %collective-permute-done.2, bf16[2,384,5,768]{3,1,0,2:T(8,128)(2,1)} %copy-done.16, bf16[2,384,768]{2,1,0:T(8,128)(2,1)} %copy-done.13, s32[384]{0:T(512)S(1)} %bitcast.136), kind=kOutput, calls=%fused_computation.4 | convolution fusion | flops 2719973376 | bytes 18875904 | tf_op jit(solution)/shard_map/blo,blki->oki/dot_general | solution.py:106
  48.4 3.5 %fusion.51 = (f32[1,128,5,768]{3,1,2,0:T(8,128)S(1)}, f32[1,128,5,768]{3,1,2,0:T(8,128)S(1)}, f32[1,128,5,768]{3,1,2,0:T(8,128)S(1)}) fusion(f32[3,128,5,768]{3,1,0,2:T(8,128)} %bitcast.133), kind=kLoop, calls=%fused_computation.106 | loop fusion | bytes 11796480 | tf_op jit(solution)/shard_map/slice | solution.py:145
  56.0 3.0 %collective-permute-start.8 = (f32[64,5,768]{2,0,1:T(8,128)}, f32[64,5,768]{2,0,1:T(8,128)}, u32[]{:S(2)}, u32[]{:S(2)}) collective-permute-start(f32[64,5,768]{2,0,1:T(8,128)} %dynamic-slice_bitcast_fusion.1), channel_id=1, source_target_pairs={{0,32},{16,48},{32,0},{48,16},{64,96},{80,112},{96,64},{112,80},{1... | collective-permute-start | bytes 2949128 | tf_op jit(solution)/shard_map/ppermute | solution.py:32
  60.1 3.4 %collective-permute-start.5 = (f32[64,5,768]{2,0,1:T(8,128)}, f32[64,5,768]{2,0,1:T(8,128)}, u32[]{:S(2)}, u32[]{:S(2)}) collective-permute-start(f32[64,5,768]{2,0,1:T(8,128)} %dynamic-slice_bitcast_fusion.2), channel_id=1, source_target_pairs={{0,64},{16,80},{32,96},{48,112},{64,0},{80,16},{96,32},{112,48},{1... | collective-permute-start | bytes 2949128 | tf_op jit(solution)/shard_map/ppermute | solution.py:32
  65.9 6.2 %bitcast_add_fusion.1 = f32[2,384,768]{2,1,0:T(8,128)} fusion(f32[2,384,768]{2,1,0:T(8,128)S(1)} %copy-done.2, bf16[2,384,5,768]{3,1,0,2:T(8,128)(2,1)S(1)} %bitcast_dynamic-update-slice_fusion.5, bf16[5,768,768]{2,1,0:T(8,128)(2,1)S(1)} %bitcast.139), kind=kOutput, calls=%fused_computation.11 | convolution fusion | flops 4530438144 | bytes 16515072 | tf_op jit(solution)/shard_map/blki,kio->blo/dot_general | solution.py:128
  72.0 4.0 %reshape.61 = f32[2,192,2,768]{3,2,1,0:T(2,128)} reshape(f32[2,384,768]{2,1,0:T(8,128)} %bitcast_add_fusion.1) | data formatting | bytes 4718592 | tf_op jit(solution)/shard_map/reshape | solution.py:130
  76.0 4.4 %fusion.52 = (f32[2,192,1,768]{3,2,1,0:T(1,128)S(1)}, f32[2,192,1,768]{3,2,1,0:T(1,128)S(1)}) fusion(f32[2,192,2,768]{3,2,1,0:T(2,128)} %reshape.61), kind=kLoop, calls=%fused_computation.107 | loop fusion | bytes 4718592 | tf_op jit(solution)/shard_map/slice | solution.py:131
  82.4 5.6 %all-to-all-start = ((bf16[2,192,768]{1,0,2:T(2,128)(2,1)}), bf16[2,192,768]{1,0,2:T(2,128)(2,1)S(1)}, u32[]{:S(2)}, u32[]{:S(2)}) async-start(bf16[2,192,768]{1,0,2:T(2,128)(2,1)} %copy.39), calls=%async_computation | async-start | bytes 1572864 | tf_op jit(solution)/shard_map/all_to_all | solution.py:132
  98.8 3.1 %collective-permute-start.6 = (f32[32,5,768]{2,0,1:T(8,128)S(1)}, f32[32,5,768]{2,0,1:T(8,128)S(1)}, u32[]{:S(2)}, u32[]{:S(2)}) collective-permute-start(f32[32,5,768]{2,0,1:T(8,128)S(1)} %constant_dynamic-slice_fusion.9), channel_id=1, source_target_pairs={{0,32},{16,48},{32,0},{48,16},{64,96},{80,112},{96,64},{112,80},{1... | collective-permute-start | bytes 1474568 | tf_op jit(solution)/shard_map/ppermute | solution.py:32
  103.4 7.0 %collective-permute-done.12 = f32[64,5,384]{2,0,1:T(8,128)S(1)} collective-permute-done((f32[64,5,384]{2,0,1:T(8,128)S(1)}, f32[64,5,384]{2,0,1:T(8,128)S(1)}, u32[]{:S(2)}, u32[]{:S(2)}) %collective-permute-start.12) | collective-permute-done | bytes 491552 | tf_op jit(solution)/shard_map/ppermute | solution.py:32
  110.5 3.0 %collective-permute-start.13 = (f32[32,5,384]{2,0,1:T(8,128)S(1)}, f32[32,5,384]{2,0,1:T(8,128)S(1)}, u32[]{:S(2)}, u32[]{:S(2)}) collective-permute-start(f32[32,5,384]{2,0,1:T(8,128)S(1)} %constant_dynamic-slice_fusion.4), channel_id=1, source_target_pairs={{0,32},{16,48},{32,0},{48,16},{64,96},{80,112},{96,64},{112,80},{1... | collective-permute-start | bytes 737288 | tf_op jit(solution)/shard_map/ppermute | solution.py:32
  113.7 2.6 %collective-permute-done.9 = f32[64,5,384]{2,0,1:T(8,128)S(1)} collective-permute-done((f32[64,5,384]{2,0,1:T(8,128)S(1)}, f32[64,5,384]{2,0,1:T(8,128)S(1)}, u32[]{:S(2)}, u32[]{:S(2)}) %collective-permute-start.9) | collective-permute-done | bytes 491552 | tf_op jit(solution)/shard_map/ppermute | solution.py:32
  117.6 2.7 %collective-permute-done.13 = f32[32,5,384]{2,0,1:T(8,128)S(1)} collective-permute-done((f32[32,5,384]{2,0,1:T(8,128)S(1)}, f32[32,5,384]{2,0,1:T(8,128)S(1)}, u32[]{:S(2)}, u32[]{:S(2)}) %collective-permute-start.13) | collective-permute-done | bytes 245792 | tf_op jit(solution)/shard_map/ppermute | solution.py:32
  123.7 2.8 %collective-permute-start.14 = (f32[3,16,5,384]{3,1,2,0:T(8,128)S(1)}, f32[3,16,5,384]{3,1,2,0:T(8,128)S(1)}, u32[]{:S(2)}, u32[]{:S(2)}) collective-permute-start(f32[3,16,5,384]{3,1,2,0:T(8,128)S(1)} %constant_dynamic-slice_fusion.3), channel_id=1, source_target_pairs={{0,128},{16,144},{32,160},{48,176},{64,192},{80,208},{96,224},{112... | collective-permute-start | bytes 1105928 | tf_op jit(solution)/shard_map/ppermute | solution.py:32
  128.9 2.6 %all_to_all.16 = bf16[2,3072,48]{1,2,0:T(8,128)(2,1)} reshape(bf16[2,16,192,48]{2,1,3,0:T(8,128)(2,1)} %copy.41) | data formatting | bytes 1179648 | tf_op jit(solution)/shard_map/all_to_all | solution.py:132
  136.0 9.3 %multiply_reduce_fusion = (f32[2,384]{1,0:T(2,128)S(1)}, f32[2,384,768]{2,1,0:T(8,128)S(1)}) fusion(f32[2,384,768]{2,1,0:T(8,128)S(1)} %copy-done.4, f32[2,384]{1,0:T(2,128)S(1)} %get-tuple-element.38, bf16[2,384,5,768]{3,1,0,2:T(8,128)(2,1)} %bitcast_dynamic-update-slice_fusion, bf16[5,768,768]{2,1,0:T(8,128)(2,1)} %param.6), kind=kOutput, calls=%fused_computation.13 | convolution fusion | flops 4536925184 | bytes 16521216 | tf_op jit(solution)/shard_map/blko,kio->bli/dot_general | solution.py:121
  145.5 3.4 %collective-permute-start.16 = (f32[3,16,5,96]{3,1,2,0:T(8,128)S(1)}, f32[3,16,5,96]{3,1,2,0:T(8,128)S(1)}, u32[]{:S(2)}, u32[]{:S(2)}) collective-permute-start(f32[3,16,5,96]{3,1,2,0:T(8,128)S(1)} %constant_dynamic-slice_fusion.1), channel_id=1, source_target_pairs={{0,2},{1,3},{2,0},{3,1},{4,6},{5,7},{6,4},{7,5},{8,10},{9,11},{10,... | collective-permute-start | bytes 276488 | tf_op jit(solution)/shard_map/ppermute | solution.py:32
  148.9 4.2 %collective-permute-done.16 = f32[3,16,5,96]{3,1,2,0:T(8,128)S(1)} collective-permute-done((f32[3,16,5,96]{3,1,2,0:T(8,128)S(1)}, f32[3,16,5,96]{3,1,2,0:T(8,128)S(1)}, u32[]{:S(2)}, u32[]{:S(2)}) %collective-permute-start.16) | collective-permute-done | bytes 92192 | tf_op jit(solution)/shard_map/ppermute | solution.py:32
  153.3 8.8 %collective-permute-start.17 = (f32[3,16,5,48]{3,1,2,0:T(8,128)S(1)}, f32[3,16,5,48]{3,1,2,0:T(8,128)S(1)}, u32[]{:S(2)}, u32[]{:S(2)}) collective-permute-start(f32[3,16,5,48]{3,1,2,0:T(8,128)S(1)} %constant_dynamic-slice_fusion), channel_id=1, source_target_pairs={{0,4},{1,5},{2,6},{3,7},{4,0},{5,1},{6,2},{7,3},{8,12},{9,13},{10,... | collective-permute-start | bytes 138248 | tf_op jit(solution)/shard_map/ppermute | solution.py:32
  (130 shorter events, 54.8 us)
Async XLA Ops:
  4.2 6.5 %collective-permute-start.1 = (bf16[2,2,768]{2,1,0:T(2,128)(2,1)S(1)}, bf16[2,2,768]{2,1,0:T(2,128)(2,1)S(1)}, u32[]{:S(2)}, u32[]{:S(2)}) collective-permute-start(bf16[2,2,768]{2,1,0:T(2,128)(2,1)S(1)} %get-tuple-element.36), channel_id=1, source_target_pairs={{16,0},{32,16},{48,32},{64,48},{80,64},{96,80},{112,96},{128,112},... | collective-permute-start | bytes 18440 | tf_op jit(solution)/shard_map/ppermute | solution.py:20
  5.6 5.1 %collective-permute-start = (bf16[2,2,768]{2,1,0:T(2,128)(2,1)S(1)}, bf16[2,2,768]{2,1,0:T(2,128)(2,1)S(1)}, u32[]{:S(2)}, u32[]{:S(2)}) collective-permute-start(bf16[2,2,768]{2,1,0:T(2,128)(2,1)S(1)} %get-tuple-element.35), channel_id=1, source_target_pairs={{0,16},{16,32},{32,48},{48,64},{64,80},{80,96},{96,112},{112,128},... | collective-permute-start | bytes 18440 | tf_op jit(solution)/shard_map/ppermute | solution.py:17
  10.6 16.4 %copy-start.13 = (bf16[2,384,768]{2,1,0:T(8,128)(2,1)}, bf16[2,384,768]{2,1,0:T(8,128)(2,1)S(1)}, u32[]{:S(2)}) copy-start(bf16[2,384,768]{2,1,0:T(8,128)(2,1)S(1)} %get-tuple-element.39) | copy-start | bytes 3538948
  15.8 15.8 %copy-start.5 = (bf16[2,384,768]{2,1,0:T(8,128)(2,1)S(1)}, bf16[2,384,768]{2,1,0:T(8,128)(2,1)}, u32[]{:S(2)}) copy-start(bf16[2,384,768]{2,1,0:T(8,128)(2,1)} %param.5) | copy-start | bytes 3538948
  24.4 13.4 %collective-permute-start.2 = (f32[384,5,768]{2,0,1:T(8,128)}, f32[384,5,768]{2,0,1:T(8,128)}, u32[]{:S(2)}, u32[]{:S(2)}) collective-permute-start(f32[384,5,768]{2,0,1:T(8,128)} %convolution_bitcast_fusion), channel_id=1, source_target_pairs={{0,16},{16,0},{32,48},{48,32},{64,80},{80,64},{96,112},{112,96},{1... | collective-permute-start | bytes 17694728 | tf_op jit(solution)/shard_map/ppermute | solution.py:111
  27.0 9.1 %collective-permute-start.4 = (bf16[2,2,768]{2,1,0:T(2,128)(2,1)S(1)}, bf16[2,2,768]{2,1,0:T(2,128)(2,1)S(1)}, u32[]{:S(2)}, u32[]{:S(2)}) collective-permute-start(bf16[2,2,768]{2,1,0:T(2,128)(2,1)S(1)} %get-tuple-element.34), channel_id=1, source_target_pairs={{16,0},{32,16},{48,32},{64,48},{80,64},{96,80},{112,96},{128,112},... | collective-permute-start | bytes 18440 | tf_op jit(solution)/shard_map/ppermute | solution.py:20
  28.3 7.9 %collective-permute-start.3 = (bf16[2,2,768]{2,1,0:T(2,128)(2,1)S(1)}, bf16[2,2,768]{2,1,0:T(2,128)(2,1)S(1)}, u32[]{:S(2)}, u32[]{:S(2)}) collective-permute-start(bf16[2,2,768]{2,1,0:T(2,128)(2,1)S(1)} %get-tuple-element.33), channel_id=1, source_target_pairs={{0,16},{16,32},{32,48},{48,64},{64,80},{80,96},{96,112},{112,128},... | collective-permute-start | bytes 18440 | tf_op jit(solution)/shard_map/ppermute | solution.py:17
  48.4 16.4 %slice-start = ((s8[5898240]{0:T(1024)(128)(4,1)}), s8[4194304]{0:T(1024)(128)(4,1)S(1)}, s32[]{:S(2)}) async-start(s8[5898240]{0:T(1024)(128)(4,1)} %bitcast.138), calls=%async_computation.1 | async-start | bytes 8388608
  53.1 40.3 %collective-permute-start.11 = (f32[128,5,384]{2,0,1:T(8,128)}, f32[128,5,384]{2,0,1:T(8,128)}, u32[]{:S(2)}, u32[]{:S(2)}) collective-permute-start(f32[128,5,384]{2,0,1:T(8,128)} %dynamic-slice_bitcast_fusion), channel_id=1, source_target_pairs={{0,1},{1,0},{2,3},{3,2},{4,5},{5,4},{6,7},{7,6},{8,9},{9,8},{10,11... | collective-permute-start | bytes 2949128 | tf_op jit(solution)/shard_map/ppermute | solution.py:32
  55.0 9.8 %slice-start.1 = ((s8[5898240]{0:T(1024)(128)(4,1)}), s8[1703936]{0:T(1024)(128)(4,1)S(1)}, s32[]{:S(2)}) async-start(s8[5898240]{0:T(1024)(128)(4,1)} %bitcast.138), calls=%async_computation.2 | async-start | bytes 3407872
  56.0 45.8 %collective-permute-start.8 = (f32[64,5,768]{2,0,1:T(8,128)}, f32[64,5,768]{2,0,1:T(8,128)}, u32[]{:S(2)}, u32[]{:S(2)}) collective-permute-start(f32[64,5,768]{2,0,1:T(8,128)} %dynamic-slice_bitcast_fusion.1), channel_id=1, source_target_pairs={{0,32},{16,48},{32,0},{48,16},{64,96},{80,112},{96,64},{112,80},{1... | collective-permute-start | bytes 2949128 | tf_op jit(solution)/shard_map/ppermute | solution.py:32
  60.1 37.3 %collective-permute-start.5 = (f32[64,5,768]{2,0,1:T(8,128)}, f32[64,5,768]{2,0,1:T(8,128)}, u32[]{:S(2)}, u32[]{:S(2)}) collective-permute-start(f32[64,5,768]{2,0,1:T(8,128)} %dynamic-slice_bitcast_fusion.2), channel_id=1, source_target_pairs={{0,64},{16,80},{32,96},{48,112},{64,0},{80,16},{96,32},{112,48},{1... | collective-permute-start | bytes 2949128 | tf_op jit(solution)/shard_map/ppermute | solution.py:32
  82.4 45.2 %all-to-all-start = ((bf16[2,192,768]{1,0,2:T(2,128)(2,1)}), bf16[2,192,768]{1,0,2:T(2,128)(2,1)S(1)}, u32[]{:S(2)}, u32[]{:S(2)}) async-start(bf16[2,192,768]{1,0,2:T(2,128)(2,1)} %copy.39), calls=%async_computation | async-start | bytes 1572864 | tf_op jit(solution)/shard_map/all_to_all | solution.py:132
  95.4 15.0 %collective-permute-start.12 = (f32[64,5,384]{2,0,1:T(8,128)S(1)}, f32[64,5,384]{2,0,1:T(8,128)S(1)}, u32[]{:S(2)}, u32[]{:S(2)}) collective-permute-start(f32[64,5,384]{2,0,1:T(8,128)S(1)} %constant_dynamic-slice_fusion.5), channel_id=1, source_target_pairs={{0,64},{16,80},{32,96},{48,112},{64,0},{80,16},{96,32},{112,48},{1... | collective-permute-start | bytes 1474568 | tf_op jit(solution)/shard_map/ppermute | solution.py:32
  98.8 14.7 %collective-permute-start.6 = (f32[32,5,768]{2,0,1:T(8,128)S(1)}, f32[32,5,768]{2,0,1:T(8,128)S(1)}, u32[]{:S(2)}, u32[]{:S(2)}) collective-permute-start(f32[32,5,768]{2,0,1:T(8,128)S(1)} %constant_dynamic-slice_fusion.9), channel_id=1, source_target_pairs={{0,32},{16,48},{32,0},{48,16},{64,96},{80,112},{96,64},{112,80},{1... | collective-permute-start | bytes 1474568 | tf_op jit(solution)/shard_map/ppermute | solution.py:32
  103.2 13.1 %collective-permute-start.9 = (f32[64,5,384]{2,0,1:T(8,128)S(1)}, f32[64,5,384]{2,0,1:T(8,128)S(1)}, u32[]{:S(2)}, u32[]{:S(2)}) collective-permute-start(f32[64,5,384]{2,0,1:T(8,128)S(1)} %constant_dynamic-slice_fusion.7), channel_id=1, source_target_pairs={{0,1},{1,0},{2,3},{3,2},{4,5},{5,4},{6,7},{7,6},{8,9},{9,8},{10,11... | collective-permute-start | bytes 1474568 | tf_op jit(solution)/shard_map/ppermute | solution.py:32
  110.5 9.8 %collective-permute-start.13 = (f32[32,5,384]{2,0,1:T(8,128)S(1)}, f32[32,5,384]{2,0,1:T(8,128)S(1)}, u32[]{:S(2)}, u32[]{:S(2)}) collective-permute-start(f32[32,5,384]{2,0,1:T(8,128)S(1)} %constant_dynamic-slice_fusion.4), channel_id=1, source_target_pairs={{0,32},{16,48},{32,0},{48,16},{64,96},{80,112},{96,64},{112,80},{1... | collective-permute-start | bytes 737288 | tf_op jit(solution)/shard_map/ppermute | solution.py:32
  113.5 7.7 %collective-permute-start.7 = (f32[32,5,384]{2,0,1:T(8,128)S(1)}, f32[32,5,384]{2,0,1:T(8,128)S(1)}, u32[]{:S(2)}, u32[]{:S(2)}) collective-permute-start(f32[32,5,384]{2,0,1:T(8,128)S(1)} %constant_dynamic-slice_fusion.8), channel_id=1, source_target_pairs={{0,1},{1,0},{2,3},{3,2},{4,5},{5,4},{6,7},{7,6},{8,9},{9,8},{10,11... | collective-permute-start | bytes 737288 | tf_op jit(solution)/shard_map/ppermute | solution.py:32
  116.4 6.3 %collective-permute-start.10 = (f32[32,5,384]{2,0,1:T(8,128)S(1)}, f32[32,5,384]{2,0,1:T(8,128)S(1)}, u32[]{:S(2)}, u32[]{:S(2)}) collective-permute-start(f32[32,5,384]{2,0,1:T(8,128)S(1)} %constant_dynamic-slice_fusion.6), channel_id=1, source_target_pairs={{0,64},{16,80},{32,96},{48,112},{64,0},{80,16},{96,32},{112,48},{1... | collective-permute-start | bytes 737288 | tf_op jit(solution)/shard_map/ppermute | solution.py:32
  123.7 9.6 %collective-permute-start.14 = (f32[3,16,5,384]{3,1,2,0:T(8,128)S(1)}, f32[3,16,5,384]{3,1,2,0:T(8,128)S(1)}, u32[]{:S(2)}, u32[]{:S(2)}) collective-permute-start(f32[3,16,5,384]{3,1,2,0:T(8,128)S(1)} %constant_dynamic-slice_fusion.3), channel_id=1, source_target_pairs={{0,128},{16,144},{32,160},{48,176},{64,192},{80,208},{96,224},{112... | collective-permute-start | bytes 1105928 | tf_op jit(solution)/shard_map/ppermute | solution.py:32
  134.5 10.8 %collective-permute-start.15 = (f32[3,16,5,192]{3,1,2,0:T(8,128)S(1)}, f32[3,16,5,192]{3,1,2,0:T(8,128)S(1)}, u32[]{:S(2)}, u32[]{:S(2)}) collective-permute-start(f32[3,16,5,192]{3,1,2,0:T(8,128)S(1)} %constant_dynamic-slice_fusion.2), channel_id=1, source_target_pairs={{0,8},{1,9},{2,10},{3,11},{4,12},{5,13},{6,14},{7,15},{8,0},{9,1},... | collective-permute-start | bytes 552968 | tf_op jit(solution)/shard_map/ppermute | solution.py:32
  136.0 26.1 %copy-start.6 = (f32[2,384,768]{2,1,0:T(8,128)S(1)}, f32[2,384,768]{2,1,0:T(8,128)}, u32[]{:S(2)}) copy-start(f32[2,384,768]{2,1,0:T(8,128)} %get-tuple-element.14) | copy-start | bytes 7077892
  145.5 7.5 %collective-permute-start.16 = (f32[3,16,5,96]{3,1,2,0:T(8,128)S(1)}, f32[3,16,5,96]{3,1,2,0:T(8,128)S(1)}, u32[]{:S(2)}, u32[]{:S(2)}) collective-permute-start(f32[3,16,5,96]{3,1,2,0:T(8,128)S(1)} %constant_dynamic-slice_fusion.1), channel_id=1, source_target_pairs={{0,2},{1,3},{2,0},{3,1},{4,6},{5,7},{6,4},{7,5},{8,10},{9,11},{10,... | collective-permute-start | bytes 276488 | tf_op jit(solution)/shard_map/ppermute | solution.py:32
  153.3 11.6 %collective-permute-start.17 = (f32[3,16,5,48]{3,1,2,0:T(8,128)S(1)}, f32[3,16,5,48]{3,1,2,0:T(8,128)S(1)}, u32[]{:S(2)}, u32[]{:S(2)}) collective-permute-start(f32[3,16,5,48]{3,1,2,0:T(8,128)S(1)} %constant_dynamic-slice_fusion), channel_id=1, source_target_pairs={{0,4},{1,5},{2,6},{3,7},{4,0},{5,1},{6,2},{7,3},{8,12},{9,13},{10,... | collective-permute-start | bytes 138248 | tf_op jit(solution)/shard_map/ppermute | solution.py:32
  (16 other events, 85.9 us)

commit v6 on v0

--- a/solution.py
+++ b/solution.py
@@ -134,9 +134,11 @@
     for step in range(1, len(CHAINS[0])):
         if step in shared:
             if isinstance(partial, list):
-                partial, trunk_input = lax.optimization_barrier((jnp.stack(partial), trunk_input))
+                partial = jnp.stack(partial)
             axis, bit = CHAINS[0][step]
             partial = halved(partial, axis, bit, 1 if axis == "seq" else 3)
+            if step == shared[2]:
+                partial, trunk_input = lax.optimization_barrier((partial, trunk_input))
         else:
             partial = [
                 halved(partial[piece], axis, bit, 0 if axis == "seq" else 2)

time: 170 us -> 164 us (0.965)
  waiting for transfers between devices: 41.9 us -> 29.7 us
  starting transfers between devices: 45.9 us -> 48.9 us
  other arithmetic: 15.5 us -> 17.3 us
    all_to_all x1, waiting for transfers between devices: 11.3 us -> 0.01 us  [shards(): lax.all_to_all(pooled, 'seq', split_axis=2, concat_axis=1, tiled=True)]
    ppermute x13, starting transfers between devices: 28.9 us -> 31.8 us  [halved(): return keep + lax.ppermute(send, axis, partners)]
    convert_element_type x1, other arithmetic: 1.53 us -> 3.97 us  [shards(): (upward + inverse * slope_grad - floats * inverse ** 3 * centred).astype(...]
    all_to_all x3, local copies, waits for them, and re-layouts: 2 us -> 3.79 us  [shards(): lax.all_to_all(pooled, 'seq', split_axis=2, concat_axis=1, tiled=True)]
    unnamed x61 -> x55, local copies, waits for them, and re-layouts: 10.2 us -> 8.9 us
  transfers between devices with their start and end apart: 19 -> 19, of which waited for: 12 -> 8; matrix products, arithmetic and copies ran while one was open for 24% -> 27% of each run, Pallas kernels for 0% -> 0%
where the time goes in v6:
time: 164 us; the launch traced here: 163 us
  starting transfers between devices  48.9 us (30%)
  matrix products  35.3 us (22%)
  local copies, waits for them, and re-layouts  30.9 us (19%)
  waiting for transfers between devices  29.7 us (18%)
  other arithmetic  17.3 us (11%)
    ppermute x13, starting transfers between devices, halved(): return keep + lax.ppermute(send, axis, partners)  31.8 us
    ppermute x13, waiting for transfers between devices, halved(): return keep + lax.ppermute(send, axis, partners)  28.1 us
    dot_general x2, matrix products, shards(): jnp.einsum('blo,blki->oki', picked(branch_grad, chosen), act_window, pref...  19.2 us
    unnamed x55, local copies, waits for them, and re-layouts  8.9 us
    dot_general x1, matrix products, shards(): jnp.einsum('blko,kio->bli', grad_window, weight, preferred_element_type=j...  6.68 us
    ppermute x2, starting transfers between devices, with_halo(): lax.ppermute(lax.slice_in_dim(block, block.shape[dim] - width, None, axis...  6.24 us
    dot_general x1, matrix products, shards(): jnp.einsum('blki,kio->blo', window, weight, preferred_element_type=jnp.fl...  6.18 us
    all_to_all x1, starting transfers between devices, shards(): lax.all_to_all(pooled, 'seq', split_axis=2, concat_axis=1, tiled=True)  5.57 us
  transfers between devices with their start and end apart: 19, of which 8 were waited for; matrix products, arithmetic and copies ran while one was open for 27% of the time, Pallas kernels for 0%

profile of v6, /device:TPU:2, one launch (start us, length us, event | category | flops | bytes accessed | tf_op | source)
XLA Modules:
  0.0 163.3 jit_solution(15712940764969882224)
XLA Ops:
  5.6 3.0 %collective-permute-start = (bf16[2,2,768]{2,1,0:T(2,128)(2,1)S(1)}, bf16[2,2,768]{2,1,0:T(2,128)(2,1)S(1)}, u32[]{:S(2)}, u32[]{:S(2)}) collective-permute-start(bf16[2,2,768]{2,1,0:T(2,128)(2,1)S(1)} %get-tuple-element.35), channel_id=1, source_target_pairs={{0,16},{16,32},{32,48},{48,64},{64,80},{80,96},{96,112},{112,128},... | collective-permute-start | bytes 18440 | tf_op jit(solution)/shard_map/ppermute | solution.py:17
  15.8 8.6 %convolution_bitcast_fusion = f32[384,5,768]{2,0,1:T(8,128)} fusion(bf16[2,384,5,768]{3,1,0,2:T(8,128)(2,1)} %copy-done.14, bf16[2,384,768]{2,1,0:T(8,128)(2,1)S(1)} %get-tuple-element.39, s32[384]{0:T(512)S(1)} %bitcast.137), kind=kOutput, calls=%fused_computation.6 | convolution fusion | flops 2718498816 | bytes 12977664 | tf_op jit(solution)/shard_map/blo,blki->oki/dot_general | solution.py:106
  24.4 2.6 %collective-permute-start.2 = (f32[384,5,768]{2,0,1:T(8,128)}, f32[384,5,768]{2,0,1:T(8,128)}, u32[]{:S(2)}, u32[]{:S(2)}) collective-permute-start(f32[384,5,768]{2,0,1:T(8,128)} %convolution_bitcast_fusion), channel_id=1, source_target_pairs={{0,16},{16,0},{32,48},{48,32},{64,80},{80,64},{96,112},{112,96},{1... | collective-permute-start | bytes 17694728 | tf_op jit(solution)/shard_map/ppermute | solution.py:111
  28.3 3.2 %collective-permute-start.3 = (bf16[2,2,768]{2,1,0:T(2,128)(2,1)S(1)}, bf16[2,2,768]{2,1,0:T(2,128)(2,1)S(1)}, u32[]{:S(2)}, u32[]{:S(2)}) collective-permute-start(bf16[2,2,768]{2,1,0:T(2,128)(2,1)S(1)} %get-tuple-element.33), channel_id=1, source_target_pairs={{0,16},{16,32},{32,48},{48,64},{64,80},{80,96},{96,112},{112,128},... | collective-permute-start | bytes 18440 | tf_op jit(solution)/shard_map/ppermute | solution.py:17
  37.8 10.6 %bitcast_add_fusion = f32[384,5,768]{2,0,1:T(8,128)} fusion(f32[384,5,768]{2,0,1:T(8,128)} %collective-permute-done.2, bf16[2,384,5,768]{3,1,0,2:T(8,128)(2,1)} %copy-done.14, bf16[2,384,768]{2,1,0:T(8,128)(2,1)} %copy-done.12, s32[384]{0:T(512)S(1)} %bitcast.136), kind=kOutput, calls=%fused_computation.4 | convolution fusion | flops 2719973376 | bytes 18875904 | tf_op jit(solution)/shard_map/blo,blki->oki/dot_general | solution.py:106
  48.4 3.5 %fusion.51 = (f32[1,128,5,768]{3,1,2,0:T(8,128)S(1)}, f32[1,128,5,768]{3,1,2,0:T(8,128)S(1)}, f32[1,128,5,768]{3,1,2,0:T(8,128)S(1)}) fusion(f32[3,128,5,768]{3,1,0,2:T(8,128)} %bitcast.133), kind=kLoop, calls=%fused_computation.106 | loop fusion | bytes 11796480 | tf_op jit(solution)/shard_map/slice | solution.py:144
  56.0 3.0 %collective-permute-start.8 = (f32[64,5,768]{2,0,1:T(8,128)}, f32[64,5,768]{2,0,1:T(8,128)}, u32[]{:S(2)}, u32[]{:S(2)}) collective-permute-start(f32[64,5,768]{2,0,1:T(8,128)} %dynamic-slice_bitcast_fusion.1), channel_id=1, source_target_pairs={{0,32},{16,48},{32,0},{48,16},{64,96},{80,112},{96,64},{112,80},{1... | collective-permute-start | bytes 2949128 | tf_op jit(solution)/shard_map/ppermute | solution.py:32
  60.1 3.4 %collective-permute-start.5 = (f32[64,5,768]{2,0,1:T(8,128)}, f32[64,5,768]{2,0,1:T(8,128)}, u32[]{:S(2)}, u32[]{:S(2)}) collective-permute-start(f32[64,5,768]{2,0,1:T(8,128)} %dynamic-slice_bitcast_fusion.2), channel_id=1, source_target_pairs={{0,64},{16,80},{32,96},{48,112},{64,0},{80,16},{96,32},{112,48},{1... | collective-permute-start | bytes 2949128 | tf_op jit(solution)/shard_map/ppermute | solution.py:32
  65.9 6.2 %bitcast_add_fusion.1 = f32[2,384,768]{2,1,0:T(8,128)} fusion(f32[2,384,768]{2,1,0:T(8,128)S(1)} %copy-done.2, bf16[2,384,5,768]{3,1,0,2:T(8,128)(2,1)S(1)} %bitcast_dynamic-update-slice_fusion.5, bf16[5,768,768]{2,1,0:T(8,128)(2,1)S(1)} %bitcast.139), kind=kOutput, calls=%fused_computation.11 | convolution fusion | flops 4530438144 | bytes 16515072 | tf_op jit(solution)/shard_map/blki,kio->blo/dot_general | solution.py:128
  72.1 4.0 %reshape.61 = f32[2,192,2,768]{3,2,1,0:T(2,128)} reshape(f32[2,384,768]{2,1,0:T(8,128)} %bitcast_add_fusion.1) | data formatting | bytes 4718592 | tf_op jit(solution)/shard_map/reshape | solution.py:130
  76.0 4.4 %fusion.52 = (f32[2,192,1,768]{3,2,1,0:T(1,128)S(1)}, f32[2,192,1,768]{3,2,1,0:T(1,128)S(1)}) fusion(f32[2,192,2,768]{3,2,1,0:T(2,128)} %reshape.61), kind=kLoop, calls=%fused_computation.107 | loop fusion | bytes 4718592 | tf_op jit(solution)/shard_map/slice | solution.py:131
  82.4 5.6 %all-to-all-start = ((bf16[2,192,768]{1,0,2:T(2,128)(2,1)}), bf16[2,192,768]{1,0,2:T(2,128)(2,1)S(1)}, u32[]{:S(2)}, u32[]{:S(2)}) async-start(bf16[2,192,768]{1,0,2:T(2,128)(2,1)} %copy.39), calls=%async_computation | async-start | bytes 1572864 | tf_op jit(solution)/shard_map/all_to_all | solution.py:132
  95.8 3.1 %collective-permute-start.6 = (f32[32,5,768]{2,0,1:T(8,128)S(1)}, f32[32,5,768]{2,0,1:T(8,128)S(1)}, u32[]{:S(2)}, u32[]{:S(2)}) collective-permute-start(f32[32,5,768]{2,0,1:T(8,128)S(1)} %constant_dynamic-slice_fusion.9), channel_id=1, source_target_pairs={{0,32},{16,48},{32,0},{48,16},{64,96},{80,112},{96,64},{112,80},{1... | collective-permute-start | bytes 1474568 | tf_op jit(solution)/shard_map/ppermute | solution.py:32
  100.4 9.7 %collective-permute-done.12 = f32[64,5,384]{2,0,1:T(8,128)S(1)} collective-permute-done((f32[64,5,384]{2,0,1:T(8,128)S(1)}, f32[64,5,384]{2,0,1:T(8,128)S(1)}, u32[]{:S(2)}, u32[]{:S(2)}) %collective-permute-start.12) | collective-permute-done | bytes 491552 | tf_op jit(solution)/shard_map/ppermute | solution.py:32
  110.2 3.3 %collective-permute-start.13 = (f32[32,5,384]{2,0,1:T(8,128)S(1)}, f32[32,5,384]{2,0,1:T(8,128)S(1)}, u32[]{:S(2)}, u32[]{:S(2)}) collective-permute-start(f32[32,5,384]{2,0,1:T(8,128)S(1)} %constant_dynamic-slice_fusion.4), channel_id=1, source_target_pairs={{0,32},{16,48},{32,0},{48,16},{64,96},{80,112},{96,64},{112,80},{1... | collective-permute-start | bytes 737288 | tf_op jit(solution)/shard_map/ppermute | solution.py:32
  114.3 5.2 %collective-permute-done.13 = f32[32,5,384]{2,0,1:T(8,128)S(1)} collective-permute-done((f32[32,5,384]{2,0,1:T(8,128)S(1)}, f32[32,5,384]{2,0,1:T(8,128)S(1)}, u32[]{:S(2)}, u32[]{:S(2)}) %collective-permute-start.13) | collective-permute-done | bytes 245792 | tf_op jit(solution)/shard_map/ppermute | solution.py:32
  121.2 2.8 %collective-permute-start.14 = (f32[3,16,5,384]{3,1,2,0:T(8,128)S(1)}, f32[3,16,5,384]{3,1,2,0:T(8,128)S(1)}, u32[]{:S(2)}, u32[]{:S(2)}) collective-permute-start(f32[3,16,5,384]{3,1,2,0:T(8,128)S(1)} %constant_dynamic-slice_fusion.3), channel_id=1, source_target_pairs={{0,128},{16,144},{32,160},{48,176},{64,192},{80,208},{96,224},{112... | collective-permute-start | bytes 1105928 | tf_op jit(solution)/shard_map/ppermute | solution.py:32
  124.1 7.6 %collective-permute-done.14 = f32[3,16,5,384]{3,1,2,0:T(8,128)S(1)} collective-permute-done((f32[3,16,5,384]{3,1,2,0:T(8,128)S(1)}, f32[3,16,5,384]{3,1,2,0:T(8,128)S(1)}, u32[]{:S(2)}, u32[]{:S(2)}) %collective-permute-start.14) | collective-permute-done | bytes 368672 | tf_op jit(solution)/shard_map/ppermute | solution.py:32
  133.4 6.7 %multiply_reduce_fusion = (f32[2,384]{1,0:T(2,128)S(1)}, f32[2,384,768]{2,1,0:T(8,128)}) fusion(f32[2,384,768]{2,1,0:T(8,128)S(1)} %copy-done.3, f32[2,384]{1,0:T(2,128)S(1)} %get-tuple-element.38, bf16[2,384,5,768]{3,1,0,2:T(8,128)(2,1)S(1)} %bitcast_dynamic-update-slice_fusion, bf16[5,768,768]{2,1,0:T(8,128)(2,1)S(1)} %bitcast.141), kind=kOutput, calls=%fused_computation.13 | convolution fusion | flops 4536925184 | bytes 16521216 | tf_op jit(solution)/shard_map/blko,kio->bli/dot_general | solution.py:121
  141.4 2.6 %all_to_all.16 = bf16[2,3072,48]{1,2,0:T(8,128)(2,1)} reshape(bf16[2,16,192,48]{2,1,3,0:T(8,128)(2,1)} %copy.41) | data formatting | bytes 1179648 | tf_op jit(solution)/shard_map/all_to_all | solution.py:132
  144.2 3.4 %collective-permute-start.16 = (f32[3,16,5,96]{3,1,2,0:T(8,128)S(1)}, f32[3,16,5,96]{3,1,2,0:T(8,128)S(1)}, u32[]{:S(2)}, u32[]{:S(2)}) collective-permute-start(f32[3,16,5,96]{3,1,2,0:T(8,128)S(1)} %constant_dynamic-slice_fusion.1), channel_id=1, source_target_pairs={{0,2},{1,3},{2,0},{3,1},{4,6},{5,7},{6,4},{7,5},{8,10},{9,11},{10,... | collective-permute-start | bytes 276488 | tf_op jit(solution)/shard_map/ppermute | solution.py:32
  147.5 4.2 %collective-permute-done.16 = f32[3,16,5,96]{3,1,2,0:T(8,128)S(1)} collective-permute-done((f32[3,16,5,96]{3,1,2,0:T(8,128)S(1)}, f32[3,16,5,96]{3,1,2,0:T(8,128)S(1)}, u32[]{:S(2)}, u32[]{:S(2)}) %collective-permute-start.16) | collective-permute-done | bytes 92192 | tf_op jit(solution)/shard_map/ppermute | solution.py:32
  151.9 6.5 %collective-permute-start.17 = (f32[3,16,5,48]{3,1,2,0:T(8,128)S(1)}, f32[3,16,5,48]{3,1,2,0:T(8,128)S(1)}, u32[]{:S(2)}, u32[]{:S(2)}) collective-permute-start(f32[3,16,5,48]{3,1,2,0:T(8,128)S(1)} %constant_dynamic-slice_fusion), channel_id=1, source_target_pairs={{0,4},{1,5},{2,6},{3,7},{4,0},{5,1},{6,2},{7,3},{8,12},{9,13},{10,... | collective-permute-start | bytes 138248 | tf_op jit(solution)/shard_map/ppermute | solution.py:32
  158.4 4.0 %subtract_convert_fusion = bf16[2,384,768]{2,1,0:T(8,128)(2,1)} fusion(f32[2,384,768]{2,1,0:T(8,128)S(1)} %copy-done.4, f32[2,384,768]{2,1,0:T(8,128)} %get-tuple-element.14, f32[2,384,768]{2,1,0:T(8,128)} %get-tuple-element.42, f32[2,384]{1,0:T(2,128)S(1)} %broadcast_multiply_fusion, f32[2,384]{1,0:T(2,128)S(1)} %get-tuple-element.37, ...), kind=kLoop, calls=%fused_computation.12 | loop fusion | flops 3538944 | bytes 8266752 | tf_op jit(solution)/shard_map/convert_element_type | solution.py:124
  (131 shorter events, 45.1 us)
Async XLA Ops:
  4.2 6.5 %collective-permute-start.1 = (bf16[2,2,768]{2,1,0:T(2,128)(2,1)S(1)}, bf16[2,2,768]{2,1,0:T(2,128)(2,1)S(1)}, u32[]{:S(2)}, u32[]{:S(2)}) collective-permute-start(bf16[2,2,768]{2,1,0:T(2,128)(2,1)S(1)} %get-tuple-element.36), channel_id=1, source_target_pairs={{16,0},{32,16},{48,32},{64,48},{80,64},{96,80},{112,96},{128,112},... | collective-permute-start | bytes 18440 | tf_op jit(solution)/shard_map/ppermute | solution.py:20
  5.6 5.0 %collective-permute-start = (bf16[2,2,768]{2,1,0:T(2,128)(2,1)S(1)}, bf16[2,2,768]{2,1,0:T(2,128)(2,1)S(1)}, u32[]{:S(2)}, u32[]{:S(2)}) collective-permute-start(bf16[2,2,768]{2,1,0:T(2,128)(2,1)S(1)} %get-tuple-element.35), channel_id=1, source_target_pairs={{0,16},{16,32},{32,48},{48,64},{64,80},{80,96},{96,112},{112,128},... | collective-permute-start | bytes 18440 | tf_op jit(solution)/shard_map/ppermute | solution.py:17
  10.6 16.4 %copy-start.12 = (bf16[2,384,768]{2,1,0:T(8,128)(2,1)}, bf16[2,384,768]{2,1,0:T(8,128)(2,1)S(1)}, u32[]{:S(2)}) copy-start(bf16[2,384,768]{2,1,0:T(8,128)(2,1)S(1)} %get-tuple-element.39) | copy-start | bytes 3538948
  15.8 15.8 %copy-start.5 = (bf16[2,384,768]{2,1,0:T(8,128)(2,1)S(1)}, bf16[2,384,768]{2,1,0:T(8,128)(2,1)}, u32[]{:S(2)}) copy-start(bf16[2,384,768]{2,1,0:T(8,128)(2,1)} %param.5) | copy-start | bytes 3538948
  24.4 13.4 %collective-permute-start.2 = (f32[384,5,768]{2,0,1:T(8,128)}, f32[384,5,768]{2,0,1:T(8,128)}, u32[]{:S(2)}, u32[]{:S(2)}) collective-permute-start(f32[384,5,768]{2,0,1:T(8,128)} %convolution_bitcast_fusion), channel_id=1, source_target_pairs={{0,16},{16,0},{32,48},{48,32},{64,80},{80,64},{96,112},{112,96},{1... | collective-permute-start | bytes 17694728 | tf_op jit(solution)/shard_map/ppermute | solution.py:111
  27.0 9.1 %collective-permute-start.4 = (bf16[2,2,768]{2,1,0:T(2,128)(2,1)S(1)}, bf16[2,2,768]{2,1,0:T(2,128)(2,1)S(1)}, u32[]{:S(2)}, u32[]{:S(2)}) collective-permute-start(bf16[2,2,768]{2,1,0:T(2,128)(2,1)S(1)} %get-tuple-element.34), channel_id=1, source_target_pairs={{16,0},{32,16},{48,32},{64,48},{80,64},{96,80},{112,96},{128,112},... | collective-permute-start | bytes 18440 | tf_op jit(solution)/shard_map/ppermute | solution.py:20
  28.3 7.9 %collective-permute-start.3 = (bf16[2,2,768]{2,1,0:T(2,128)(2,1)S(1)}, bf16[2,2,768]{2,1,0:T(2,128)(2,1)S(1)}, u32[]{:S(2)}, u32[]{:S(2)}) collective-permute-start(bf16[2,2,768]{2,1,0:T(2,128)(2,1)S(1)} %get-tuple-element.33), channel_id=1, source_target_pairs={{0,16},{16,32},{32,48},{48,64},{64,80},{80,96},{96,112},{112,128},... | collective-permute-start | bytes 18440 | tf_op jit(solution)/shard_map/ppermute | solution.py:17
  48.4 16.4 %slice-start = ((s8[5898240]{0:T(1024)(128)(4,1)}), s8[4194304]{0:T(1024)(128)(4,1)S(1)}, s32[]{:S(2)}) async-start(s8[5898240]{0:T(1024)(128)(4,1)} %bitcast.138), calls=%async_computation.1 | async-start | bytes 8388608
  53.0 37.4 %collective-permute-start.11 = (f32[128,5,384]{2,0,1:T(8,128)}, f32[128,5,384]{2,0,1:T(8,128)}, u32[]{:S(2)}, u32[]{:S(2)}) collective-permute-start(f32[128,5,384]{2,0,1:T(8,128)} %dynamic-slice_bitcast_fusion), channel_id=1, source_target_pairs={{0,1},{1,0},{2,3},{3,2},{4,5},{5,4},{6,7},{7,6},{8,9},{9,8},{10,11... | collective-permute-start | bytes 2949128 | tf_op jit(solution)/shard_map/ppermute | solution.py:32
  56.0 42.8 %collective-permute-start.8 = (f32[64,5,768]{2,0,1:T(8,128)}, f32[64,5,768]{2,0,1:T(8,128)}, u32[]{:S(2)}, u32[]{:S(2)}) collective-permute-start(f32[64,5,768]{2,0,1:T(8,128)} %dynamic-slice_bitcast_fusion.1), channel_id=1, source_target_pairs={{0,32},{16,48},{32,0},{48,16},{64,96},{80,112},{96,64},{112,80},{1... | collective-permute-start | bytes 2949128 | tf_op jit(solution)/shard_map/ppermute | solution.py:32
  60.1 34.3 %collective-permute-start.5 = (f32[64,5,768]{2,0,1:T(8,128)}, f32[64,5,768]{2,0,1:T(8,128)}, u32[]{:S(2)}, u32[]{:S(2)}) collective-permute-start(f32[64,5,768]{2,0,1:T(8,128)} %dynamic-slice_bitcast_fusion.2), channel_id=1, source_target_pairs={{0,64},{16,80},{32,96},{48,112},{64,0},{80,16},{96,32},{112,48},{1... | collective-permute-start | bytes 2949128 | tf_op jit(solution)/shard_map/ppermute | solution.py:32
  82.4 57.7 %all-to-all-start = ((bf16[2,192,768]{1,0,2:T(2,128)(2,1)}), bf16[2,192,768]{1,0,2:T(2,128)(2,1)S(1)}, u32[]{:S(2)}, u32[]{:S(2)}) async-start(bf16[2,192,768]{1,0,2:T(2,128)(2,1)} %copy.39), calls=%async_computation | async-start | bytes 1572864 | tf_op jit(solution)/shard_map/all_to_all | solution.py:132
  92.4 17.7 %collective-permute-start.12 = (f32[64,5,384]{2,0,1:T(8,128)S(1)}, f32[64,5,384]{2,0,1:T(8,128)S(1)}, u32[]{:S(2)}, u32[]{:S(2)}) collective-permute-start(f32[64,5,384]{2,0,1:T(8,128)S(1)} %constant_dynamic-slice_fusion.5), channel_id=1, source_target_pairs={{0,64},{16,80},{32,96},{48,112},{64,0},{80,16},{96,32},{112,48},{1... | collective-permute-start | bytes 1474568 | tf_op jit(solution)/shard_map/ppermute | solution.py:32
  95.8 17.7 %collective-permute-start.6 = (f32[32,5,768]{2,0,1:T(8,128)S(1)}, f32[32,5,768]{2,0,1:T(8,128)S(1)}, u32[]{:S(2)}, u32[]{:S(2)}) collective-permute-start(f32[32,5,768]{2,0,1:T(8,128)S(1)} %constant_dynamic-slice_fusion.9), channel_id=1, source_target_pairs={{0,32},{16,48},{32,0},{48,16},{64,96},{80,112},{96,64},{112,80},{1... | collective-permute-start | bytes 1474568 | tf_op jit(solution)/shard_map/ppermute | solution.py:32
  100.2 33.3 %slice-start.2 = ((s8[5898240]{0:T(1024)(128)(4,1)}), s8[4194304]{0:T(1024)(128)(4,1)S(1)}, s32[]{:S(2)}) async-start(s8[5898240]{0:T(1024)(128)(4,1)} %bitcast.140), calls=%async_computation.3 | async-start | bytes 8388608
  100.2 13.5 %collective-permute-start.9 = (f32[64,5,384]{2,0,1:T(8,128)S(1)}, f32[64,5,384]{2,0,1:T(8,128)S(1)}, u32[]{:S(2)}, u32[]{:S(2)}) collective-permute-start(f32[64,5,384]{2,0,1:T(8,128)S(1)} %constant_dynamic-slice_fusion.7), channel_id=1, source_target_pairs={{0,1},{1,0},{2,3},{3,2},{4,5},{5,4},{6,7},{7,6},{8,9},{9,8},{10,11... | collective-permute-start | bytes 1474568 | tf_op jit(solution)/shard_map/ppermute | solution.py:32
  110.2 9.3 %collective-permute-start.13 = (f32[32,5,384]{2,0,1:T(8,128)S(1)}, f32[32,5,384]{2,0,1:T(8,128)S(1)}, u32[]{:S(2)}, u32[]{:S(2)}) collective-permute-start(f32[32,5,384]{2,0,1:T(8,128)S(1)} %constant_dynamic-slice_fusion.4), channel_id=1, source_target_pairs={{0,32},{16,48},{32,0},{48,16},{64,96},{80,112},{96,64},{112,80},{1... | collective-permute-start | bytes 737288 | tf_op jit(solution)/shard_map/ppermute | solution.py:32
  113.6 7.3 %collective-permute-start.7 = (f32[32,5,384]{2,0,1:T(8,128)S(1)}, f32[32,5,384]{2,0,1:T(8,128)S(1)}, u32[]{:S(2)}, u32[]{:S(2)}) collective-permute-start(f32[32,5,384]{2,0,1:T(8,128)S(1)} %constant_dynamic-slice_fusion.8), channel_id=1, source_target_pairs={{0,1},{1,0},{2,3},{3,2},{4,5},{5,4},{6,7},{7,6},{8,9},{9,8},{10,11... | collective-permute-start | bytes 737288 | tf_op jit(solution)/shard_map/ppermute | solution.py:32
  113.8 7.3 %collective-permute-start.10 = (f32[32,5,384]{2,0,1:T(8,128)S(1)}, f32[32,5,384]{2,0,1:T(8,128)S(1)}, u32[]{:S(2)}, u32[]{:S(2)}) collective-permute-start(f32[32,5,384]{2,0,1:T(8,128)S(1)} %constant_dynamic-slice_fusion.6), channel_id=1, source_target_pairs={{0,64},{16,80},{32,96},{48,112},{64,0},{80,16},{96,32},{112,48},{1... | collective-permute-start | bytes 737288 | tf_op jit(solution)/shard_map/ppermute | solution.py:32
  121.2 10.5 %collective-permute-start.14 = (f32[3,16,5,384]{3,1,2,0:T(8,128)S(1)}, f32[3,16,5,384]{3,1,2,0:T(8,128)S(1)}, u32[]{:S(2)}, u32[]{:S(2)}) collective-permute-start(f32[3,16,5,384]{3,1,2,0:T(8,128)S(1)} %constant_dynamic-slice_fusion.3), channel_id=1, source_target_pairs={{0,128},{16,144},{32,160},{48,176},{64,192},{80,208},{96,224},{112... | collective-permute-start | bytes 1105928 | tf_op jit(solution)/shard_map/ppermute | solution.py:32
  131.9 12.0 %collective-permute-start.15 = (f32[3,16,5,192]{3,1,2,0:T(8,128)S(1)}, f32[3,16,5,192]{3,1,2,0:T(8,128)S(1)}, u32[]{:S(2)}, u32[]{:S(2)}) collective-permute-start(f32[3,16,5,192]{3,1,2,0:T(8,128)S(1)} %constant_dynamic-slice_fusion.2), channel_id=1, source_target_pairs={{0,8},{1,9},{2,10},{3,11},{4,12},{5,13},{6,14},{7,15},{8,0},{9,1},... | collective-permute-start | bytes 552968 | tf_op jit(solution)/shard_map/ppermute | solution.py:32
  140.2 18.2 %copy-start.4 = (f32[2,384,768]{2,1,0:T(8,128)S(1)}, f32[2,384,768]{2,1,0:T(8,128)}, u32[]{:S(2)}) copy-start(f32[2,384,768]{2,1,0:T(8,128)} %convert_element_type.33) | copy-start | bytes 7077892
  144.2 7.5 %collective-permute-start.16 = (f32[3,16,5,96]{3,1,2,0:T(8,128)S(1)}, f32[3,16,5,96]{3,1,2,0:T(8,128)S(1)}, u32[]{:S(2)}, u32[]{:S(2)}) collective-permute-start(f32[3,16,5,96]{3,1,2,0:T(8,128)S(1)} %constant_dynamic-slice_fusion.1), channel_id=1, source_target_pairs={{0,2},{1,3},{2,0},{3,1},{4,6},{5,7},{6,4},{7,5},{8,10},{9,11},{10,... | collective-permute-start | bytes 276488 | tf_op jit(solution)/shard_map/ppermute | solution.py:32
  151.9 10.5 %collective-permute-start.17 = (f32[3,16,5,48]{3,1,2,0:T(8,128)S(1)}, f32[3,16,5,48]{3,1,2,0:T(8,128)S(1)}, u32[]{:S(2)}, u32[]{:S(2)}) collective-permute-start(f32[3,16,5,48]{3,1,2,0:T(8,128)S(1)} %constant_dynamic-slice_fusion), channel_id=1, source_target_pairs={{0,4},{1,5},{2,6},{3,7},{4,0},{5,1},{6,2},{7,3},{8,12},{9,13},{10,... | collective-permute-start | bytes 138248 | tf_op jit(solution)/shard_map/ppermute | solution.py:32
  (16 other events, 100.7 us)

commit v7 on v6

--- a/solution.py
+++ b/solution.py
@@ -137,7 +137,7 @@
                 partial = jnp.stack(partial)
             axis, bit = CHAINS[0][step]
             partial = halved(partial, axis, bit, 1 if axis == "seq" else 3)
-            if step == shared[2]:
+            if step == shared[3]:
                 partial, trunk_input = lax.optimization_barrier((partial, trunk_input))
         else:
             partial = [

time: 164 us -> 161 us (0.982)
  waiting for transfers between devices: 29.7 us -> 25.5 us
    ppermute x13, waiting for transfers between devices: 28.1 us -> 24 us  [halved(): return keep + lax.ppermute(send, axis, partners)]
  transfers between devices with their start and end apart: 19 -> 19, of which waited for: 8 -> 7; matrix products, arithmetic and copies ran while one was open for 27% -> 29% of each run, Pallas kernels for 0% -> 0%
where the time goes in v7:
time: 161 us; the launch traced here: 159 us
  starting transfers between devices  48 us (30%)
  matrix products  35.3 us (22%)
  local copies, waits for them, and re-layouts  32.1 us (20%)
  waiting for transfers between devices  25.5 us (16%)
  other arithmetic  17.3 us (11%)
    ppermute x13, starting transfers between devices, halved(): return keep + lax.ppermute(send, axis, partners)  30.8 us
    ppermute x13, waiting for transfers between devices, halved(): return keep + lax.ppermute(send, axis, partners)  24 us
    dot_general x2, matrix products, shards(): jnp.einsum('blo,blki->oki', picked(branch_grad, chosen), act_window, pref...  19.2 us
    unnamed x55, local copies, waits for them, and re-layouts  8.9 us
    dot_general x1, matrix products, shards(): jnp.einsum('blko,kio->bli', grad_window, weight, preferred_element_type=j...  6.68 us
    ppermute x2, starting transfers between devices, with_halo(): lax.ppermute(lax.slice_in_dim(block, block.shape[dim] - width, None, axis...  6.24 us
    dot_general x1, matrix products, shards(): jnp.einsum('blki,kio->blo', window, weight, preferred_element_type=jnp.fl...  6.18 us
    all_to_all x1, starting transfers between devices, shards(): lax.all_to_all(pooled, 'seq', split_axis=2, concat_axis=1, tiled=True)  5.61 us
  transfers between devices with their start and end apart: 19, of which 7 were waited for; matrix products, arithmetic and copies ran while one was open for 29% of the time, Pallas kernels for 0%

profile of v7, /device:TPU:2, one launch (start us, length us, event | category | flops | bytes accessed | tf_op | source)
XLA Modules:
  0.0 159.5 jit_solution(16998072319065873710)
XLA Ops:
  5.6 3.0 %collective-permute-start = (bf16[2,2,768]{2,1,0:T(2,128)(2,1)S(1)}, bf16[2,2,768]{2,1,0:T(2,128)(2,1)S(1)}, u32[]{:S(2)}, u32[]{:S(2)}) collective-permute-start(bf16[2,2,768]{2,1,0:T(2,128)(2,1)S(1)} %get-tuple-element.35), channel_id=1, source_target_pairs={{0,16},{16,32},{32,48},{48,64},{64,80},{80,96},{96,112},{112,128},... | collective-permute-start | bytes 18440 | tf_op jit(solution)/shard_map/ppermute | solution.py:17
  13.3 2.5 %copy-done.14 = bf16[2,384,5,768]{3,1,0,2:T(8,128)(2,1)} copy-done((bf16[2,384,5,768]{3,1,0,2:T(8,128)(2,1)}, bf16[2,384,5,768]{3,1,0,2:T(8,128)(2,1)S(1)}, u32[]{:S(2)}) %copy-start.14) | copy-done | bytes 5898264
  15.8 8.6 %convolution_bitcast_fusion = f32[384,5,768]{2,0,1:T(8,128)} fusion(bf16[2,384,5,768]{3,1,0,2:T(8,128)(2,1)} %copy-done.14, bf16[2,384,768]{2,1,0:T(8,128)(2,1)S(1)} %get-tuple-element.39, s32[384]{0:T(512)S(1)} %bitcast.137), kind=kOutput, calls=%fused_computation.6 | convolution fusion | flops 2718498816 | bytes 12977664 | tf_op jit(solution)/shard_map/blo,blki->oki/dot_general | solution.py:106
  24.4 2.6 %collective-permute-start.2 = (f32[384,5,768]{2,0,1:T(8,128)}, f32[384,5,768]{2,0,1:T(8,128)}, u32[]{:S(2)}, u32[]{:S(2)}) collective-permute-start(f32[384,5,768]{2,0,1:T(8,128)} %convolution_bitcast_fusion), channel_id=1, source_target_pairs={{0,16},{16,0},{32,48},{48,32},{64,80},{80,64},{96,112},{112,96},{1... | collective-permute-start | bytes 17694728 | tf_op jit(solution)/shard_map/ppermute | solution.py:111
  28.3 3.2 %collective-permute-start.3 = (bf16[2,2,768]{2,1,0:T(2,128)(2,1)S(1)}, bf16[2,2,768]{2,1,0:T(2,128)(2,1)S(1)}, u32[]{:S(2)}, u32[]{:S(2)}) collective-permute-start(bf16[2,2,768]{2,1,0:T(2,128)(2,1)S(1)} %get-tuple-element.33), channel_id=1, source_target_pairs={{0,16},{16,32},{32,48},{48,64},{64,80},{80,96},{96,112},{112,128},... | collective-permute-start | bytes 18440 | tf_op jit(solution)/shard_map/ppermute | solution.py:17
  37.8 10.6 %bitcast_add_fusion = f32[384,5,768]{2,0,1:T(8,128)} fusion(f32[384,5,768]{2,0,1:T(8,128)} %collective-permute-done.2, bf16[2,384,5,768]{3,1,0,2:T(8,128)(2,1)} %copy-done.14, bf16[2,384,768]{2,1,0:T(8,128)(2,1)} %copy-done.12, s32[384]{0:T(512)S(1)} %bitcast.136), kind=kOutput, calls=%fused_computation.4 | convolution fusion | flops 2719973376 | bytes 18875904 | tf_op jit(solution)/shard_map/blo,blki->oki/dot_general | solution.py:106
  48.4 3.5 %fusion.51 = (f32[1,128,5,768]{3,1,2,0:T(8,128)S(1)}, f32[1,128,5,768]{3,1,2,0:T(8,128)S(1)}, f32[1,128,5,768]{3,1,2,0:T(8,128)S(1)}) fusion(f32[3,128,5,768]{3,1,0,2:T(8,128)} %bitcast.133), kind=kLoop, calls=%fused_computation.106 | loop fusion | bytes 11796480 | tf_op jit(solution)/shard_map/slice | solution.py:144
  56.0 3.0 %collective-permute-start.8 = (f32[64,5,768]{2,0,1:T(8,128)}, f32[64,5,768]{2,0,1:T(8,128)}, u32[]{:S(2)}, u32[]{:S(2)}) collective-permute-start(f32[64,5,768]{2,0,1:T(8,128)} %dynamic-slice_bitcast_fusion.1), channel_id=1, source_target_pairs={{0,32},{16,48},{32,0},{48,16},{64,96},{80,112},{96,64},{112,80},{1... | collective-permute-start | bytes 2949128 | tf_op jit(solution)/shard_map/ppermute | solution.py:32
  60.1 3.4 %collective-permute-start.5 = (f32[64,5,768]{2,0,1:T(8,128)}, f32[64,5,768]{2,0,1:T(8,128)}, u32[]{:S(2)}, u32[]{:S(2)}) collective-permute-start(f32[64,5,768]{2,0,1:T(8,128)} %dynamic-slice_bitcast_fusion.2), channel_id=1, source_target_pairs={{0,64},{16,80},{32,96},{48,112},{64,0},{80,16},{96,32},{112,48},{1... | collective-permute-start | bytes 2949128 | tf_op jit(solution)/shard_map/ppermute | solution.py:32
  65.9 6.2 %bitcast_add_fusion.1 = f32[2,384,768]{2,1,0:T(8,128)} fusion(f32[2,384,768]{2,1,0:T(8,128)S(1)} %copy-done.2, bf16[2,384,5,768]{3,1,0,2:T(8,128)(2,1)S(1)} %bitcast_dynamic-update-slice_fusion.5, bf16[5,768,768]{2,1,0:T(8,128)(2,1)S(1)} %bitcast.139), kind=kOutput, calls=%fused_computation.11 | convolution fusion | flops 4530438144 | bytes 16515072 | tf_op jit(solution)/shard_map/blki,kio->blo/dot_general | solution.py:128
  72.1 4.0 %reshape.61 = f32[2,192,2,768]{3,2,1,0:T(2,128)} reshape(f32[2,384,768]{2,1,0:T(8,128)} %bitcast_add_fusion.1) | data formatting | bytes 4718592 | tf_op jit(solution)/shard_map/reshape | solution.py:130
  76.0 4.4 %fusion.52 = (f32[2,192,1,768]{3,2,1,0:T(1,128)S(1)}, f32[2,192,1,768]{3,2,1,0:T(1,128)S(1)}) fusion(f32[2,192,2,768]{3,2,1,0:T(2,128)} %reshape.61), kind=kLoop, calls=%fused_computation.107 | loop fusion | bytes 4718592 | tf_op jit(solution)/shard_map/slice | solution.py:131
  82.4 5.6 %all-to-all-start = ((bf16[2,192,768]{1,0,2:T(2,128)(2,1)}), bf16[2,192,768]{1,0,2:T(2,128)(2,1)}, u32[]{:S(2)}, u32[]{:S(2)}) async-start(bf16[2,192,768]{1,0,2:T(2,128)(2,1)} %copy.39), calls=%async_computation | async-start | bytes 1572864 | tf_op jit(solution)/shard_map/all_to_all | solution.py:132
  95.8 3.1 %collective-permute-start.6 = (f32[32,5,768]{2,0,1:T(8,128)S(1)}, f32[32,5,768]{2,0,1:T(8,128)S(1)}, u32[]{:S(2)}, u32[]{:S(2)}) collective-permute-start(f32[32,5,768]{2,0,1:T(8,128)S(1)} %constant_dynamic-slice_fusion.9), channel_id=1, source_target_pairs={{0,32},{16,48},{32,0},{48,16},{64,96},{80,112},{96,64},{112,80},{1... | collective-permute-start | bytes 1474568 | tf_op jit(solution)/shard_map/ppermute | solution.py:32
  100.4 9.7 %collective-permute-done.12 = f32[64,5,384]{2,0,1:T(8,128)S(1)} collective-permute-done((f32[64,5,384]{2,0,1:T(8,128)S(1)}, f32[64,5,384]{2,0,1:T(8,128)S(1)}, u32[]{:S(2)}, u32[]{:S(2)}) %collective-permute-start.12) | collective-permute-done | bytes 491552 | tf_op jit(solution)/shard_map/ppermute | solution.py:32
  110.1 3.3 %collective-permute-start.13 = (f32[32,5,384]{2,0,1:T(8,128)S(1)}, f32[32,5,384]{2,0,1:T(8,128)S(1)}, u32[]{:S(2)}, u32[]{:S(2)}) collective-permute-start(f32[32,5,384]{2,0,1:T(8,128)S(1)} %constant_dynamic-slice_fusion.4), channel_id=1, source_target_pairs={{0,32},{16,48},{32,0},{48,16},{64,96},{80,112},{96,64},{112,80},{1... | collective-permute-start | bytes 737288 | tf_op jit(solution)/shard_map/ppermute | solution.py:32
  114.3 5.2 %collective-permute-done.13 = f32[32,5,384]{2,0,1:T(8,128)S(1)} collective-permute-done((f32[32,5,384]{2,0,1:T(8,128)S(1)}, f32[32,5,384]{2,0,1:T(8,128)S(1)}, u32[]{:S(2)}, u32[]{:S(2)}) %collective-permute-start.13) | collective-permute-done | bytes 245792 | tf_op jit(solution)/shard_map/ppermute | solution.py:32
  121.2 2.8 %collective-permute-start.14 = (f32[3,16,5,384]{3,1,2,0:T(8,128)S(1)}, f32[3,16,5,384]{3,1,2,0:T(8,128)S(1)}, u32[]{:S(2)}, u32[]{:S(2)}) collective-permute-start(f32[3,16,5,384]{3,1,2,0:T(8,128)S(1)} %constant_dynamic-slice_fusion.3), channel_id=1, source_target_pairs={{0,128},{16,144},{32,160},{48,176},{64,192},{80,208},{96,224},{112... | collective-permute-start | bytes 1105928 | tf_op jit(solution)/shard_map/ppermute | solution.py:32
  124.1 7.6 %collective-permute-done.14 = f32[3,16,5,384]{3,1,2,0:T(8,128)S(1)} collective-permute-done((f32[3,16,5,384]{3,1,2,0:T(8,128)S(1)}, f32[3,16,5,384]{3,1,2,0:T(8,128)S(1)}, u32[]{:S(2)}, u32[]{:S(2)}) %collective-permute-start.14) | collective-permute-done | bytes 368672 | tf_op jit(solution)/shard_map/ppermute | solution.py:32
  133.4 6.7 %multiply_reduce_fusion = (f32[2,384]{1,0:T(2,128)S(1)}, f32[2,384,768]{2,1,0:T(8,128)}) fusion(f32[2,384,768]{2,1,0:T(8,128)S(1)} %copy-done.3, f32[2,384]{1,0:T(2,128)S(1)} %get-tuple-element.38, bf16[2,384,5,768]{3,1,0,2:T(8,128)(2,1)S(1)} %bitcast_dynamic-update-slice_fusion, bf16[5,768,768]{2,1,0:T(8,128)(2,1)S(1)} %bitcast.141), kind=kOutput, calls=%fused_computation.13 | convolution fusion | flops 4536925184 | bytes 16521216 | tf_op jit(solution)/shard_map/blko,kio->bli/dot_general | solution.py:121
  140.3 3.4 %collective-permute-start.16 = (f32[3,16,5,96]{3,1,2,0:T(8,128)S(1)}, f32[3,16,5,96]{3,1,2,0:T(8,128)S(1)}, u32[]{:S(2)}, u32[]{:S(2)}) collective-permute-start(f32[3,16,5,96]{3,1,2,0:T(8,128)S(1)} %constant_dynamic-slice_fusion.1), channel_id=1, source_target_pairs={{0,2},{1,3},{2,0},{3,1},{4,6},{5,7},{6,4},{7,5},{8,10},{9,11},{10,... | collective-permute-start | bytes 276488 | tf_op jit(solution)/shard_map/ppermute | solution.py:32
  146.2 2.6 %all_to_all.16 = bf16[2,3072,48]{1,2,0:T(8,128)(2,1)} reshape(bf16[2,16,192,48]{2,1,3,0:T(8,128)(2,1)} %copy.41) | data formatting | bytes 1179648 | tf_op jit(solution)/shard_map/all_to_all | solution.py:132
  149.0 5.7 %collective-permute-start.17 = (f32[3,16,5,48]{3,1,2,0:T(8,128)S(1)}, f32[3,16,5,48]{3,1,2,0:T(8,128)S(1)}, u32[]{:S(2)}, u32[]{:S(2)}) collective-permute-start(f32[3,16,5,48]{3,1,2,0:T(8,128)S(1)} %constant_dynamic-slice_fusion), channel_id=1, source_target_pairs={{0,4},{1,5},{2,6},{3,7},{4,0},{5,1},{6,2},{7,3},{8,12},{9,13},{10,... | collective-permute-start | bytes 138248 | tf_op jit(solution)/shard_map/ppermute | solution.py:32
  154.6 4.0 %subtract_convert_fusion = bf16[2,384,768]{2,1,0:T(8,128)(2,1)} fusion(f32[2,384,768]{2,1,0:T(8,128)S(1)} %copy-done.4, f32[2,384,768]{2,1,0:T(8,128)} %get-tuple-element.14, f32[2,384,768]{2,1,0:T(8,128)} %get-tuple-element.42, f32[2,384]{1,0:T(2,128)S(1)} %broadcast_multiply_fusion, f32[2,384]{1,0:T(2,128)S(1)} %get-tuple-element.37, ...), kind=kLoop, calls=%fused_computation.12 | loop fusion | flops 3538944 | bytes 8266752 | tf_op jit(solution)/shard_map/convert_element_type | solution.py:124
  (131 shorter events, 43.8 us)
Async XLA Ops:
  4.2 6.5 %collective-permute-start.1 = (bf16[2,2,768]{2,1,0:T(2,128)(2,1)S(1)}, bf16[2,2,768]{2,1,0:T(2,128)(2,1)S(1)}, u32[]{:S(2)}, u32[]{:S(2)}) collective-permute-start(bf16[2,2,768]{2,1,0:T(2,128)(2,1)S(1)} %get-tuple-element.36), channel_id=1, source_target_pairs={{16,0},{32,16},{48,32},{64,48},{80,64},{96,80},{112,96},{128,112},... | collective-permute-start | bytes 18440 | tf_op jit(solution)/shard_map/ppermute | solution.py:20
  5.6 5.0 %collective-permute-start = (bf16[2,2,768]{2,1,0:T(2,128)(2,1)S(1)}, bf16[2,2,768]{2,1,0:T(2,128)(2,1)S(1)}, u32[]{:S(2)}, u32[]{:S(2)}) collective-permute-start(bf16[2,2,768]{2,1,0:T(2,128)(2,1)S(1)} %get-tuple-element.35), channel_id=1, source_target_pairs={{0,16},{16,32},{32,48},{48,64},{64,80},{80,96},{96,112},{112,128},... | collective-permute-start | bytes 18440 | tf_op jit(solution)/shard_map/ppermute | solution.py:17
  10.6 16.4 %copy-start.12 = (bf16[2,384,768]{2,1,0:T(8,128)(2,1)}, bf16[2,384,768]{2,1,0:T(8,128)(2,1)S(1)}, u32[]{:S(2)}) copy-start(bf16[2,384,768]{2,1,0:T(8,128)(2,1)S(1)} %get-tuple-element.39) | copy-start | bytes 3538948
  15.8 15.8 %copy-start.5 = (bf16[2,384,768]{2,1,0:T(8,128)(2,1)S(1)}, bf16[2,384,768]{2,1,0:T(8,128)(2,1)}, u32[]{:S(2)}) copy-start(bf16[2,384,768]{2,1,0:T(8,128)(2,1)} %param.5) | copy-start | bytes 3538948
  24.4 13.4 %collective-permute-start.2 = (f32[384,5,768]{2,0,1:T(8,128)}, f32[384,5,768]{2,0,1:T(8,128)}, u32[]{:S(2)}, u32[]{:S(2)}) collective-permute-start(f32[384,5,768]{2,0,1:T(8,128)} %convolution_bitcast_fusion), channel_id=1, source_target_pairs={{0,16},{16,0},{32,48},{48,32},{64,80},{80,64},{96,112},{112,96},{1... | collective-permute-start | bytes 17694728 | tf_op jit(solution)/shard_map/ppermute | solution.py:111
  27.0 9.1 %collective-permute-start.4 = (bf16[2,2,768]{2,1,0:T(2,128)(2,1)S(1)}, bf16[2,2,768]{2,1,0:T(2,128)(2,1)S(1)}, u32[]{:S(2)}, u32[]{:S(2)}) collective-permute-start(bf16[2,2,768]{2,1,0:T(2,128)(2,1)S(1)} %get-tuple-element.34), channel_id=1, source_target_pairs={{16,0},{32,16},{48,32},{64,48},{80,64},{96,80},{112,96},{128,112},... | collective-permute-start | bytes 18440 | tf_op jit(solution)/shard_map/ppermute | solution.py:20
  28.3 7.9 %collective-permute-start.3 = (bf16[2,2,768]{2,1,0:T(2,128)(2,1)S(1)}, bf16[2,2,768]{2,1,0:T(2,128)(2,1)S(1)}, u32[]{:S(2)}, u32[]{:S(2)}) collective-permute-start(bf16[2,2,768]{2,1,0:T(2,128)(2,1)S(1)} %get-tuple-element.33), channel_id=1, source_target_pairs={{0,16},{16,32},{32,48},{48,64},{64,80},{80,96},{96,112},{112,128},... | collective-permute-start | bytes 18440 | tf_op jit(solution)/shard_map/ppermute | solution.py:17
  48.4 16.4 %slice-start = ((s8[5898240]{0:T(1024)(128)(4,1)}), s8[4194304]{0:T(1024)(128)(4,1)S(1)}, s32[]{:S(2)}) async-start(s8[5898240]{0:T(1024)(128)(4,1)} %bitcast.138), calls=%async_computation.1 | async-start | bytes 8388608
  53.0 37.5 %collective-permute-start.11 = (f32[128,5,384]{2,0,1:T(8,128)}, f32[128,5,384]{2,0,1:T(8,128)}, u32[]{:S(2)}, u32[]{:S(2)}) collective-permute-start(f32[128,5,384]{2,0,1:T(8,128)} %dynamic-slice_bitcast_fusion), channel_id=1, source_target_pairs={{0,1},{1,0},{2,3},{3,2},{4,5},{5,4},{6,7},{7,6},{8,9},{9,8},{10,11... | collective-permute-start | bytes 2949128 | tf_op jit(solution)/shard_map/ppermute | solution.py:32
  56.0 42.8 %collective-permute-start.8 = (f32[64,5,768]{2,0,1:T(8,128)}, f32[64,5,768]{2,0,1:T(8,128)}, u32[]{:S(2)}, u32[]{:S(2)}) collective-permute-start(f32[64,5,768]{2,0,1:T(8,128)} %dynamic-slice_bitcast_fusion.1), channel_id=1, source_target_pairs={{0,32},{16,48},{32,0},{48,16},{64,96},{80,112},{96,64},{112,80},{1... | collective-permute-start | bytes 2949128 | tf_op jit(solution)/shard_map/ppermute | solution.py:32
  60.1 34.3 %collective-permute-start.5 = (f32[64,5,768]{2,0,1:T(8,128)}, f32[64,5,768]{2,0,1:T(8,128)}, u32[]{:S(2)}, u32[]{:S(2)}) collective-permute-start(f32[64,5,768]{2,0,1:T(8,128)} %dynamic-slice_bitcast_fusion.2), channel_id=1, source_target_pairs={{0,64},{16,80},{32,96},{48,112},{64,0},{80,16},{96,32},{112,48},{1... | collective-permute-start | bytes 2949128 | tf_op jit(solution)/shard_map/ppermute | solution.py:32
  82.4 61.3 %all-to-all-start = ((bf16[2,192,768]{1,0,2:T(2,128)(2,1)}), bf16[2,192,768]{1,0,2:T(2,128)(2,1)}, u32[]{:S(2)}, u32[]{:S(2)}) async-start(bf16[2,192,768]{1,0,2:T(2,128)(2,1)} %copy.39), calls=%async_computation | async-start | bytes 1572864 | tf_op jit(solution)/shard_map/all_to_all | solution.py:132
  92.4 17.6 %collective-permute-start.12 = (f32[64,5,384]{2,0,1:T(8,128)S(1)}, f32[64,5,384]{2,0,1:T(8,128)S(1)}, u32[]{:S(2)}, u32[]{:S(2)}) collective-permute-start(f32[64,5,384]{2,0,1:T(8,128)S(1)} %constant_dynamic-slice_fusion.5), channel_id=1, source_target_pairs={{0,64},{16,80},{32,96},{48,112},{64,0},{80,16},{96,32},{112,48},{1... | collective-permute-start | bytes 1474568 | tf_op jit(solution)/shard_map/ppermute | solution.py:32
  95.8 17.7 %collective-permute-start.6 = (f32[32,5,768]{2,0,1:T(8,128)S(1)}, f32[32,5,768]{2,0,1:T(8,128)S(1)}, u32[]{:S(2)}, u32[]{:S(2)}) collective-permute-start(f32[32,5,768]{2,0,1:T(8,128)S(1)} %constant_dynamic-slice_fusion.9), channel_id=1, source_target_pairs={{0,32},{16,48},{32,0},{48,16},{64,96},{80,112},{96,64},{112,80},{1... | collective-permute-start | bytes 1474568 | tf_op jit(solution)/shard_map/ppermute | solution.py:32
  100.1 33.3 %slice-start.2 = ((s8[5898240]{0:T(1024)(128)(4,1)}), s8[4194304]{0:T(1024)(128)(4,1)S(1)}, s32[]{:S(2)}) async-start(s8[5898240]{0:T(1024)(128)(4,1)} %bitcast.140), calls=%async_computation.3 | async-start | bytes 8388608
  100.2 13.5 %collective-permute-start.9 = (f32[64,5,384]{2,0,1:T(8,128)S(1)}, f32[64,5,384]{2,0,1:T(8,128)S(1)}, u32[]{:S(2)}, u32[]{:S(2)}) collective-permute-start(f32[64,5,384]{2,0,1:T(8,128)S(1)} %constant_dynamic-slice_fusion.7), channel_id=1, source_target_pairs={{0,1},{1,0},{2,3},{3,2},{4,5},{5,4},{6,7},{7,6},{8,9},{9,8},{10,11... | collective-permute-start | bytes 1474568 | tf_op jit(solution)/shard_map/ppermute | solution.py:32
  110.1 9.3 %collective-permute-start.13 = (f32[32,5,384]{2,0,1:T(8,128)S(1)}, f32[32,5,384]{2,0,1:T(8,128)S(1)}, u32[]{:S(2)}, u32[]{:S(2)}) collective-permute-start(f32[32,5,384]{2,0,1:T(8,128)S(1)} %constant_dynamic-slice_fusion.4), channel_id=1, source_target_pairs={{0,32},{16,48},{32,0},{48,16},{64,96},{80,112},{96,64},{112,80},{1... | collective-permute-start | bytes 737288 | tf_op jit(solution)/shard_map/ppermute | solution.py:32
  113.6 7.3 %collective-permute-start.7 = (f32[32,5,384]{2,0,1:T(8,128)S(1)}, f32[32,5,384]{2,0,1:T(8,128)S(1)}, u32[]{:S(2)}, u32[]{:S(2)}) collective-permute-start(f32[32,5,384]{2,0,1:T(8,128)S(1)} %constant_dynamic-slice_fusion.8), channel_id=1, source_target_pairs={{0,1},{1,0},{2,3},{3,2},{4,5},{5,4},{6,7},{7,6},{8,9},{9,8},{10,11... | collective-permute-start | bytes 737288 | tf_op jit(solution)/shard_map/ppermute | solution.py:32
  113.8 7.3 %collective-permute-start.10 = (f32[32,5,384]{2,0,1:T(8,128)S(1)}, f32[32,5,384]{2,0,1:T(8,128)S(1)}, u32[]{:S(2)}, u32[]{:S(2)}) collective-permute-start(f32[32,5,384]{2,0,1:T(8,128)S(1)} %constant_dynamic-slice_fusion.6), channel_id=1, source_target_pairs={{0,64},{16,80},{32,96},{48,112},{64,0},{80,16},{96,32},{112,48},{1... | collective-permute-start | bytes 737288 | tf_op jit(solution)/shard_map/ppermute | solution.py:32
  119.5 13.9 %slice-start.3 = ((s8[5898240]{0:T(1024)(128)(4,1)}), s8[1703936]{0:T(1024)(128)(4,1)S(1)}, s32[]{:S(2)}) async-start(s8[5898240]{0:T(1024)(128)(4,1)} %bitcast.140), calls=%async_computation.4 | async-start | bytes 3407872
  121.2 10.5 %collective-permute-start.14 = (f32[3,16,5,384]{3,1,2,0:T(8,128)S(1)}, f32[3,16,5,384]{3,1,2,0:T(8,128)S(1)}, u32[]{:S(2)}, u32[]{:S(2)}) collective-permute-start(f32[3,16,5,384]{3,1,2,0:T(8,128)S(1)} %constant_dynamic-slice_fusion.3), channel_id=1, source_target_pairs={{0,128},{16,144},{32,160},{48,176},{64,192},{80,208},{96,224},{112... | collective-permute-start | bytes 1105928 | tf_op jit(solution)/shard_map/ppermute | solution.py:32
  131.9 8.2 %collective-permute-start.15 = (f32[3,16,5,192]{3,1,2,0:T(8,128)S(1)}, f32[3,16,5,192]{3,1,2,0:T(8,128)S(1)}, u32[]{:S(2)}, u32[]{:S(2)}) collective-permute-start(f32[3,16,5,192]{3,1,2,0:T(8,128)S(1)} %constant_dynamic-slice_fusion.2), channel_id=1, source_target_pairs={{0,8},{1,9},{2,10},{3,11},{4,12},{5,13},{6,14},{7,15},{8,0},{9,1},... | collective-permute-start | bytes 552968 | tf_op jit(solution)/shard_map/ppermute | solution.py:32
  140.3 8.4 %collective-permute-start.16 = (f32[3,16,5,96]{3,1,2,0:T(8,128)S(1)}, f32[3,16,5,96]{3,1,2,0:T(8,128)S(1)}, u32[]{:S(2)}, u32[]{:S(2)}) collective-permute-start(f32[3,16,5,96]{3,1,2,0:T(8,128)S(1)} %constant_dynamic-slice_fusion.1), channel_id=1, source_target_pairs={{0,2},{1,3},{2,0},{3,1},{4,6},{5,7},{6,4},{7,5},{8,10},{9,11},{10,... | collective-permute-start | bytes 276488 | tf_op jit(solution)/shard_map/ppermute | solution.py:32
  149.0 9.6 %collective-permute-start.17 = (f32[3,16,5,48]{3,1,2,0:T(8,128)S(1)}, f32[3,16,5,48]{3,1,2,0:T(8,128)S(1)}, u32[]{:S(2)}, u32[]{:S(2)}) collective-permute-start(f32[3,16,5,48]{3,1,2,0:T(8,128)S(1)} %constant_dynamic-slice_fusion), channel_id=1, source_target_pairs={{0,4},{1,5},{2,6},{3,7},{4,0},{5,1},{6,2},{7,3},{8,12},{9,13},{10,... | collective-permute-start | bytes 138248 | tf_op jit(solution)/shard_map/ppermute | solution.py:32
  (16 other events, 97.7 us)

commit v8 on v7

--- a/solution.py
+++ b/solution.py
@@ -137,7 +137,7 @@
                 partial = jnp.stack(partial)
             axis, bit = CHAINS[0][step]
             partial = halved(partial, axis, bit, 1 if axis == "seq" else 3)
-            if step == shared[3]:
+            if step == shared[4]:
                 partial, trunk_input = lax.optimization_barrier((partial, trunk_input))
         else:
             partial = [

time: 161 us -> 159 us (0.988)
  waiting for transfers between devices: 25.5 us -> 29.7 us
  local copies, waits for them, and re-layouts: 32.1 us -> 29.1 us
  other arithmetic: 17.3 us -> 14.9 us
    ppermute x13, waiting for transfers between devices: 24 us -> 28.1 us  [halved(): return keep + lax.ppermute(send, axis, partners)]
    all_to_all x3, local copies, waits for them, and re-layouts: 5.08 us -> 2 us  [shards(): lax.all_to_all(pooled, 'seq', split_axis=2, concat_axis=1, tiled=True)]
    convert_element_type x1, other arithmetic: 3.97 us -> 1.53 us  [shards(): (upward + inverse * slope_grad - floats * inverse ** 3 * centred).astype(...]
  transfers between devices with their start and end apart: 19 -> 19, of which waited for: 7 -> 8; matrix products, arithmetic and copies ran while one was open for 29% -> 26% of each run, Pallas kernels for 0% -> 0%
where the time goes in v8:
time: 159 us; the launch traced here: 158 us
  starting transfers between devices  48.9 us (31%)
  matrix products  34 us (21%)
  waiting for transfers between devices  29.7 us (19%)
  local copies, waits for them, and re-layouts  29.1 us (18%)
  other arithmetic  14.9 us (9%)
    ppermute x13, starting transfers between devices, halved(): return keep + lax.ppermute(send, axis, partners)  31.8 us
    ppermute x13, waiting for transfers between devices, halved(): return keep + lax.ppermute(send, axis, partners)  28.1 us
    dot_general x2, matrix products, shards(): jnp.einsum('blo,blki->oki', picked(branch_grad, chosen), act_window, pref...  19.2 us
    unnamed x55, local copies, waits for them, and re-layouts  8.9 us
    ppermute x2, starting transfers between devices, with_halo(): lax.ppermute(lax.slice_in_dim(block, block.shape[dim] - width, None, axis...  6.24 us
    dot_general x1, matrix products, shards(): jnp.einsum('blki,kio->blo', window, weight, preferred_element_type=jnp.fl...  6.18 us
    all_to_all x1, starting transfers between devices, shards(): lax.all_to_all(pooled, 'seq', split_axis=2, concat_axis=1, tiled=True)  5.57 us
    dot_general x1, matrix products, shards(): jnp.einsum('blko,kio->bli', grad_window, weight, preferred_element_type=j...  5.34 us
  transfers between devices with their start and end apart: 19, of which 8 were waited for; matrix products, arithmetic and copies ran while one was open for 26% of the time, Pallas kernels for 0%

profile of v8, /device:TPU:2, one launch (start us, length us, event | category | flops | bytes accessed | tf_op | source)
XLA Modules:
  0.0 157.7 jit_solution(14456176397080359367)
XLA Ops:
  5.6 3.0 %collective-permute-start = (bf16[2,2,768]{2,1,0:T(2,128)(2,1)S(1)}, bf16[2,2,768]{2,1,0:T(2,128)(2,1)S(1)}, u32[]{:S(2)}, u32[]{:S(2)}) collective-permute-start(bf16[2,2,768]{2,1,0:T(2,128)(2,1)S(1)} %get-tuple-element.35), channel_id=1, source_target_pairs={{0,16},{16,32},{32,48},{48,64},{64,80},{80,96},{96,112},{112,128},... | collective-permute-start | bytes 18440 | tf_op jit(solution)/shard_map/ppermute | solution.py:17
  13.3 2.5 %copy-done.14 = bf16[2,384,5,768]{3,1,0,2:T(8,128)(2,1)} copy-done((bf16[2,384,5,768]{3,1,0,2:T(8,128)(2,1)}, bf16[2,384,5,768]{3,1,0,2:T(8,128)(2,1)S(1)}, u32[]{:S(2)}) %copy-start.14) | copy-done | bytes 5898264
  15.8 8.6 %convolution_bitcast_fusion = f32[384,5,768]{2,0,1:T(8,128)} fusion(bf16[2,384,5,768]{3,1,0,2:T(8,128)(2,1)} %copy-done.14, bf16[2,384,768]{2,1,0:T(8,128)(2,1)S(1)} %get-tuple-element.39, s32[384]{0:T(512)S(1)} %bitcast.137), kind=kOutput, calls=%fused_computation.6 | convolution fusion | flops 2718498816 | bytes 12977664 | tf_op jit(solution)/shard_map/blo,blki->oki/dot_general | solution.py:106
  24.4 2.6 %collective-permute-start.2 = (f32[384,5,768]{2,0,1:T(8,128)}, f32[384,5,768]{2,0,1:T(8,128)}, u32[]{:S(2)}, u32[]{:S(2)}) collective-permute-start(f32[384,5,768]{2,0,1:T(8,128)} %convolution_bitcast_fusion), channel_id=1, source_target_pairs={{0,16},{16,0},{32,48},{48,32},{64,80},{80,64},{96,112},{112,96},{1... | collective-permute-start | bytes 17694728 | tf_op jit(solution)/shard_map/ppermute | solution.py:111
  28.3 3.2 %collective-permute-start.3 = (bf16[2,2,768]{2,1,0:T(2,128)(2,1)S(1)}, bf16[2,2,768]{2,1,0:T(2,128)(2,1)S(1)}, u32[]{:S(2)}, u32[]{:S(2)}) collective-permute-start(bf16[2,2,768]{2,1,0:T(2,128)(2,1)S(1)} %get-tuple-element.33), channel_id=1, source_target_pairs={{0,16},{16,32},{32,48},{48,64},{64,80},{80,96},{96,112},{112,128},... | collective-permute-start | bytes 18440 | tf_op jit(solution)/shard_map/ppermute | solution.py:17
  37.8 10.6 %bitcast_add_fusion = f32[384,5,768]{2,0,1:T(8,128)} fusion(f32[384,5,768]{2,0,1:T(8,128)} %collective-permute-done.2, bf16[2,384,5,768]{3,1,0,2:T(8,128)(2,1)} %copy-done.14, bf16[2,384,768]{2,1,0:T(8,128)(2,1)} %copy-done.12, s32[384]{0:T(512)S(1)} %bitcast.136), kind=kOutput, calls=%fused_computation.4 | convolution fusion | flops 2719973376 | bytes 18875904 | tf_op jit(solution)/shard_map/blo,blki->oki/dot_general | solution.py:106
  48.4 3.5 %fusion.51 = (f32[1,128,5,768]{3,1,2,0:T(8,128)S(1)}, f32[1,128,5,768]{3,1,2,0:T(8,128)S(1)}, f32[1,128,5,768]{3,1,2,0:T(8,128)S(1)}) fusion(f32[3,128,5,768]{3,1,0,2:T(8,128)} %bitcast.133), kind=kLoop, calls=%fused_computation.106 | loop fusion | bytes 11796480 | tf_op jit(solution)/shard_map/slice | solution.py:144
  56.0 3.0 %collective-permute-start.8 = (f32[64,5,768]{2,0,1:T(8,128)}, f32[64,5,768]{2,0,1:T(8,128)}, u32[]{:S(2)}, u32[]{:S(2)}) collective-permute-start(f32[64,5,768]{2,0,1:T(8,128)} %dynamic-slice_bitcast_fusion.1), channel_id=1, source_target_pairs={{0,32},{16,48},{32,0},{48,16},{64,96},{80,112},{96,64},{112,80},{1... | collective-permute-start | bytes 2949128 | tf_op jit(solution)/shard_map/ppermute | solution.py:32
  60.1 3.4 %collective-permute-start.5 = (f32[64,5,768]{2,0,1:T(8,128)}, f32[64,5,768]{2,0,1:T(8,128)}, u32[]{:S(2)}, u32[]{:S(2)}) collective-permute-start(f32[64,5,768]{2,0,1:T(8,128)} %dynamic-slice_bitcast_fusion.2), channel_id=1, source_target_pairs={{0,64},{16,80},{32,96},{48,112},{64,0},{80,16},{96,32},{112,48},{1... | collective-permute-start | bytes 2949128 | tf_op jit(solution)/shard_map/ppermute | solution.py:32
  65.9 6.2 %bitcast_add_fusion.1 = f32[2,384,768]{2,1,0:T(8,128)} fusion(f32[2,384,768]{2,1,0:T(8,128)S(1)} %copy-done.2, bf16[2,384,5,768]{3,1,0,2:T(8,128)(2,1)S(1)} %bitcast_dynamic-update-slice_fusion.5, bf16[5,768,768]{2,1,0:T(8,128)(2,1)S(1)} %bitcast.139), kind=kOutput, calls=%fused_computation.11 | convolution fusion | flops 4530438144 | bytes 16515072 | tf_op jit(solution)/shard_map/blki,kio->blo/dot_general | solution.py:128
  72.1 4.0 %reshape.61 = f32[2,192,2,768]{3,2,1,0:T(2,128)} reshape(f32[2,384,768]{2,1,0:T(8,128)} %bitcast_add_fusion.1) | data formatting | bytes 4718592 | tf_op jit(solution)/shard_map/reshape | solution.py:130
  76.0 4.4 %fusion.52 = (f32[2,192,1,768]{3,2,1,0:T(1,128)S(1)}, f32[2,192,1,768]{3,2,1,0:T(1,128)S(1)}) fusion(f32[2,192,2,768]{3,2,1,0:T(2,128)} %reshape.61), kind=kLoop, calls=%fused_computation.107 | loop fusion | bytes 4718592 | tf_op jit(solution)/shard_map/slice | solution.py:131
  82.4 5.6 %all-to-all-start = ((bf16[2,192,768]{1,0,2:T(2,128)(2,1)}), bf16[2,192,768]{1,0,2:T(2,128)(2,1)S(1)}, u32[]{:S(2)}, u32[]{:S(2)}) async-start(bf16[2,192,768]{1,0,2:T(2,128)(2,1)} %copy.39), calls=%async_computation | async-start | bytes 1572864 | tf_op jit(solution)/shard_map/all_to_all | solution.py:132
  92.4 2.0 %collective-permute-start.12 = (f32[64,5,384]{2,0,1:T(8,128)S(1)}, f32[64,5,384]{2,0,1:T(8,128)S(1)}, u32[]{:S(2)}, u32[]{:S(2)}) collective-permute-start(f32[64,5,384]{2,0,1:T(8,128)S(1)} %constant_dynamic-slice_fusion.5), channel_id=1, source_target_pairs={{0,64},{16,80},{32,96},{48,112},{64,0},{80,16},{96,32},{112,48},{1... | collective-permute-start | bytes 1474568 | tf_op jit(solution)/shard_map/ppermute | solution.py:32
  95.8 3.1 %collective-permute-start.6 = (f32[32,5,768]{2,0,1:T(8,128)S(1)}, f32[32,5,768]{2,0,1:T(8,128)S(1)}, u32[]{:S(2)}, u32[]{:S(2)}) collective-permute-start(f32[32,5,768]{2,0,1:T(8,128)S(1)} %constant_dynamic-slice_fusion.9), channel_id=1, source_target_pairs={{0,32},{16,48},{32,0},{48,16},{64,96},{80,112},{96,64},{112,80},{1... | collective-permute-start | bytes 1474568 | tf_op jit(solution)/shard_map/ppermute | solution.py:32
  100.4 9.7 %collective-permute-done.12 = f32[64,5,384]{2,0,1:T(8,128)S(1)} collective-permute-done((f32[64,5,384]{2,0,1:T(8,128)S(1)}, f32[64,5,384]{2,0,1:T(8,128)S(1)}, u32[]{:S(2)}, u32[]{:S(2)}) %collective-permute-start.12) | collective-permute-done | bytes 491552 | tf_op jit(solution)/shard_map/ppermute | solution.py:32
  110.2 3.3 %collective-permute-start.13 = (f32[32,5,384]{2,0,1:T(8,128)S(1)}, f32[32,5,384]{2,0,1:T(8,128)S(1)}, u32[]{:S(2)}, u32[]{:S(2)}) collective-permute-start(f32[32,5,384]{2,0,1:T(8,128)S(1)} %constant_dynamic-slice_fusion.4), channel_id=1, source_target_pairs={{0,32},{16,48},{32,0},{48,16},{64,96},{80,112},{96,64},{112,80},{1... | collective-permute-start | bytes 737288 | tf_op jit(solution)/shard_map/ppermute | solution.py:32
  114.3 5.2 %collective-permute-done.13 = f32[32,5,384]{2,0,1:T(8,128)S(1)} collective-permute-done((f32[32,5,384]{2,0,1:T(8,128)S(1)}, f32[32,5,384]{2,0,1:T(8,128)S(1)}, u32[]{:S(2)}, u32[]{:S(2)}) %collective-permute-start.13) | collective-permute-done | bytes 245792 | tf_op jit(solution)/shard_map/ppermute | solution.py:32
  121.2 2.8 %collective-permute-start.14 = (f32[3,16,5,384]{3,1,2,0:T(8,128)S(1)}, f32[3,16,5,384]{3,1,2,0:T(8,128)S(1)}, u32[]{:S(2)}, u32[]{:S(2)}) collective-permute-start(f32[3,16,5,384]{3,1,2,0:T(8,128)S(1)} %constant_dynamic-slice_fusion.3), channel_id=1, source_target_pairs={{0,128},{16,144},{32,160},{48,176},{64,192},{80,208},{96,224},{112... | collective-permute-start | bytes 1105928 | tf_op jit(solution)/shard_map/ppermute | solution.py:32
  124.1 7.6 %collective-permute-done.14 = f32[3,16,5,384]{3,1,2,0:T(8,128)S(1)} collective-permute-done((f32[3,16,5,384]{3,1,2,0:T(8,128)S(1)}, f32[3,16,5,384]{3,1,2,0:T(8,128)S(1)}, u32[]{:S(2)}, u32[]{:S(2)}) %collective-permute-start.14) | collective-permute-done | bytes 368672 | tf_op jit(solution)/shard_map/ppermute | solution.py:32
  133.4 5.3 %multiply_reduce_fusion = (f32[2,384]{1,0:T(2,128)S(1)}, f32[2,384,768]{2,1,0:T(8,128)S(1)}) fusion(f32[2,384,768]{2,1,0:T(8,128)S(1)} %copy-done.3, f32[2,384]{1,0:T(2,128)S(1)} %get-tuple-element.38, bf16[2,384,5,768]{3,1,0,2:T(8,128)(2,1)S(1)} %bitcast_dynamic-update-slice_fusion, bf16[5,768,768]{2,1,0:T(8,128)(2,1)S(1)} %bitcast.141), kind=kOutput, calls=%fused_computation.13 | convolution fusion | flops 4536925184 | bytes 16521216 | tf_op jit(solution)/shard_map/blko,kio->bli/dot_general | solution.py:121
  139.0 3.4 %collective-permute-start.16 = (f32[3,16,5,96]{3,1,2,0:T(8,128)S(1)}, f32[3,16,5,96]{3,1,2,0:T(8,128)S(1)}, u32[]{:S(2)}, u32[]{:S(2)}) collective-permute-start(f32[3,16,5,96]{3,1,2,0:T(8,128)S(1)} %constant_dynamic-slice_fusion.1), channel_id=1, source_target_pairs={{0,2},{1,3},{2,0},{3,1},{4,6},{5,7},{6,4},{7,5},{8,10},{9,11},{10,... | collective-permute-start | bytes 276488 | tf_op jit(solution)/shard_map/ppermute | solution.py:32
  142.4 4.2 %collective-permute-done.16 = f32[3,16,5,96]{3,1,2,0:T(8,128)S(1)} collective-permute-done((f32[3,16,5,96]{3,1,2,0:T(8,128)S(1)}, f32[3,16,5,96]{3,1,2,0:T(8,128)S(1)}, u32[]{:S(2)}, u32[]{:S(2)}) %collective-permute-start.16) | collective-permute-done | bytes 92192 | tf_op jit(solution)/shard_map/ppermute | solution.py:32
  146.8 6.5 %collective-permute-start.17 = (f32[3,16,5,48]{3,1,2,0:T(8,128)S(1)}, f32[3,16,5,48]{3,1,2,0:T(8,128)S(1)}, u32[]{:S(2)}, u32[]{:S(2)}) collective-permute-start(f32[3,16,5,48]{3,1,2,0:T(8,128)S(1)} %constant_dynamic-slice_fusion), channel_id=1, source_target_pairs={{0,4},{1,5},{2,6},{3,7},{4,0},{5,1},{6,2},{7,3},{8,12},{9,13},{10,... | collective-permute-start | bytes 138248 | tf_op jit(solution)/shard_map/ppermute | solution.py:32
  (131 shorter events, 42.9 us)
Async XLA Ops:
  4.2 6.5 %collective-permute-start.1 = (bf16[2,2,768]{2,1,0:T(2,128)(2,1)S(1)}, bf16[2,2,768]{2,1,0:T(2,128)(2,1)S(1)}, u32[]{:S(2)}, u32[]{:S(2)}) collective-permute-start(bf16[2,2,768]{2,1,0:T(2,128)(2,1)S(1)} %get-tuple-element.36), channel_id=1, source_target_pairs={{16,0},{32,16},{48,32},{64,48},{80,64},{96,80},{112,96},{128,112},... | collective-permute-start | bytes 18440 | tf_op jit(solution)/shard_map/ppermute | solution.py:20
  5.6 5.0 %collective-permute-start = (bf16[2,2,768]{2,1,0:T(2,128)(2,1)S(1)}, bf16[2,2,768]{2,1,0:T(2,128)(2,1)S(1)}, u32[]{:S(2)}, u32[]{:S(2)}) collective-permute-start(bf16[2,2,768]{2,1,0:T(2,128)(2,1)S(1)} %get-tuple-element.35), channel_id=1, source_target_pairs={{0,16},{16,32},{32,48},{48,64},{64,80},{80,96},{96,112},{112,128},... | collective-permute-start | bytes 18440 | tf_op jit(solution)/shard_map/ppermute | solution.py:17
  10.6 16.4 %copy-start.12 = (bf16[2,384,768]{2,1,0:T(8,128)(2,1)}, bf16[2,384,768]{2,1,0:T(8,128)(2,1)S(1)}, u32[]{:S(2)}) copy-start(bf16[2,384,768]{2,1,0:T(8,128)(2,1)S(1)} %get-tuple-element.39) | copy-start | bytes 3538948
  15.8 15.8 %copy-start.4 = (bf16[2,384,768]{2,1,0:T(8,128)(2,1)S(1)}, bf16[2,384,768]{2,1,0:T(8,128)(2,1)}, u32[]{:S(2)}) copy-start(bf16[2,384,768]{2,1,0:T(8,128)(2,1)} %param.5) | copy-start | bytes 3538948
  24.4 13.4 %collective-permute-start.2 = (f32[384,5,768]{2,0,1:T(8,128)}, f32[384,5,768]{2,0,1:T(8,128)}, u32[]{:S(2)}, u32[]{:S(2)}) collective-permute-start(f32[384,5,768]{2,0,1:T(8,128)} %convolution_bitcast_fusion), channel_id=1, source_target_pairs={{0,16},{16,0},{32,48},{48,32},{64,80},{80,64},{96,112},{112,96},{1... | collective-permute-start | bytes 17694728 | tf_op jit(solution)/shard_map/ppermute | solution.py:111
  27.0 9.1 %collective-permute-start.4 = (bf16[2,2,768]{2,1,0:T(2,128)(2,1)S(1)}, bf16[2,2,768]{2,1,0:T(2,128)(2,1)S(1)}, u32[]{:S(2)}, u32[]{:S(2)}) collective-permute-start(bf16[2,2,768]{2,1,0:T(2,128)(2,1)S(1)} %get-tuple-element.34), channel_id=1, source_target_pairs={{16,0},{32,16},{48,32},{64,48},{80,64},{96,80},{112,96},{128,112},... | collective-permute-start | bytes 18440 | tf_op jit(solution)/shard_map/ppermute | solution.py:20
  28.3 7.9 %collective-permute-start.3 = (bf16[2,2,768]{2,1,0:T(2,128)(2,1)S(1)}, bf16[2,2,768]{2,1,0:T(2,128)(2,1)S(1)}, u32[]{:S(2)}, u32[]{:S(2)}) collective-permute-start(bf16[2,2,768]{2,1,0:T(2,128)(2,1)S(1)} %get-tuple-element.33), channel_id=1, source_target_pairs={{0,16},{16,32},{32,48},{48,64},{64,80},{80,96},{96,112},{112,128},... | collective-permute-start | bytes 18440 | tf_op jit(solution)/shard_map/ppermute | solution.py:17
  48.4 16.4 %slice-start = ((s8[5898240]{0:T(1024)(128)(4,1)}), s8[4194304]{0:T(1024)(128)(4,1)S(1)}, s32[]{:S(2)}) async-start(s8[5898240]{0:T(1024)(128)(4,1)} %bitcast.138), calls=%async_computation.1 | async-start | bytes 8388608
  53.0 37.4 %collective-permute-start.11 = (f32[128,5,384]{2,0,1:T(8,128)}, f32[128,5,384]{2,0,1:T(8,128)}, u32[]{:S(2)}, u32[]{:S(2)}) collective-permute-start(f32[128,5,384]{2,0,1:T(8,128)} %dynamic-slice_bitcast_fusion), channel_id=1, source_target_pairs={{0,1},{1,0},{2,3},{3,2},{4,5},{5,4},{6,7},{7,6},{8,9},{9,8},{10,11... | collective-permute-start | bytes 2949128 | tf_op jit(solution)/shard_map/ppermute | solution.py:32
  56.0 42.8 %collective-permute-start.8 = (f32[64,5,768]{2,0,1:T(8,128)}, f32[64,5,768]{2,0,1:T(8,128)}, u32[]{:S(2)}, u32[]{:S(2)}) collective-permute-start(f32[64,5,768]{2,0,1:T(8,128)} %dynamic-slice_bitcast_fusion.1), channel_id=1, source_target_pairs={{0,32},{16,48},{32,0},{48,16},{64,96},{80,112},{96,64},{112,80},{1... | collective-permute-start | bytes 2949128 | tf_op jit(solution)/shard_map/ppermute | solution.py:32
  60.1 34.3 %collective-permute-start.5 = (f32[64,5,768]{2,0,1:T(8,128)}, f32[64,5,768]{2,0,1:T(8,128)}, u32[]{:S(2)}, u32[]{:S(2)}) collective-permute-start(f32[64,5,768]{2,0,1:T(8,128)} %dynamic-slice_bitcast_fusion.2), channel_id=1, source_target_pairs={{0,64},{16,80},{32,96},{48,112},{64,0},{80,16},{96,32},{112,48},{1... | collective-permute-start | bytes 2949128 | tf_op jit(solution)/shard_map/ppermute | solution.py:32
  82.4 72.4 %all-to-all-start = ((bf16[2,192,768]{1,0,2:T(2,128)(2,1)}), bf16[2,192,768]{1,0,2:T(2,128)(2,1)S(1)}, u32[]{:S(2)}, u32[]{:S(2)}) async-start(bf16[2,192,768]{1,0,2:T(2,128)(2,1)} %copy.39), calls=%async_computation | async-start | bytes 1572864 | tf_op jit(solution)/shard_map/all_to_all | solution.py:132
  92.4 17.7 %collective-permute-start.12 = (f32[64,5,384]{2,0,1:T(8,128)S(1)}, f32[64,5,384]{2,0,1:T(8,128)S(1)}, u32[]{:S(2)}, u32[]{:S(2)}) collective-permute-start(f32[64,5,384]{2,0,1:T(8,128)S(1)} %constant_dynamic-slice_fusion.5), channel_id=1, source_target_pairs={{0,64},{16,80},{32,96},{48,112},{64,0},{80,16},{96,32},{112,48},{1... | collective-permute-start | bytes 1474568 | tf_op jit(solution)/shard_map/ppermute | solution.py:32
  95.8 17.7 %collective-permute-start.6 = (f32[32,5,768]{2,0,1:T(8,128)S(1)}, f32[32,5,768]{2,0,1:T(8,128)S(1)}, u32[]{:S(2)}, u32[]{:S(2)}) collective-permute-start(f32[32,5,768]{2,0,1:T(8,128)S(1)} %constant_dynamic-slice_fusion.9), channel_id=1, source_target_pairs={{0,32},{16,48},{32,0},{48,16},{64,96},{80,112},{96,64},{112,80},{1... | collective-permute-start | bytes 1474568 | tf_op jit(solution)/shard_map/ppermute | solution.py:32
  100.2 33.3 %slice-start.2 = ((s8[5898240]{0:T(1024)(128)(4,1)}), s8[4194304]{0:T(1024)(128)(4,1)S(1)}, s32[]{:S(2)}) async-start(s8[5898240]{0:T(1024)(128)(4,1)} %bitcast.140), calls=%async_computation.3 | async-start | bytes 8388608
  100.2 13.5 %collective-permute-start.9 = (f32[64,5,384]{2,0,1:T(8,128)S(1)}, f32[64,5,384]{2,0,1:T(8,128)S(1)}, u32[]{:S(2)}, u32[]{:S(2)}) collective-permute-start(f32[64,5,384]{2,0,1:T(8,128)S(1)} %constant_dynamic-slice_fusion.7), channel_id=1, source_target_pairs={{0,1},{1,0},{2,3},{3,2},{4,5},{5,4},{6,7},{7,6},{8,9},{9,8},{10,11... | collective-permute-start | bytes 1474568 | tf_op jit(solution)/shard_map/ppermute | solution.py:32
  110.2 9.3 %collective-permute-start.13 = (f32[32,5,384]{2,0,1:T(8,128)S(1)}, f32[32,5,384]{2,0,1:T(8,128)S(1)}, u32[]{:S(2)}, u32[]{:S(2)}) collective-permute-start(f32[32,5,384]{2,0,1:T(8,128)S(1)} %constant_dynamic-slice_fusion.4), channel_id=1, source_target_pairs={{0,32},{16,48},{32,0},{48,16},{64,96},{80,112},{96,64},{112,80},{1... | collective-permute-start | bytes 737288 | tf_op jit(solution)/shard_map/ppermute | solution.py:32
  113.6 7.3 %collective-permute-start.7 = (f32[32,5,384]{2,0,1:T(8,128)S(1)}, f32[32,5,384]{2,0,1:T(8,128)S(1)}, u32[]{:S(2)}, u32[]{:S(2)}) collective-permute-start(f32[32,5,384]{2,0,1:T(8,128)S(1)} %constant_dynamic-slice_fusion.8), channel_id=1, source_target_pairs={{0,1},{1,0},{2,3},{3,2},{4,5},{5,4},{6,7},{7,6},{8,9},{9,8},{10,11... | collective-permute-start | bytes 737288 | tf_op jit(solution)/shard_map/ppermute | solution.py:32
  113.8 7.3 %collective-permute-start.10 = (f32[32,5,384]{2,0,1:T(8,128)S(1)}, f32[32,5,384]{2,0,1:T(8,128)S(1)}, u32[]{:S(2)}, u32[]{:S(2)}) collective-permute-start(f32[32,5,384]{2,0,1:T(8,128)S(1)} %constant_dynamic-slice_fusion.6), channel_id=1, source_target_pairs={{0,64},{16,80},{32,96},{48,112},{64,0},{80,16},{96,32},{112,48},{1... | collective-permute-start | bytes 737288 | tf_op jit(solution)/shard_map/ppermute | solution.py:32
  121.2 10.5 %collective-permute-start.14 = (f32[3,16,5,384]{3,1,2,0:T(8,128)S(1)}, f32[3,16,5,384]{3,1,2,0:T(8,128)S(1)}, u32[]{:S(2)}, u32[]{:S(2)}) collective-permute-start(f32[3,16,5,384]{3,1,2,0:T(8,128)S(1)} %constant_dynamic-slice_fusion.3), channel_id=1, source_target_pairs={{0,128},{16,144},{32,160},{48,176},{64,192},{80,208},{96,224},{112... | collective-permute-start | bytes 1105928 | tf_op jit(solution)/shard_map/ppermute | solution.py:32
  131.9 6.9 %collective-permute-start.15 = (f32[3,16,5,192]{3,1,2,0:T(8,128)S(1)}, f32[3,16,5,192]{3,1,2,0:T(8,128)S(1)}, u32[]{:S(2)}, u32[]{:S(2)}) collective-permute-start(f32[3,16,5,192]{3,1,2,0:T(8,128)S(1)} %constant_dynamic-slice_fusion.2), channel_id=1, source_target_pairs={{0,8},{1,9},{2,10},{3,11},{4,12},{5,13},{6,14},{7,15},{8,0},{9,1},... | collective-permute-start | bytes 552968 | tf_op jit(solution)/shard_map/ppermute | solution.py:32
  133.4 19.9 %copy-start.5 = (f32[2,384,768]{2,1,0:T(8,128)S(1)}, f32[2,384,768]{2,1,0:T(8,128)}, u32[]{:S(2)}) copy-start(f32[2,384,768]{2,1,0:T(8,128)} %get-tuple-element.14) | copy-start | bytes 7077892
  139.0 7.5 %collective-permute-start.16 = (f32[3,16,5,96]{3,1,2,0:T(8,128)S(1)}, f32[3,16,5,96]{3,1,2,0:T(8,128)S(1)}, u32[]{:S(2)}, u32[]{:S(2)}) collective-permute-start(f32[3,16,5,96]{3,1,2,0:T(8,128)S(1)} %constant_dynamic-slice_fusion.1), channel_id=1, source_target_pairs={{0,2},{1,3},{2,0},{3,1},{4,6},{5,7},{6,4},{7,5},{8,10},{9,11},{10,... | collective-permute-start | bytes 276488 | tf_op jit(solution)/shard_map/ppermute | solution.py:32
  146.8 10.1 %collective-permute-start.17 = (f32[3,16,5,48]{3,1,2,0:T(8,128)S(1)}, f32[3,16,5,48]{3,1,2,0:T(8,128)S(1)}, u32[]{:S(2)}, u32[]{:S(2)}) collective-permute-start(f32[3,16,5,48]{3,1,2,0:T(8,128)S(1)} %constant_dynamic-slice_fusion), channel_id=1, source_target_pairs={{0,4},{1,5},{2,6},{3,7},{4,0},{5,1},{6,2},{7,3},{8,12},{9,13},{10,... | collective-permute-start | bytes 138248 | tf_op jit(solution)/shard_map/ppermute | solution.py:32
  (16 other events, 100.3 us)
